TPU v7x, 256 devices: a whole 4x4x8 slice. The times are simulated.
256 devices in a mesh: blk: 32 (over x, y, core), req: 8 (over z).
Axes of the slice: x: 4, y: 4, z: 8, core: 2. Of those that a mesh axis runs over, the one named last changes fastest.
Arguments:
- patches: bfloat16 [6144, 1408], P('req')
- vis_ln_gain: bfloat16 [1408], replicated, may hold values from 0.25 to 4
- vis_ln_bias: bfloat16 [1408], replicated, may hold values from -3 to 3
- vis_up: bfloat16 [1408, 6144], P(None, 'blk'), may hold values from -0.15625 to 0.15625
- vis_up_bias: bfloat16 [6144], P('blk'), may hold values from -3 to 3
- vis_down: bfloat16 [6144, 1408], P('blk'), may hold values from -0.15625 to 0.15625
- vis_down_bias: bfloat16 [1408], replicated, may hold values from -3 to 3
- merge_gain: bfloat16 [1408], replicated, may hold values from 0.099609375 to 1.8984375
- merge_proj: bfloat16 [5632, 4096], P(None, 'blk'), may hold values from -0.078125 to 0.078125
- merge_proj_bias: bfloat16 [4096], P('blk'), may hold values from -3 to 3
- image_dest: int32 [1536], replicated, may hold values from 0 to 8191, as said below
- text_embed: bfloat16 [8192, 4096], P('req', 'blk')
- segment_ids: int32 [8, 1024], P('req'), may hold values from 0 to 3, never falling along the last dimension, each value on 1 to 512 neighbouring positions
- text_gain: bfloat16 [4096], replicated, may hold values from 0.099609375 to 1.8984375
- query_weight: bfloat16 [4096, 4096], P(None, 'blk')
- key_weight: bfloat16 [4096, 4096], P(None, 'blk')
- value_weight: bfloat16 [4096, 4096], P(None, 'blk'), may hold values from -0.09375 to 0.09375
- out_weight: bfloat16 [4096, 4096], P('blk'), may hold values from -0.1875 to 0.1875
Outputs:
- hidden_out: bfloat16 [8192, 4096], P(('req', 'blk'))
Inputs may be any that keep to these rules, and one draw needn't show every extreme that they name: image_dest holds distinct positions; each group of 1024 positions receives exactly 192 image rows, and of one group's 192 image rows at most 66 go to one group of positions, exactly 66 for one group. `segment_ids`: each row has 4 requests as runs of equal, non-decreasing ids, each of 1 to 512 tokens, one exactly 512.
All inputs are finite; a program needn't handle non-finite values.
Results may differ from a plain program's by a relative error of at most 0.04.
Values may be sent and summed in bfloat16 or wider, within the bound.
No kernel may reach another device: no remote copies, remote signals or barrier semaphores. Data moves between devices by JAX's collectives and lax.ppermute only.
A program may use at most 128 MiB of HBM per device.

v0:
```python
import jax
import jax.numpy as jnp
from jax import lax
from jax.sharding import PartitionSpec as P

HEAD = 128


def layer_norm(values, gain_vector, shift_vector):
    centre = jnp.mean(values, axis=-1, keepdims=True)
    centred = values - centre
    spread = jnp.mean(centred * centred, axis=-1, keepdims=True)
    result = centred * lax.rsqrt(spread + 1e-06) * gain_vector.astype(jnp.float32)
    if shift_vector is None:
        return result
    return result + shift_vector.astype(jnp.float32)


def rotate(values, positions):
    half_size = HEAD // 2
    frequency = 10000.0 ** (-2.0 * jnp.arange(half_size, dtype=jnp.float32) / HEAD)
    angles = positions.astype(jnp.float32)[:, None] * frequency[None, :]
    cosine = jnp.cos(angles)[:, None, :]
    sine_table = jnp.sin(angles)[:, None, :]
    by_head = values.reshape(values.shape[0], -1, HEAD)
    first_half = by_head[..., :half_size]
    second_half = by_head[..., half_size:]
    turned = jnp.concatenate(
        [
            first_half * cosine - second_half * sine_table,
            second_half * cosine + first_half * sine_table,
        ],
        axis=-1,
    )
    return turned.reshape(values.shape)


def causal_setup(segments):
    length = segments.shape[0]
    column_ids = jnp.arange(length)
    same_request = segments[:, None] == segments[None, :]
    earlier = column_ids[None, :] < column_ids[:, None]
    positions = jnp.sum(same_request & earlier, axis=1)
    allowed = same_request & (column_ids[None, :] <= column_ids[:, None])
    return (positions, allowed)


def attend(queries, keys, values, allowed):
    row_count = queries.shape[0]
    key_count = keys.shape[0]
    query_heads = queries.reshape(row_count, -1, HEAD)
    key_heads = keys.reshape(key_count, -1, HEAD)
    value_heads = values.reshape(key_count, -1, HEAD)
    scores = jnp.einsum(
        "thd,shd->hts", query_heads, key_heads, preferred_element_type=jnp.float32
    ) * HEAD ** (-0.5)
    scores = jnp.where(allowed[None, :, :], scores, -jnp.inf)
    top_score = jnp.max(scores, axis=-1, keepdims=True)
    weights = jnp.exp(scores - top_score)
    weights = (weights / jnp.sum(weights, axis=-1, keepdims=True)).astype(jnp.bfloat16)
    mixed = jnp.einsum("hts,shd->thd", weights, value_heads, preferred_element_type=jnp.float32)
    return mixed.astype(jnp.bfloat16).reshape(row_count, -1)


def body(
    patches,
    vis_ln_gain,
    vis_ln_bias,
    vis_up,
    vis_up_bias,
    vis_down,
    vis_down_bias,
    merge_gain,
    merge_proj,
    merge_proj_bias,
    image_dest,
    text_embed,
    segment_ids,
    text_gain,
    query_weight,
    key_weight,
    value_weight,
    out_weight,
):
    blk_count = lax.axis_size("blk")
    req_count = lax.axis_size("req")
    blk_index = lax.axis_index("blk")
    req_index = lax.axis_index("req")
    vis_width = patches.shape[1]
    patch_rows = patches.astype(jnp.float32)
    normed = layer_norm(patch_rows, vis_ln_gain, vis_ln_bias).astype(jnp.bfloat16)
    pre_act = jnp.dot(normed, vis_up, preferred_element_type=jnp.float32) + vis_up_bias.astype(
        jnp.float32
    )
    hidden = jax.nn.gelu(pre_act, approximate=False).astype(jnp.bfloat16)
    summed = lax.psum(
        jnp.dot(hidden, vis_down, preferred_element_type=jnp.float32).astype(jnp.bfloat16), "blk"
    ).astype(jnp.float32)
    vis_out = patches.astype(jnp.float32) + summed + vis_down_bias.astype(jnp.float32)
    normed = layer_norm(vis_out, merge_gain, None).astype(jnp.bfloat16)
    image_cols = jnp.dot(
        normed.reshape(-1, 4 * vis_width), merge_proj, preferred_element_type=jnp.float32
    )
    image_cols = (image_cols + merge_proj_bias.astype(jnp.float32)).astype(jnp.bfloat16)
    image_count = image_cols.shape[0]
    col_width = image_cols.shape[1]
    tok_grp = text_embed.shape[0]
    dest_group = image_dest // tok_grp
    dest_local = image_dest - dest_group * tok_grp
    target = jnp.where(dest_group == req_index, dest_local, tok_grp)
    filler = jnp.zeros((1, col_width), jnp.bfloat16)
    capacity = image_count // 4 + 3 * image_count // 4 // req_count
    by_source = dest_group.reshape(req_count, image_count)
    one_hot = (
        by_source[:, :, None] == jnp.arange(req_count, dtype=jnp.int32)[None, None, :]
    ).astype(jnp.int32)
    slot_index = jnp.sum((jnp.cumsum(one_hot, axis=1) - one_hot) * one_hot, axis=2)
    send_slot = lax.dynamic_index_in_dim(
        by_source * capacity + slot_index, req_index, 0, keepdims=False
    )
    source_row = (
        jnp.full((req_count * capacity,), image_count, jnp.int32)
        .at[send_slot]
        .set(jnp.arange(image_count, dtype=jnp.int32))
    )
    outgoing = jnp.take(jnp.concatenate([image_cols, filler], axis=0), source_row, axis=0)
    incoming = lax.all_to_all(outgoing, "req", split_axis=0, concat_axis=0, tiled=True)
    arrival = (jnp.arange(req_count, dtype=jnp.int32)[:, None] * capacity + slot_index).reshape(-1)
    row_table = jnp.concatenate([incoming, filler], axis=0)
    missing = row_table.shape[0] - 1
    lookup = jnp.full((tok_grp,), missing, jnp.int32).at[target].set(arrival, mode="drop")
    columns = jnp.where(
        (lookup < missing)[:, None], jnp.take(row_table, lookup, axis=0), text_embed
    )
    features = lax.all_gather(columns, "blk", axis=1, tiled=True)
    token_values = features.astype(jnp.float32)
    normed_tokens = (
        token_values
        * lax.rsqrt(jnp.mean(token_values * token_values, axis=-1, keepdims=True) + 1e-05)
        * text_gain.astype(jnp.float32)
    ).astype(jnp.bfloat16)
    positions, allowed = causal_setup(segment_ids[0])
    queries = rotate(
        jnp.dot(normed_tokens, query_weight, preferred_element_type=jnp.float32), positions
    ).astype(jnp.bfloat16)
    keys_rot = rotate(
        jnp.dot(normed_tokens, key_weight, preferred_element_type=jnp.float32), positions
    ).astype(jnp.bfloat16)
    values_here = jnp.dot(normed_tokens, value_weight, preferred_element_type=jnp.float32).astype(
        jnp.bfloat16
    )
    block_rows = min(512, tok_grp)
    block_count = tok_grp // block_rows

    def attend_block(block_pair):
        return attend(block_pair[0], keys_rot, values_here, block_pair[1])

    attn_out = lax.map(
        attend_block,
        (
            queries.reshape(block_count, block_rows, -1),
            allowed.reshape(block_count, block_rows, tok_grp),
        ),
    ).reshape(tok_grp, -1)
    out_share = tok_grp // blk_count
    summed_heads = lax.psum_scatter(
        jnp.dot(attn_out, out_weight, preferred_element_type=jnp.float32).astype(jnp.bfloat16),
        "blk",
        scatter_dimension=0,
        tiled=True,
    ).astype(jnp.float32)
    residual = lax.dynamic_slice_in_dim(token_values, blk_index * out_share, out_share, 0)
    return (residual + summed_heads).astype(jnp.bfloat16)


def solution(mesh):
    return jax.shard_map(
        body,
        mesh=mesh,
        in_specs=(
            P("req", None),
            P(),
            P(),
            P(None, "blk"),
            P("blk"),
            P("blk", None),
            P(),
            P(),
            P(None, "blk"),
            P("blk"),
            P(),
            P("req", "blk"),
            P("req", None),
            P(),
            P(None, "blk"),
            P(None, "blk"),
            P(None, "blk"),
            P("blk", None),
        ),
        out_specs=P(("req", "blk"), None),
        check_vma=False,
    )
```

profile of v0, /device:TPU:8, one launch (start us, length us, event | category | flops | bytes accessed | tf_op | source)
XLA Modules:
  0.0 381.3 jit_solution(12648237813361242620)
XLA Ops:
  7.4 2.0 convert_reduce_fusion
  9.4 2.3 fusion.9
  11.8 6.3 %convolution_convert_fusion.2 = bf16[768,1408]{1,0:T(8,128)(2,1)} fusion(bf16[192,1408]{1,0:T(8,128)(2,1)S(1)} %copy-done.17, bf16[1408,192]{0,1:T(8,128)(2,1)S(1)} %copy-done.18, bf16[768,1408]{1,0:T(8,128)(2,1)} %param.20, f32[1408]{0:T(1024)S(1)} %convert_element_type.103, f32[1408]{0:T(1024)S(1)} %convert_element_type.102, ...), kind=kOutput, calls=%fused_computation.35 | convolution fusion | flops 847773696 | bytes 5424896 | tf_op jit(solution)/shard_map/dot_general | solution.py:97
  18.3 4.5 %reduce-window.6 = s32[8,8,2,128]{3,1,2,0:T(8,128)S(1)} reduce-window(s32[8,8,2,128]{3,1,2,0:T(8,128)S(1)} %convert_bitcast_fusion, s32[]{:T(128)} %constant.42.clone.1), window={size=1x1x1x128 pad=0_0x0_0x0_0x127_0}, to_apply=%region_0.0 | reduce-window | flops 2080768 | bytes 131076 | tf_op jit(solution)/shard_map/reduce-window
  24.8 6.2 %scatter_custom_fusion = s32[1024]{0:T(1024)S(1)} fusion(s32[1536]{0:T(1024)S(1)} %get-tuple-element.74, s32[1536]{0:T(1024)S(1)} %reshape.297, s32[]{:T(128)} %constant.68.clone.1), kind=kCustom, calls=%fused_computation.151 | custom fusion | bytes 4100 | tf_op jit(solution)/shard_map/scatter | solution.py:131
  31.0 106.8 %all-reduce.5.cloned.1.call-done = bf16[768,1408]{1,0:T(8,128)(2,1)} async-done(((bf16[768,1408]{1,0:T(8,128)(2,1)}), bf16[768,1408]{1,0:T(8,128)(2,1)}) %all-reduce.5.cloned.1.call-update) | async-done | bytes 2162704 | tf_op jit(solution)/shard_map/psum | solution.py:96
  137.9 3.2 fusion.16
  142.5 2.4 multiply_convert_fusion.1
  144.9 4.4 %reshape.272 = bf16[192,5632]{1,0:T(8,128)(2,1)} reshape(bf16[768,1408]{1,0:T(8,128)(2,1)} %multiply_convert_fusion.1) | data formatting | bytes 4325376 | tf_op jit(solution)/shard_map/reshape | solution.py:102
  149.4 2.4 fusion.22
  151.8 1.9 gather_fusion
  154.6 7.0 %all-to-all-start = ((bf16[8,66,128]{2,1,0:T(8,128)(2,1)}), bf16[8,66,128]{2,1,0:T(8,128)(2,1)S(1)}, u32[]{:S(2)}, u32[]{:S(2)}) async-start(bf16[8,66,128]{2,1,0:T(8,128)(2,1)} %broadcast_select_fusion), calls=%async_computation | async-start | bytes 294912 | tf_op jit(solution)/shard_map/all_to_all | solution.py:127
  161.7 9.6 %all-to-all-done = bf16[8,66,128]{2,1,0:T(8,128)(2,1)S(1)} async-done(((bf16[8,66,128]{2,1,0:T(8,128)(2,1)}), bf16[8,66,128]{2,1,0:T(8,128)(2,1)S(1)}, u32[]{:S(2)}, u32[]{:S(2)}) %all-to-all-start) | async-done | bytes 135200 | tf_op jit(solution)/shard_map/all_to_all | solution.py:127
  171.3 3.2 gather_fusion.1
  178.8 55.6 %all-gather.2.cloned.1.call-done = bf16[1024,4096]{1,0:T(8,128)(2,1)} async-done(((bf16[1024,128]{1,0:T(8,128)(2,1)}), bf16[1024,4096]{1,0:T(8,128)(2,1)}) %all-gather.2.cloned.1.call-update) | async-done | bytes 8388624 | tf_op jit(solution)/shard_map/all_gather | solution.py:135
  234.5 5.1 %multiply_reduce_fusion = f32[1024]{0:T(1024)S(1)} fusion(bf16[1024,4096]{1,0:T(8,128)(2,1)} %all-gather.2.cloned.1.call-done), kind=kLoop, calls=%fused_computation.16 | loop fusion | flops 12581888 | bytes 8392704 | tf_op jit(solution)/shard_map/reduce_sum | solution.py:139
  239.6 10.4 %multiply_convert_fusion = bf16[1024,4096]{1,0:T(8,128)(2,1)} fusion(f32[4096]{0:T(1024)S(1)} %convert_element_type.115, f32[1024]{0:T(1024)S(1)} %add_rsqrt_fusion, bf16[1024,4096]{1,0:T(8,128)(2,1)} %all-gather.2.cloned.1.call-done), kind=kLoop, calls=%fused_computation.15 | loop fusion | flops 16777216 | bytes 16797696 | tf_op jit(solution)/shard_map/convert_element_type | solution.py:141
  250.0 5.9 %convolution_convert_fusion.3 = bf16[1024,128]{1,0:T(8,128)(2,1)S(1)} fusion(bf16[1024,4096]{1,0:T(8,128)(2,1)} %multiply_convert_fusion, bf16[4096,128]{1,0:T(8,128)(2,1)S(1)} %copy-done.16), kind=kOutput, calls=%fused_computation.41 | convolution fusion | flops 1073872896 | bytes 9699328 | tf_op jit(solution)/shard_map/dot_general | solution.py:149
  256.0 2.9 convolution_bitcast_fusion
  258.9 2.9 convolution_bitcast_fusion.1
  263.6 3.4 while.10
  267.1 5.5 %convolution_convert_fusion.1 = bf16[1024,4096]{1,0:T(8,128)(2,1)} fusion(bf16[1024,128]{1,0:T(8,128)(2,1)S(1)} %bitcast.70, bf16[128,4096]{1,0:T(8,128)(2,1)S(1)} %copy-done.7), kind=kOutput, calls=%fused_computation.17 | convolution fusion | flops 1077936128 | bytes 9699328 | tf_op jit(solution)/shard_map/dot_general | solution.py:167
  272.7 11.5 %convert_element_type.114 = f32[1024,4096]{1,0:T(8,128)} convert(bf16[1024,4096]{1,0:T(8,128)(2,1)} %all-gather.2.cloned.1.call-done) | non-fusion elementwise | flops 4194304 | bytes 25165824 | tf_op jit(solution)/shard_map/convert_element_type | solution.py:136
  284.2 88.8 %reduce-scatter.2.cloned.1.call-done = bf16[32,4096]{1,0:T(8,128)(2,1)} async-done(((bf16[1024,4096]{1,0:T(8,128)(2,1)}), bf16[32,4096]{1,0:T(8,128)(2,1)}) %reduce-scatter.2.cloned.1.call-update) | async-done | bytes 262160 | tf_op jit(solution)/shard_map/reduce_scatter | solution.py:166
  (109 shorter events, 16.8 us)
Async XLA Ops:
  6.5 142.9 %copy-start = (bf16[5632,128]{1,0:T(8,128)(2,1)S(1)}, bf16[5632,128]{1,0:T(8,128)(2,1)}, u32[]{:S(2)}) copy-start(bf16[5632,128]{1,0:T(8,128)(2,1)} %param.28) | copy-start | bytes 4325380
  6.5 5.2 %copy-start.12 = (bf16[1408]{0:T(1024)(128)(2,1)S(1)}, bf16[1408]{0:T(1024)(128)(2,1)}, u32[]{:S(2)}) copy-start(bf16[1408]{0:T(1024)(128)(2,1)} %param.21) | copy-start | bytes 8452
  6.5 5.2 %copy-start.13 = (bf16[1408]{0:T(1024)(128)(2,1)S(1)}, bf16[1408]{0:T(1024)(128)(2,1)}, u32[]{:S(2)}) copy-start(bf16[1408]{0:T(1024)(128)(2,1)} %param.22) | copy-start | bytes 8452
  6.5 5.2 %copy-start.17 = (bf16[192,1408]{1,0:T(8,128)(2,1)S(1)}, bf16[192,1408]{1,0:T(8,128)(2,1)}, u32[]{:S(2)}) copy-start(bf16[192,1408]{1,0:T(8,128)(2,1)} %param.25) | copy-start | bytes 1622020
  6.5 5.2 %copy-start.18 = (bf16[1408,192]{0,1:T(8,128)(2,1)S(1)}, bf16[1408,192]{0,1:T(8,128)(2,1)}, u32[]{:S(2)}) copy-start(bf16[1408,192]{0,1:T(8,128)(2,1)} %param.23) | copy-start | bytes 1622020
  6.5 131.3 %all-reduce.5.cloned.1.call-start = ((), (), s32[]{:S(2)}) async-start(), calls=%async_computation.2 | async-start | bytes 4325376 | tf_op jit(solution)/shard_map/psum | solution.py:96
  11.8 6.4 %copy-start.19 = (bf16[128]{0:T(256)(128)(2,1)S(1)}, bf16[128]{0:T(256)(128)(2,1)}, u32[]{:S(2)}) copy-start(bf16[128]{0:T(256)(128)(2,1)} %param.29) | copy-start | bytes 772
  11.8 6.4 %copy-start.14 = (bf16[1408]{0:T(1024)(128)(2,1)S(1)}, bf16[1408]{0:T(1024)(128)(2,1)}, u32[]{:S(2)}) copy-start(bf16[1408]{0:T(1024)(128)(2,1)} %param.26) | copy-start | bytes 8452
  11.8 6.4 %copy-start.15 = (bf16[1408]{0:T(1024)(128)(2,1)S(1)}, bf16[1408]{0:T(1024)(128)(2,1)}, u32[]{:S(2)}) copy-start(bf16[1408]{0:T(1024)(128)(2,1)} %param.27) | copy-start | bytes 8452
  11.8 6.4 %copy-start.10 = (s32[1536]{0:T(1024)S(1)}, s32[1536]{0:T(1024)}, u32[]{:S(2)}) copy-start(s32[1536]{0:T(1024)} %param.30) | copy-start | bytes 18436
  137.9 3.2 copy-start.3
  137.9 3.6 copy-start.4
  149.4 25.1 %copy-start.8 = (bf16[1024,128]{1,0:T(8,128)(2,1)S(1)}, bf16[1024,128]{1,0:T(8,128)(2,1)}, u32[]{:S(2)}) copy-start(bf16[1024,128]{1,0:T(8,128)(2,1)} %param.31) | copy-start | bytes 786436
  149.4 26.8 %copy-start.9 = (s32[1,1024]{1,0:T(1,128)S(1)}, s32[1,1024]{1,0:T(1,128)}, u32[]{:S(2)}) copy-start(s32[1,1024]{1,0:T(1,128)} %param.32) | copy-start | bytes 12292
  149.4 28.0 %copy-start.11 = (bf16[4096]{0:T(1024)(128)(2,1)S(1)}, bf16[4096]{0:T(1024)(128)(2,1)}, u32[]{:S(2)}) copy-start(bf16[4096]{0:T(1024)(128)(2,1)} %param.33) | copy-start | bytes 24580
  154.6 16.7 %all-to-all-start = ((bf16[8,66,128]{2,1,0:T(8,128)(2,1)}), bf16[8,66,128]{2,1,0:T(8,128)(2,1)S(1)}, u32[]{:S(2)}, u32[]{:S(2)}) async-start(bf16[8,66,128]{2,1,0:T(8,128)(2,1)} %broadcast_select_fusion), calls=%async_computation | async-start | bytes 294912 | tf_op jit(solution)/shard_map/all_to_all | solution.py:127
  161.6 72.9 %all-gather.2.cloned.1.call-start = ((), (), s32[]{:S(2)}) async-start(), calls=%async_computation.3 | async-start | bytes 8650752 | tf_op jit(solution)/shard_map/all_gather | solution.py:135
  175.6 197.3 %reduce-scatter.2.cloned.1.call-start = ((), (), s32[]{:S(2)}) async-start(), calls=%async_computation.4 | async-start | bytes 8650752 | tf_op jit(solution)/shard_map/reduce_scatter | solution.py:166
  239.5 10.4 %copy-start.16 = (bf16[4096,128]{1,0:T(8,128)(2,1)S(1)}, bf16[4096,128]{1,0:T(8,128)(2,1)}, u32[]{:S(2)}) copy-start(bf16[4096,128]{1,0:T(8,128)(2,1)} %param.36) | copy-start | bytes 3145732
  250.0 5.9 %copy-start.2 = (bf16[1024,4096]{1,0:T(8,128)(2,1)S(1)}, bf16[1024,4096]{1,0:T(8,128)(2,1)}, u32[]{:S(2)}) copy-start(bf16[1024,4096]{1,0:T(8,128)(2,1)} %multiply_convert_fusion) | copy-start | bytes 25165828
  250.0 6.0 %copy-start.5 = (bf16[4096,128]{1,0:T(8,128)(2,1)S(1)}, bf16[4096,128]{1,0:T(8,128)(2,1)}, u32[]{:S(2)}) copy-start(bf16[4096,128]{1,0:T(8,128)(2,1)} %param.35) | copy-start | bytes 3145732
  256.0 2.9 copy-start.6
  263.6 3.4 copy-start.7
  272.6 102.1 %copy-start.1 = (bf16[5632,128]{1,0:T(8,128)(2,1)S(1)}, bf16[5632,128]{1,0:T(8,128)(2,1)}, u32[]{:S(2)}) copy-start(bf16[5632,128]{1,0:T(8,128)(2,1)} %param.28) | copy-start | bytes 4325380
Sparse Core Ops, SparseCore 0:
  18.3 119.5 all-reduce.4
  175.7 58.6 all-gather.1
  272.8 100.1 reduce-scatter.1
where the time goes:
time: 382 us; the launch traced here: 381 us
  waiting for transfers between devices  261 us (68%)
  other arithmetic  52.5 us (14%)
  matrix products  28.2 us (7%)
  local copies, waits for them, and re-layouts  19 us (5%)
  between operations  13.7 us (4%)
  starting transfers between devices  7.13 us (2%)
    psum x1, waiting for transfers between devices, body(): lax.psum(jnp.dot(hidden, vis_down, preferred_element_type=jnp.float32).as...  107 us
    reduce_scatter x1, waiting for transfers between devices, body(): lax.psum_scatter(jnp.dot(attn_out, out_weight, preferred_element_type=jnp...  88.8 us
    all_gather x1, waiting for transfers between devices, body(): features = lax.all_gather(columns, 'blk', axis=1, tiled=True)  55.6 us
    convert_element_type x1, other arithmetic, body(): token_values = features.astype(jnp.float32)  11.5 us
    convert_element_type x1, other arithmetic, body(): normed_tokens = (token_values * lax.rsqrt(jnp.mean(token_values * token_v...  10.4 us
    all_to_all x1, waiting for transfers between devices, body(): lax.all_to_all(outgoing, 'req', split_axis=0, concat_axis=0, tiled=True)  9.59 us
  transfers between devices with their start and end apart: 4, of which 4 were waited for; matrix products, arithmetic and copies ran while one was open for 7% of the time, Pallas kernels for 0%

commit v1 on v0

--- a/solution.py
+++ b/solution.py
@@ -93,13 +93,26 @@
         jnp.float32
     )
     hidden = jax.nn.gelu(pre_act, approximate=False).astype(jnp.bfloat16)
-    summed = lax.psum(
-        jnp.dot(hidden, vis_down, preferred_element_type=jnp.float32).astype(jnp.bfloat16), "blk"
-    ).astype(jnp.float32)
-    vis_out = patches.astype(jnp.float32) + summed + vis_down_bias.astype(jnp.float32)
+    partial = jnp.dot(hidden, vis_down, preferred_element_type=jnp.float32).astype(jnp.bfloat16)
+    patch_count = patches.shape[0]
+    row_share = patch_count // blk_count
+    parts_here = lax.all_to_all(
+        partial.reshape(blk_count, row_share, vis_width), "blk", 0, 0, tiled=False
+    )
+    summed = jnp.sum(parts_here.astype(jnp.float32), axis=0)
+    own_rows = lax.dynamic_slice_in_dim(patch_rows, blk_index * row_share, row_share, 0)
+    vis_out = own_rows + summed + vis_down_bias.astype(jnp.float32)
     normed = layer_norm(vis_out, merge_gain, None).astype(jnp.bfloat16)
+    merged_here = normed.reshape(-1, 4 * vis_width)
+    merged_all = lax.all_to_all(
+        jnp.broadcast_to(merged_here[None], (blk_count,) + merged_here.shape),
+        "blk",
+        0,
+        0,
+        tiled=False,
+    )
     image_cols = jnp.dot(
-        normed.reshape(-1, 4 * vis_width), merge_proj, preferred_element_type=jnp.float32
+        merged_all.reshape(-1, 4 * vis_width), merge_proj, preferred_element_type=jnp.float32
     )
     image_cols = (image_cols + merge_proj_bias.astype(jnp.float32)).astype(jnp.bfloat16)
     image_count = image_cols.shape[0]

time: 382 us -> 338 us (0.88)
  waiting for transfers between devices: 261 us -> 199 us
  starting transfers between devices: 7.13 us -> 22.9 us
    psum x1 -> x0, waiting for transfers between devices: 107 us -> none  [body(): lax.psum(jnp.dot(hidden, vis_down, preferred_element_type=jnp.float32).as...]
    all_to_all x0 -> x2, waiting for transfers between devices: none -> 47.1 us  [the longest x1 23.6 us: body(): lax.all_to_all(partial.reshape(blk_count, row_share, vis_width), 'blk', 0...]
    all_to_all x0 -> x2, starting transfers between devices: none -> 14.3 us  [the longest x1 7.58 us: body(): lax.all_to_all(partial.reshape(blk_count, row_share, vis_width), 'blk', 0...]
    convert_element_type x1 -> x2, other arithmetic: 0.01 us -> 3.88 us  [the longest x1 3.88 us: body(): patch_rows = patches.astype(jnp.float32)]
  transfers between devices with their start and end apart: 4 -> 5, of which waited for: 4 -> 5; matrix products, arithmetic and copies ran while one was open for 7% -> 9% of each run, Pallas kernels for 0% -> 0%
where the time goes in v1:
time: 338 us; the launch traced here: 337 us
  waiting for transfers between devices  199 us (59%)
  other arithmetic  52.9 us (16%)
  matrix products  28.3 us (8%)
  starting transfers between devices  22.9 us (7%)
  local copies, waits for them, and re-layouts  20.3 us (6%)
  between operations  13.9 us (4%)
    reduce_scatter x1, waiting for transfers between devices, body(): lax.psum_scatter(jnp.dot(attn_out, out_weight, preferred_element_type=jnp...  88.8 us
    all_gather x1, waiting for transfers between devices, body(): features = lax.all_gather(columns, 'blk', axis=1, tiled=True)  53.9 us
    all_to_all x1, waiting for transfers between devices, body(): lax.all_to_all(partial.reshape(blk_count, row_share, vis_width), 'blk', 0...  23.6 us
    all_to_all x1, waiting for transfers between devices, body(): lax.all_to_all(jnp.broadcast_to(merged_here[None], (blk_count,) + merged_...  23.5 us
    convert_element_type x1, other arithmetic, body(): token_values = features.astype(jnp.float32)  11.5 us
    convert_element_type x1, other arithmetic, body(): normed_tokens = (token_values * lax.rsqrt(jnp.mean(token_values * token_v...  10.4 us
    all_to_all x1, waiting for transfers between devices, body(): lax.all_to_all(outgoing, 'req', split_axis=0, concat_axis=0, tiled=True)  9.18 us
    all_to_all x1, starting transfers between devices, body(): lax.all_to_all(outgoing, 'req', split_axis=0, concat_axis=0, tiled=True)  8.47 us
  transfers between devices with their start and end apart: 5, of which 5 were waited for; matrix products, arithmetic and copies ran while one was open for 9% of the time, Pallas kernels for 0%

profile of v1, /device:TPU:8, one launch (start us, length us, event | category | flops | bytes accessed | tf_op | source)
XLA Modules:
  0.0 337.3 jit_solution(811712265640372366)
XLA Ops:
  9.3 2.3 multiply_reduce_fusion.1
  11.7 6.4 %convolution_convert_fusion.2 = bf16[768,1408]{1,0:T(8,128)(2,1)} fusion(bf16[192,1408]{1,0:T(8,128)(2,1)S(1)} %copy-done.15, bf16[1408,192]{0,1:T(8,128)(2,1)S(1)} %copy-done.16, bf16[768,1408]{1,0:T(8,128)(2,1)} %param.20, f32[1408]{0:T(1024)S(1)} %convert_element_type.102, f32[1408]{0:T(1024)S(1)} %convert_element_type.101, ...), kind=kOutput, calls=%fused_computation.26 | convolution fusion | flops 847773696 | bytes 5424896 | tf_op jit(solution)/shard_map/dot_general | solution.py:96
  18.1 7.6 %all-to-all-start = ((bf16[32,24,1408]{2,1,0:T(8,128)(2,1)}), bf16[32,24,1408]{2,1,0:T(8,128)(2,1)}, u32[]{:S(2)}, u32[]{:S(2)}) async-start(bf16[32,24,1408]{2,1,0:T(8,128)(2,1)} %bitcast.71), calls=%async_computation | async-start | bytes 4325376 | tf_op jit(solution)/shard_map/all_to_all | solution.py:99
  25.7 3.9 %convert_element_type.100 = f32[768,1408]{1,0:T(8,128)} convert(bf16[768,1408]{1,0:T(8,128)(2,1)} %param.20) | non-fusion elementwise | flops 1081344 | bytes 6488064 | tf_op jit(solution)/shard_map/convert_element_type | solution.py:90
  29.6 23.6 %all-to-all-done = bf16[32,24,1408]{2,1,0:T(8,128)(2,1)} async-done(((bf16[32,24,1408]{2,1,0:T(8,128)(2,1)}), bf16[32,24,1408]{2,1,0:T(8,128)(2,1)}, u32[]{:S(2)}, u32[]{:S(2)}) %all-to-all-start) | async-done | bytes 2162720 | tf_op jit(solution)/shard_map/all_to_all | solution.py:99
  58.4 6.8 %all-to-all-start.1 = ((bf16[32,6,5632]{2,1,0:T(8,128)(2,1)}), bf16[32,6,5632]{2,1,0:T(8,128)(2,1)}, u32[]{:S(2)}, u32[]{:S(2)}) async-start(bf16[32,6,5632]{2,1,0:T(8,128)(2,1)} %broadcast_in_dim.60), calls=%async_computation.1 | async-start | bytes 5767168 | tf_op jit(solution)/shard_map/all_to_all | solution.py:107
  65.3 4.5 %reduce-window.6 = s32[8,8,2,128]{3,1,2,0:T(8,128)S(1)} reduce-window(s32[8,8,2,128]{3,1,2,0:T(8,128)S(1)} %convert_bitcast_fusion, s32[]{:T(128)} %constant.72.clone.1), window={size=1x1x1x128 pad=0_0x0_0x0_0x127_0}, to_apply=%region_0.0 | reduce-window | flops 2080768 | bytes 131076 | tf_op jit(solution)/shard_map/reduce-window
  71.8 6.2 %scatter_custom_fusion = s32[1024]{0:T(1024)S(1)} fusion(s32[1536]{0:T(1024)S(1)} %get-tuple-element.76, s32[1536]{0:T(1024)S(1)} %reshape.302, s32[]{:T(128)} %constant.70.clone.1), kind=kCustom, calls=%fused_computation.143 | custom fusion | bytes 4100 | tf_op jit(solution)/shard_map/scatter | solution.py:144
  78.0 23.5 %all-to-all-done.1 = bf16[32,6,5632]{2,1,0:T(8,128)(2,1)} async-done(((bf16[32,6,5632]{2,1,0:T(8,128)(2,1)}), bf16[32,6,5632]{2,1,0:T(8,128)(2,1)}, u32[]{:S(2)}, u32[]{:S(2)}) %all-to-all-start.1) | async-done | bytes 2162720 | tf_op jit(solution)/shard_map/all_to_all | solution.py:107
  101.5 4.3 %reshape.277 = bf16[192,5632]{1,0:T(8,128)(2,1)} reshape(bf16[32,6,5632]{2,1,0:T(8,128)(2,1)} %all-to-all-done.1) | data formatting | bytes 4325376 | tf_op jit(solution)/shard_map/reshape | solution.py:115
  105.8 2.4 fusion.11
  110.9 8.5 %all-to-all-start.2 = ((bf16[8,66,128]{2,1,0:T(8,128)(2,1)}), bf16[8,66,128]{2,1,0:T(8,128)(2,1)S(1)}, u32[]{:S(2)}, u32[]{:S(2)}) async-start(bf16[8,66,128]{2,1,0:T(8,128)(2,1)} %broadcast_select_fusion), calls=%async_computation.2 | async-start | bytes 294912 | tf_op jit(solution)/shard_map/all_to_all | solution.py:140
  119.5 9.2 %all-to-all-done.2 = bf16[8,66,128]{2,1,0:T(8,128)(2,1)S(1)} async-done(((bf16[8,66,128]{2,1,0:T(8,128)(2,1)}), bf16[8,66,128]{2,1,0:T(8,128)(2,1)S(1)}, u32[]{:S(2)}, u32[]{:S(2)}) %all-to-all-start.2) | async-done | bytes 135200 | tf_op jit(solution)/shard_map/all_to_all | solution.py:140
  128.7 3.2 gather_fusion.1
  136.2 53.9 %all-gather.2.cloned.1.call-done = bf16[1024,4096]{1,0:T(8,128)(2,1)} async-done(((bf16[1024,128]{1,0:T(8,128)(2,1)}), bf16[1024,4096]{1,0:T(8,128)(2,1)}) %all-gather.2.cloned.1.call-update) | async-done | bytes 8388624 | tf_op jit(solution)/shard_map/all_gather | solution.py:148
  190.1 5.1 %multiply_reduce_fusion = f32[1024]{0:T(1024)S(1)} fusion(bf16[1024,4096]{1,0:T(8,128)(2,1)} %all-gather.2.cloned.1.call-done), kind=kLoop, calls=%fused_computation.16 | loop fusion | flops 12581888 | bytes 8392704 | tf_op jit(solution)/shard_map/reduce_sum | solution.py:152
  195.2 10.4 %multiply_convert_fusion = bf16[1024,4096]{1,0:T(8,128)(2,1)} fusion(f32[4096]{0:T(1024)S(1)} %convert_element_type.114, f32[1024]{0:T(1024)S(1)} %add_rsqrt_fusion, bf16[1024,4096]{1,0:T(8,128)(2,1)} %all-gather.2.cloned.1.call-done), kind=kLoop, calls=%fused_computation.15 | loop fusion | flops 16777216 | bytes 16797696 | tf_op jit(solution)/shard_map/convert_element_type | solution.py:154
  205.6 5.9 %convolution_convert_fusion.3 = bf16[1024,128]{1,0:T(8,128)(2,1)S(1)} fusion(bf16[1024,4096]{1,0:T(8,128)(2,1)} %multiply_convert_fusion, bf16[4096,128]{1,0:T(8,128)(2,1)S(1)} %copy-done.14), kind=kOutput, calls=%fused_computation.32 | convolution fusion | flops 1073872896 | bytes 9699328 | tf_op jit(solution)/shard_map/dot_general | solution.py:162
  211.6 2.9 convolution_bitcast_fusion
  214.5 2.9 convolution_bitcast_fusion.1
  219.3 3.4 %while.10 = (s32[]{:T(128)}, bf16[2,512,128]{2,1,0:T(8,128)(2,1)S(1)}, pred[2,512,1024]{2,1,0:T(32,128)(4,1)S(1)}, bf16[2,512,128]{2,1,0:T(8,128)(2,1)S(1)}, bf1...) while((s32[]{:T(128)}, bf16[2,512,128]{2,1,0:T(8,128)(2,1)S(1)}, ...), condition=%wide.region_15.16_spmd, body=%wide.region_12.15_spmd.sunk | while | flops 272694272 | bytes 7613529 | solution.py:171
  222.7 5.5 %convolution_convert_fusion.1 = bf16[1024,4096]{1,0:T(8,128)(2,1)} fusion(bf16[1024,128]{1,0:T(8,128)(2,1)S(1)} %bitcast.72, bf16[128,4096]{1,0:T(8,128)(2,1)S(1)} %copy-done.5), kind=kOutput, calls=%fused_computation.17 | convolution fusion | flops 1077936128 | bytes 9699328 | tf_op jit(solution)/shard_map/dot_general | solution.py:180
  228.3 11.5 %convert_element_type.113 = f32[1024,4096]{1,0:T(8,128)} convert(bf16[1024,4096]{1,0:T(8,128)(2,1)} %all-gather.2.cloned.1.call-done) | non-fusion elementwise | flops 4194304 | bytes 25165824 | tf_op jit(solution)/shard_map/convert_element_type | solution.py:149
  239.8 88.8 %reduce-scatter.2.cloned.1.call-done = bf16[32,4096]{1,0:T(8,128)(2,1)} async-done(((bf16[1024,4096]{1,0:T(8,128)(2,1)}), bf16[32,4096]{1,0:T(8,128)(2,1)}) %reduce-scatter.2.cloned.1.call-update) | async-done | bytes 262160 | tf_op jit(solution)/shard_map/reduce_scatter | solution.py:179
  (110 shorter events, 24.3 us)
Async XLA Ops:
  6.5 99.2 %copy-start = (bf16[5632,128]{1,0:T(8,128)(2,1)S(1)}, bf16[5632,128]{1,0:T(8,128)(2,1)}, u32[]{:S(2)}) copy-start(bf16[5632,128]{1,0:T(8,128)(2,1)} %param.28) | copy-start | bytes 4325380
  6.5 5.1 %copy-start.10 = (bf16[1408]{0:T(1024)(128)(2,1)S(1)}, bf16[1408]{0:T(1024)(128)(2,1)}, u32[]{:S(2)}) copy-start(bf16[1408]{0:T(1024)(128)(2,1)} %param.21) | copy-start | bytes 8452
  6.5 5.1 %copy-start.11 = (bf16[1408]{0:T(1024)(128)(2,1)S(1)}, bf16[1408]{0:T(1024)(128)(2,1)}, u32[]{:S(2)}) copy-start(bf16[1408]{0:T(1024)(128)(2,1)} %param.22) | copy-start | bytes 8452
  6.5 5.2 %copy-start.15 = (bf16[192,1408]{1,0:T(8,128)(2,1)S(1)}, bf16[192,1408]{1,0:T(8,128)(2,1)}, u32[]{:S(2)}) copy-start(bf16[192,1408]{1,0:T(8,128)(2,1)} %param.25) | copy-start | bytes 1622020
  6.5 5.2 %copy-start.16 = (bf16[1408,192]{0,1:T(8,128)(2,1)S(1)}, bf16[1408,192]{0,1:T(8,128)(2,1)}, u32[]{:S(2)}) copy-start(bf16[1408,192]{0,1:T(8,128)(2,1)} %param.23) | copy-start | bytes 1622020
  18.1 35.2 %all-to-all-start = ((bf16[32,24,1408]{2,1,0:T(8,128)(2,1)}), bf16[32,24,1408]{2,1,0:T(8,128)(2,1)}, u32[]{:S(2)}, u32[]{:S(2)}) async-start(bf16[32,24,1408]{2,1,0:T(8,128)(2,1)} %bitcast.71), calls=%async_computation | async-start | bytes 4325376 | tf_op jit(solution)/shard_map/all_to_all | solution.py:99
  25.7 3.9 %copy-start.17 = (bf16[128]{0:T(256)(128)(2,1)S(1)}, bf16[128]{0:T(256)(128)(2,1)}, u32[]{:S(2)}) copy-start(bf16[128]{0:T(256)(128)(2,1)} %param.29) | copy-start | bytes 772
  25.7 3.9 %copy-start.12 = (bf16[1408]{0:T(1024)(128)(2,1)S(1)}, bf16[1408]{0:T(1024)(128)(2,1)}, u32[]{:S(2)}) copy-start(bf16[1408]{0:T(1024)(128)(2,1)} %param.26) | copy-start | bytes 8452
  25.7 3.9 %copy-start.13 = (bf16[1408]{0:T(1024)(128)(2,1)S(1)}, bf16[1408]{0:T(1024)(128)(2,1)}, u32[]{:S(2)}) copy-start(bf16[1408]{0:T(1024)(128)(2,1)} %param.27) | copy-start | bytes 8452
  56.6 8.6 %copy-start.8 = (s32[1536]{0:T(1024)S(1)}, s32[1536]{0:T(1024)}, u32[]{:S(2)}) copy-start(s32[1536]{0:T(1024)} %param.30) | copy-start | bytes 18436
  58.4 43.1 %all-to-all-start.1 = ((bf16[32,6,5632]{2,1,0:T(8,128)(2,1)}), bf16[32,6,5632]{2,1,0:T(8,128)(2,1)}, u32[]{:S(2)}, u32[]{:S(2)}) async-start(bf16[32,6,5632]{2,1,0:T(8,128)(2,1)} %broadcast_in_dim.60), calls=%async_computation.1 | async-start | bytes 5767168 | tf_op jit(solution)/shard_map/all_to_all | solution.py:107
  105.7 26.2 %copy-start.6 = (bf16[1024,128]{1,0:T(8,128)(2,1)S(1)}, bf16[1024,128]{1,0:T(8,128)(2,1)}, u32[]{:S(2)}) copy-start(bf16[1024,128]{1,0:T(8,128)(2,1)} %param.31) | copy-start | bytes 786436
  105.7 27.9 %copy-start.7 = (s32[1,1024]{1,0:T(1,128)S(1)}, s32[1,1024]{1,0:T(1,128)}, u32[]{:S(2)}) copy-start(s32[1,1024]{1,0:T(1,128)} %param.32) | copy-start | bytes 12292
  108.1 26.7 %copy-start.9 = (bf16[4096]{0:T(1024)(128)(2,1)S(1)}, bf16[4096]{0:T(1024)(128)(2,1)}, u32[]{:S(2)}) copy-start(bf16[4096]{0:T(1024)(128)(2,1)} %param.33) | copy-start | bytes 24580
  110.9 17.7 %all-to-all-start.2 = ((bf16[8,66,128]{2,1,0:T(8,128)(2,1)}), bf16[8,66,128]{2,1,0:T(8,128)(2,1)S(1)}, u32[]{:S(2)}, u32[]{:S(2)}) async-start(bf16[8,66,128]{2,1,0:T(8,128)(2,1)} %broadcast_select_fusion), calls=%async_computation.2 | async-start | bytes 294912 | tf_op jit(solution)/shard_map/all_to_all | solution.py:140
  119.4 70.7 %all-gather.2.cloned.1.call-start = ((), (), s32[]{:S(2)}) async-start(), calls=%async_computation.4 | async-start | bytes 8650752 | tf_op jit(solution)/shard_map/all_gather | solution.py:148
  133.0 195.6 %reduce-scatter.2.cloned.1.call-start = ((), (), s32[]{:S(2)}) async-start(), calls=%async_computation.5 | async-start | bytes 8650752 | tf_op jit(solution)/shard_map/reduce_scatter | solution.py:179
  195.2 10.4 %copy-start.14 = (bf16[4096,128]{1,0:T(8,128)(2,1)S(1)}, bf16[4096,128]{1,0:T(8,128)(2,1)}, u32[]{:S(2)}) copy-start(bf16[4096,128]{1,0:T(8,128)(2,1)} %param.36) | copy-start | bytes 3145732
  205.6 5.9 %copy-start.2 = (bf16[1024,4096]{1,0:T(8,128)(2,1)S(1)}, bf16[1024,4096]{1,0:T(8,128)(2,1)}, u32[]{:S(2)}) copy-start(bf16[1024,4096]{1,0:T(8,128)(2,1)} %multiply_convert_fusion) | copy-start | bytes 25165828
  205.6 6.0 %copy-start.3 = (bf16[4096,128]{1,0:T(8,128)(2,1)S(1)}, bf16[4096,128]{1,0:T(8,128)(2,1)}, u32[]{:S(2)}) copy-start(bf16[4096,128]{1,0:T(8,128)(2,1)} %param.35) | copy-start | bytes 3145732
  211.6 2.9 copy-start.4
  219.3 3.4 %copy-start.5 = (bf16[128,4096]{1,0:T(8,128)(2,1)S(1)}, bf16[128,4096]{1,0:T(8,128)(2,1)}, u32[]{:S(2)}) copy-start(bf16[128,4096]{1,0:T(8,128)(2,1)} %param.37) | copy-start | bytes 3145732
  228.3 102.1 %copy-start.1 = (bf16[5632,128]{1,0:T(8,128)(2,1)S(1)}, bf16[5632,128]{1,0:T(8,128)(2,1)}, u32[]{:S(2)}) copy-start(bf16[5632,128]{1,0:T(8,128)(2,1)} %param.28) | copy-start | bytes 4325380
Sparse Core Ops, SparseCore 0:
  133.1 56.9 all-gather.1
  228.4 100.1 reduce-scatter.1

commit v2 on v1

--- a/solution.py
+++ b/solution.py
@@ -176,12 +176,13 @@
         ),
     ).reshape(tok_grp, -1)
     out_share = tok_grp // blk_count
-    summed_heads = lax.psum_scatter(
-        jnp.dot(attn_out, out_weight, preferred_element_type=jnp.float32).astype(jnp.bfloat16),
-        "blk",
-        scatter_dimension=0,
-        tiled=True,
-    ).astype(jnp.float32)
+    head_part = jnp.dot(attn_out, out_weight, preferred_element_type=jnp.float32).astype(
+        jnp.bfloat16
+    )
+    heads_here = lax.all_to_all(
+        head_part.reshape(blk_count, out_share, head_part.shape[1]), "blk", 0, 0, tiled=False
+    )
+    summed_heads = jnp.sum(heads_here.astype(jnp.float32), axis=0)
     residual = lax.dynamic_slice_in_dim(token_values, blk_index * out_share, out_share, 0)
     return (residual + summed_heads).astype(jnp.bfloat16)
 

time: 338 us -> 373 us (1.10)
  waiting for transfers between devices: 199 us -> 223 us
  starting transfers between devices: 22.9 us -> 29.1 us
  other arithmetic: 52.9 us -> 57.8 us
    all_to_all x0 -> x1, waiting for transfers between devices: none -> 113 us  [body(): lax.all_to_all(head_part.reshape(blk_count, out_share, head_part.shape[1]...]
    reduce_scatter x1 -> x0, waiting for transfers between devices: 88.8 us -> none  [body(): lax.psum_scatter(jnp.dot(attn_out, out_weight, preferred_element_type=jnp...]
    all_to_all x0 -> x1, starting transfers between devices: none -> 6.26 us  [body(): lax.all_to_all(head_part.reshape(blk_count, out_share, head_part.shape[1]...]
    reduce_sum x0 -> x1, other arithmetic: none -> 5.23 us  [body(): summed_heads = jnp.sum(heads_here.astype(jnp.float32), axis=0)]
  transfers between devices with their start and end apart: 5 -> 5, of which waited for: 5 -> 5; matrix products, arithmetic and copies ran while one was open for 9% -> 8% of each run, Pallas kernels for 0% -> 0%
where the time goes in v2:
time: 373 us
  waiting for transfers between devices  223 us (60%)
  other arithmetic  57.8 us (15%)
  starting transfers between devices  29.1 us (8%)
  matrix products  28.2 us (8%)
  local copies, waits for them, and re-layouts  20.3 us (5%)
  between operations  13.9 us (4%)
    all_to_all x1, waiting for transfers between devices, body(): lax.all_to_all(head_part.reshape(blk_count, out_share, head_part.shape[1]...  113 us
    all_gather x1, waiting for transfers between devices, body(): features = lax.all_gather(columns, 'blk', axis=1, tiled=True)  53.9 us
    all_to_all x1, waiting for transfers between devices, body(): lax.all_to_all(partial.reshape(blk_count, row_share, vis_width), 'blk', 0...  23.6 us
    all_to_all x1, waiting for transfers between devices, body(): lax.all_to_all(jnp.broadcast_to(merged_here[None], (blk_count,) + merged_...  23.5 us
    convert_element_type x1, other arithmetic, body(): token_values = features.astype(jnp.float32)  11.5 us
    convert_element_type x1, other arithmetic, body(): normed_tokens = (token_values * lax.rsqrt(jnp.mean(token_values * token_v...  10.4 us
    all_to_all x1, waiting for transfers between devices, body(): lax.all_to_all(outgoing, 'req', split_axis=0, concat_axis=0, tiled=True)  9.18 us
    all_to_all x1, starting transfers between devices, body(): lax.all_to_all(outgoing, 'req', split_axis=0, concat_axis=0, tiled=True)  8.47 us
  transfers between devices with their start and end apart: 5, of which 5 were waited for; matrix products, arithmetic and copies ran while one was open for 8% of the time, Pallas kernels for 0%

profile of v2, /device:TPU:8, one launch (start us, length us, event | category | flops | bytes accessed | tf_op | source)
XLA Modules:
  0.0 372.6 jit_solution(7674705421859878740)
XLA Ops:
  11.7 6.4 %convolution_convert_fusion.2 = bf16[768,1408]{1,0:T(8,128)(2,1)} fusion(bf16[192,1408]{1,0:T(8,128)(2,1)S(1)} %copy-done.15, bf16[1408,192]{0,1:T(8,128)(2,1)S(1)} %copy-done.16, bf16[768,1408]{1,0:T(8,128)(2,1)} %param.20, f32[1408]{0:T(1024)S(1)} %convert_element_type.102, f32[1408]{0:T(1024)S(1)} %convert_element_type.101, ...), kind=kOutput, calls=%fused_computation.27 | convolution fusion | flops 847773696 | bytes 5424896 | tf_op jit(solution)/shard_map/dot_general | solution.py:96
  18.1 7.6 %all-to-all-start = ((bf16[32,24,1408]{2,1,0:T(8,128)(2,1)}), bf16[32,24,1408]{2,1,0:T(8,128)(2,1)}, u32[]{:S(2)}, u32[]{:S(2)}) async-start(bf16[32,24,1408]{2,1,0:T(8,128)(2,1)} %bitcast.73), calls=%async_computation | async-start | bytes 4325376 | tf_op jit(solution)/shard_map/all_to_all | solution.py:99
  25.7 3.9 %convert_element_type.100 = f32[768,1408]{1,0:T(8,128)} convert(bf16[768,1408]{1,0:T(8,128)(2,1)} %param.20) | non-fusion elementwise | flops 1081344 | bytes 6488064 | tf_op jit(solution)/shard_map/convert_element_type | solution.py:90
  29.6 23.6 %all-to-all-done = bf16[32,24,1408]{2,1,0:T(8,128)(2,1)} async-done(((bf16[32,24,1408]{2,1,0:T(8,128)(2,1)}), bf16[32,24,1408]{2,1,0:T(8,128)(2,1)}, u32[]{:S(2)}, u32[]{:S(2)}) %all-to-all-start) | async-done | bytes 2162720 | tf_op jit(solution)/shard_map/all_to_all | solution.py:99
  58.4 6.8 %all-to-all-start.1 = ((bf16[32,6,5632]{2,1,0:T(8,128)(2,1)}), bf16[32,6,5632]{2,1,0:T(8,128)(2,1)}, u32[]{:S(2)}, u32[]{:S(2)}) async-start(bf16[32,6,5632]{2,1,0:T(8,128)(2,1)} %broadcast_in_dim.60), calls=%async_computation.1 | async-start | bytes 5767168 | tf_op jit(solution)/shard_map/all_to_all | solution.py:107
  65.3 4.5 %reduce-window.6 = s32[8,8,2,128]{3,1,2,0:T(8,128)S(1)} reduce-window(s32[8,8,2,128]{3,1,2,0:T(8,128)S(1)} %convert_bitcast_fusion, s32[]{:T(128)} %constant.72.clone.1), window={size=1x1x1x128 pad=0_0x0_0x0_0x127_0}, to_apply=%region_0.0 | reduce-window | flops 2080768 | bytes 131076 | tf_op jit(solution)/shard_map/reduce-window
  71.8 6.2 %scatter_custom_fusion = s32[1024]{0:T(1024)S(1)} fusion(s32[1536]{0:T(1024)S(1)} %get-tuple-element.76, s32[1536]{0:T(1024)S(1)} %reshape.306, s32[]{:T(128)} %constant.70.clone.1), kind=kCustom, calls=%fused_computation.144 | custom fusion | bytes 4100 | tf_op jit(solution)/shard_map/scatter | solution.py:144
  78.0 23.5 %all-to-all-done.1 = bf16[32,6,5632]{2,1,0:T(8,128)(2,1)} async-done(((bf16[32,6,5632]{2,1,0:T(8,128)(2,1)}), bf16[32,6,5632]{2,1,0:T(8,128)(2,1)}, u32[]{:S(2)}, u32[]{:S(2)}) %all-to-all-start.1) | async-done | bytes 2162720 | tf_op jit(solution)/shard_map/all_to_all | solution.py:107
  101.5 4.3 %reshape.280 = bf16[192,5632]{1,0:T(8,128)(2,1)} reshape(bf16[32,6,5632]{2,1,0:T(8,128)(2,1)} %all-to-all-done.1) | data formatting | bytes 4325376 | tf_op jit(solution)/shard_map/reshape | solution.py:115
  110.9 8.5 %all-to-all-start.2 = ((bf16[8,66,128]{2,1,0:T(8,128)(2,1)}), bf16[8,66,128]{2,1,0:T(8,128)(2,1)S(1)}, u32[]{:S(2)}, u32[]{:S(2)}) async-start(bf16[8,66,128]{2,1,0:T(8,128)(2,1)} %broadcast_select_fusion), calls=%async_computation.2 | async-start | bytes 294912 | tf_op jit(solution)/shard_map/all_to_all | solution.py:140
  119.5 9.2 %all-to-all-done.2 = bf16[8,66,128]{2,1,0:T(8,128)(2,1)S(1)} async-done(((bf16[8,66,128]{2,1,0:T(8,128)(2,1)}), bf16[8,66,128]{2,1,0:T(8,128)(2,1)S(1)}, u32[]{:S(2)}, u32[]{:S(2)}) %all-to-all-start.2) | async-done | bytes 135200 | tf_op jit(solution)/shard_map/all_to_all | solution.py:140
  128.7 3.2 gather_fusion.1
  136.2 53.9 %all-gather.2.cloned.1.call-done = bf16[1024,4096]{1,0:T(8,128)(2,1)} async-done(((bf16[1024,128]{1,0:T(8,128)(2,1)}), bf16[1024,4096]{1,0:T(8,128)(2,1)}) %all-gather.2.cloned.1.call-update) | async-done | bytes 8388624 | tf_op jit(solution)/shard_map/all_gather | solution.py:148
  190.1 5.1 %multiply_reduce_fusion = f32[1024]{0:T(1024)S(1)} fusion(bf16[1024,4096]{1,0:T(8,128)(2,1)} %all-gather.2.cloned.1.call-done), kind=kLoop, calls=%fused_computation.17 | loop fusion | flops 12581888 | bytes 8392704 | tf_op jit(solution)/shard_map/reduce_sum | solution.py:152
  195.2 10.4 %multiply_convert_fusion = bf16[1024,4096]{1,0:T(8,128)(2,1)} fusion(f32[4096]{0:T(1024)S(1)} %convert_element_type.114, f32[1024]{0:T(1024)S(1)} %add_rsqrt_fusion, bf16[1024,4096]{1,0:T(8,128)(2,1)} %all-gather.2.cloned.1.call-done), kind=kLoop, calls=%fused_computation.16 | loop fusion | flops 16777216 | bytes 16797696 | tf_op jit(solution)/shard_map/convert_element_type | solution.py:154
  205.6 5.9 %convolution_convert_fusion.3 = bf16[1024,128]{1,0:T(8,128)(2,1)S(1)} fusion(bf16[1024,4096]{1,0:T(8,128)(2,1)} %multiply_convert_fusion, bf16[4096,128]{1,0:T(8,128)(2,1)S(1)} %copy-done.14), kind=kOutput, calls=%fused_computation.33 | convolution fusion | flops 1073872896 | bytes 9699328 | tf_op jit(solution)/shard_map/dot_general | solution.py:162
  211.6 2.9 convolution_bitcast_fusion
  214.5 2.9 convolution_bitcast_fusion.1
  219.1 3.6 while.10
  222.7 5.5 %convolution_convert_fusion.1 = bf16[1024,4096]{1,0:T(8,128)(2,1)} fusion(bf16[1024,128]{1,0:T(8,128)(2,1)S(1)} %bitcast.74, bf16[128,4096]{1,0:T(8,128)(2,1)S(1)} %copy-done.5), kind=kOutput, calls=%fused_computation.18 | convolution fusion | flops 1077936128 | bytes 9699328 | tf_op jit(solution)/shard_map/dot_general | solution.py:179
  228.3 6.3 %all-to-all-start.3 = ((bf16[32,32,4096]{2,1,0:T(8,128)(2,1)}), bf16[32,32,4096]{2,1,0:T(8,128)(2,1)}, u32[]{:S(2)}, u32[]{:S(2)}) async-start(bf16[32,32,4096]{2,1,0:T(8,128)(2,1)} %bitcast.71), calls=%async_computation.3 | async-start | bytes 16777216 | tf_op jit(solution)/shard_map/all_to_all | solution.py:182
  234.5 11.5 %convert_element_type.113 = f32[1024,4096]{1,0:T(8,128)} convert(bf16[1024,4096]{1,0:T(8,128)(2,1)} %all-gather.2.cloned.1.call-done) | non-fusion elementwise | flops 4194304 | bytes 25165824 | tf_op jit(solution)/shard_map/convert_element_type | solution.py:149
  246.0 112.7 %all-to-all-done.3 = bf16[32,32,4096]{2,1,0:T(8,128)(2,1)} async-done(((bf16[32,32,4096]{2,1,0:T(8,128)(2,1)}), bf16[32,32,4096]{2,1,0:T(8,128)(2,1)}, u32[]{:S(2)}, u32[]{:S(2)}) %all-to-all-start.3) | async-done | bytes 8388640 | tf_op jit(solution)/shard_map/all_to_all | solution.py:182
  358.7 5.2 %convert_reduce_fusion = f32[32,4096]{1,0:T(8,128)S(1)} fusion(bf16[32,32,4096]{2,1,0:T(8,128)(2,1)} %all-to-all-done.3), kind=kLoop, calls=%fused_computation.15 | loop fusion | flops 8257536 | bytes 8912896 | tf_op jit(solution)/shard_map/reduce_sum | solution.py:185
  (110 shorter events, 28.6 us)
Async XLA Ops:
  6.5 99.2 %copy-start = (bf16[5632,128]{1,0:T(8,128)(2,1)S(1)}, bf16[5632,128]{1,0:T(8,128)(2,1)}, u32[]{:S(2)}) copy-start(bf16[5632,128]{1,0:T(8,128)(2,1)} %param.28) | copy-start | bytes 4325380
  6.5 5.1 %copy-start.10 = (bf16[1408]{0:T(1024)(128)(2,1)S(1)}, bf16[1408]{0:T(1024)(128)(2,1)}, u32[]{:S(2)}) copy-start(bf16[1408]{0:T(1024)(128)(2,1)} %param.21) | copy-start | bytes 8452
  6.5 5.1 %copy-start.11 = (bf16[1408]{0:T(1024)(128)(2,1)S(1)}, bf16[1408]{0:T(1024)(128)(2,1)}, u32[]{:S(2)}) copy-start(bf16[1408]{0:T(1024)(128)(2,1)} %param.22) | copy-start | bytes 8452
  6.5 5.2 %copy-start.15 = (bf16[192,1408]{1,0:T(8,128)(2,1)S(1)}, bf16[192,1408]{1,0:T(8,128)(2,1)}, u32[]{:S(2)}) copy-start(bf16[192,1408]{1,0:T(8,128)(2,1)} %param.25) | copy-start | bytes 1622020
  6.5 5.2 %copy-start.16 = (bf16[1408,192]{0,1:T(8,128)(2,1)S(1)}, bf16[1408,192]{0,1:T(8,128)(2,1)}, u32[]{:S(2)}) copy-start(bf16[1408,192]{0,1:T(8,128)(2,1)} %param.23) | copy-start | bytes 1622020
  18.1 35.2 %all-to-all-start = ((bf16[32,24,1408]{2,1,0:T(8,128)(2,1)}), bf16[32,24,1408]{2,1,0:T(8,128)(2,1)}, u32[]{:S(2)}, u32[]{:S(2)}) async-start(bf16[32,24,1408]{2,1,0:T(8,128)(2,1)} %bitcast.73), calls=%async_computation | async-start | bytes 4325376 | tf_op jit(solution)/shard_map/all_to_all | solution.py:99
  25.7 3.9 %copy-start.17 = (bf16[128]{0:T(256)(128)(2,1)S(1)}, bf16[128]{0:T(256)(128)(2,1)}, u32[]{:S(2)}) copy-start(bf16[128]{0:T(256)(128)(2,1)} %param.29) | copy-start | bytes 772
  25.7 3.9 %copy-start.12 = (bf16[1408]{0:T(1024)(128)(2,1)S(1)}, bf16[1408]{0:T(1024)(128)(2,1)}, u32[]{:S(2)}) copy-start(bf16[1408]{0:T(1024)(128)(2,1)} %param.26) | copy-start | bytes 8452
  25.7 3.9 %copy-start.13 = (bf16[1408]{0:T(1024)(128)(2,1)S(1)}, bf16[1408]{0:T(1024)(128)(2,1)}, u32[]{:S(2)}) copy-start(bf16[1408]{0:T(1024)(128)(2,1)} %param.27) | copy-start | bytes 8452
  56.6 8.6 %copy-start.8 = (s32[1536]{0:T(1024)S(1)}, s32[1536]{0:T(1024)}, u32[]{:S(2)}) copy-start(s32[1536]{0:T(1024)} %param.30) | copy-start | bytes 18436
  58.4 43.1 %all-to-all-start.1 = ((bf16[32,6,5632]{2,1,0:T(8,128)(2,1)}), bf16[32,6,5632]{2,1,0:T(8,128)(2,1)}, u32[]{:S(2)}, u32[]{:S(2)}) async-start(bf16[32,6,5632]{2,1,0:T(8,128)(2,1)} %broadcast_in_dim.60), calls=%async_computation.1 | async-start | bytes 5767168 | tf_op jit(solution)/shard_map/all_to_all | solution.py:107
  105.7 26.2 %copy-start.6 = (bf16[1024,128]{1,0:T(8,128)(2,1)S(1)}, bf16[1024,128]{1,0:T(8,128)(2,1)}, u32[]{:S(2)}) copy-start(bf16[1024,128]{1,0:T(8,128)(2,1)} %param.31) | copy-start | bytes 786436
  105.7 27.8 %copy-start.7 = (s32[1,1024]{1,0:T(1,128)S(1)}, s32[1,1024]{1,0:T(1,128)}, u32[]{:S(2)}) copy-start(s32[1,1024]{1,0:T(1,128)} %param.32) | copy-start | bytes 12292
  108.1 26.6 %copy-start.9 = (bf16[4096]{0:T(1024)(128)(2,1)S(1)}, bf16[4096]{0:T(1024)(128)(2,1)}, u32[]{:S(2)}) copy-start(bf16[4096]{0:T(1024)(128)(2,1)} %param.33) | copy-start | bytes 24580
  110.9 17.7 %all-to-all-start.2 = ((bf16[8,66,128]{2,1,0:T(8,128)(2,1)}), bf16[8,66,128]{2,1,0:T(8,128)(2,1)S(1)}, u32[]{:S(2)}, u32[]{:S(2)}) async-start(bf16[8,66,128]{2,1,0:T(8,128)(2,1)} %broadcast_select_fusion), calls=%async_computation.2 | async-start | bytes 294912 | tf_op jit(solution)/shard_map/all_to_all | solution.py:140
  119.4 70.7 %all-gather.2.cloned.1.call-start = ((), (), s32[]{:S(2)}) async-start(), calls=%async_computation.4 | async-start | bytes 8650752 | tf_op jit(solution)/shard_map/all_gather | solution.py:148
  195.2 10.4 %copy-start.14 = (bf16[4096,128]{1,0:T(8,128)(2,1)S(1)}, bf16[4096,128]{1,0:T(8,128)(2,1)}, u32[]{:S(2)}) copy-start(bf16[4096,128]{1,0:T(8,128)(2,1)} %param.36) | copy-start | bytes 3145732
  205.6 5.9 %copy-start.2 = (bf16[1024,4096]{1,0:T(8,128)(2,1)S(1)}, bf16[1024,4096]{1,0:T(8,128)(2,1)}, u32[]{:S(2)}) copy-start(bf16[1024,4096]{1,0:T(8,128)(2,1)} %multiply_convert_fusion) | copy-start | bytes 25165828
  205.6 6.0 %copy-start.3 = (bf16[4096,128]{1,0:T(8,128)(2,1)S(1)}, bf16[4096,128]{1,0:T(8,128)(2,1)}, u32[]{:S(2)}) copy-start(bf16[4096,128]{1,0:T(8,128)(2,1)} %param.35) | copy-start | bytes 3145732
  211.6 2.9 copy-start.4
  219.1 3.7 copy-start.5
  228.3 130.4 %all-to-all-start.3 = ((bf16[32,32,4096]{2,1,0:T(8,128)(2,1)}), bf16[32,32,4096]{2,1,0:T(8,128)(2,1)}, u32[]{:S(2)}, u32[]{:S(2)}) async-start(bf16[32,32,4096]{2,1,0:T(8,128)(2,1)} %bitcast.71), calls=%async_computation.3 | async-start | bytes 16777216 | tf_op jit(solution)/shard_map/all_to_all | solution.py:182
  234.5 131.2 %copy-start.1 = (bf16[5632,128]{1,0:T(8,128)(2,1)S(1)}, bf16[5632,128]{1,0:T(8,128)(2,1)}, u32[]{:S(2)}) copy-start(bf16[5632,128]{1,0:T(8,128)(2,1)} %param.28) | copy-start | bytes 4325380
Sparse Core Ops, SparseCore 0:
  133.1 56.9 all-gather.1

commit v3 on v1

--- a/solution.py
+++ b/solution.py
@@ -87,6 +87,7 @@
     blk_index = lax.axis_index("blk")
     req_index = lax.axis_index("req")
     vis_width = patches.shape[1]
+    gathered_text = lax.all_gather(text_embed, "blk", axis=1, tiled=True)
     patch_rows = patches.astype(jnp.float32)
     normed = layer_norm(patch_rows, vis_ln_gain, vis_ln_bias).astype(jnp.bfloat16)
     pre_act = jnp.dot(normed, vis_up, preferred_element_type=jnp.float32) + vis_up_bias.astype(
@@ -139,13 +140,28 @@
     outgoing = jnp.take(jnp.concatenate([image_cols, filler], axis=0), source_row, axis=0)
     incoming = lax.all_to_all(outgoing, "req", split_axis=0, concat_axis=0, tiled=True)
     arrival = (jnp.arange(req_count, dtype=jnp.int32)[:, None] * capacity + slot_index).reshape(-1)
-    row_table = jnp.concatenate([incoming, filler], axis=0)
-    missing = row_table.shape[0] - 1
-    lookup = jnp.full((tok_grp,), missing, jnp.int32).at[target].set(arrival, mode="drop")
-    columns = jnp.where(
-        (lookup < missing)[:, None], jnp.take(row_table, lookup, axis=0), text_embed
-    )
-    features = lax.all_gather(columns, "blk", axis=1, tiled=True)
+    mine = (dest_group == req_index).astype(jnp.int32)
+    rank = jnp.cumsum(mine) - mine
+    total_images = image_dest.shape[0]
+    pick = (
+        jnp.zeros((image_count,), jnp.int32)
+        .at[jnp.where(mine > 0, rank, image_count)]
+        .set(jnp.arange(total_images, dtype=jnp.int32), mode="drop")
+    )
+    mine_cols = jnp.take(incoming, jnp.take(arrival, pick), axis=0)
+    mine_rows = lax.all_to_all(
+        jnp.broadcast_to(mine_cols[None], (blk_count,) + mine_cols.shape), "blk", 0, 0, tiled=False
+    )
+    mine_rows = mine_rows.transpose(1, 0, 2).reshape(image_count, -1)
+    lookup = (
+        jnp.full((tok_grp,), image_count, jnp.int32)
+        .at[jnp.take(dest_local, pick)]
+        .set(jnp.arange(image_count, dtype=jnp.int32))
+    )
+    row_table = jnp.concatenate([mine_rows, jnp.zeros_like(mine_rows[:1])], axis=0)
+    features = jnp.where(
+        (lookup < image_count)[:, None], jnp.take(row_table, lookup, axis=0), gathered_text
+    )
     token_values = features.astype(jnp.float32)
     normed_tokens = (
         token_values

time: 338 us -> 336 us (level)
  waiting for transfers between devices: 199 us -> 173 us
  local copies, waits for them, and re-layouts: 20.3 us -> 33.3 us
  starting transfers between devices: 22.9 us -> 31.5 us
  matrix products: 28.3 us -> 31.9 us
    all_gather x1, waiting for transfers between devices: 53.9 us -> 0.01 us  [body(): gathered_text = lax.all_gather(text_embed, 'blk', axis=1, tiled=True)]
    all_to_all x0 -> x1, waiting for transfers between devices: none -> 15 us  [body(): lax.all_to_all(jnp.broadcast_to(mine_cols[None], (blk_count,) + mine_cols...]
    all_to_all x1, waiting for transfers between devices: 23.5 us -> 32.3 us  [body(): lax.all_to_all(jnp.broadcast_to(merged_here[None], (blk_count,) + merged_...]
    all_to_all x0 -> x1, starting transfers between devices: none -> 6.67 us  [body(): lax.all_to_all(jnp.broadcast_to(mine_cols[None], (blk_count,) + mine_cols...]
    reduce_scatter x1, waiting for transfers between devices: 88.8 us -> 94.4 us  [body(): lax.psum_scatter(jnp.dot(attn_out, out_weight, preferred_element_type=jnp...]
    gather x1, local copies, waits for them, and re-layouts: 3.2 us -> 7.82 us  [body(): jnp.take(row_table, lookup, axis=0)]
    gather x0 -> x3, local copies, waits for them, and re-layouts: none -> 3.67 us  [the longest x2 2.23 us: body(): mine_cols = jnp.take(incoming, jnp.take(arrival, pick), axis=0)]
    dot_general x1, matrix products: 2.9 us -> 6.43 us  [body(): jnp.dot(normed_tokens, key_weight, preferred_element_type=jnp.float32)]
  transfers between devices with their start and end apart: 5 -> 6, of which waited for: 5 -> 5; matrix products, arithmetic and copies ran while one was open for 9% -> 19% of each run, Pallas kernels for 0% -> 0%
where the time goes in v3:
time: 336 us; the launch traced here: 335 us
  waiting for transfers between devices  173 us (51%)
  other arithmetic  51.5 us (15%)
  local copies, waits for them, and re-layouts  33.3 us (10%)
  matrix products  31.9 us (9%)
  starting transfers between devices  31.5 us (9%)
  between operations  14 us (4%)
    reduce_scatter x1, waiting for transfers between devices, body(): lax.psum_scatter(jnp.dot(attn_out, out_weight, preferred_element_type=jnp...  94.4 us
    all_to_all x1, waiting for transfers between devices, body(): lax.all_to_all(jnp.broadcast_to(merged_here[None], (blk_count,) + merged_...  32.3 us
    all_to_all x1, waiting for transfers between devices, body(): lax.all_to_all(partial.reshape(blk_count, row_share, vis_width), 'blk', 0...  21.2 us
    all_to_all x1, waiting for transfers between devices, body(): lax.all_to_all(jnp.broadcast_to(mine_cols[None], (blk_count,) + mine_cols...  15 us
    convert_element_type x1, other arithmetic, body(): token_values = features.astype(jnp.float32)  12.9 us
    convert_element_type x1, other arithmetic, body(): normed_tokens = (token_values * lax.rsqrt(jnp.mean(token_values * token_v...  10.4 us
    all_to_all x1, starting transfers between devices, body(): lax.all_to_all(outgoing, 'req', split_axis=0, concat_axis=0, tiled=True)  10.1 us
    all_to_all x1, waiting for transfers between devices, body(): lax.all_to_all(outgoing, 'req', split_axis=0, concat_axis=0, tiled=True)  9.53 us
  transfers between devices with their start and end apart: 6, of which 5 were waited for; matrix products, arithmetic and copies ran while one was open for 19% of the time, Pallas kernels for 0%

profile of v3, /device:TPU:8, one launch (start us, length us, event | category | flops | bytes accessed | tf_op | source)
XLA Modules:
  0.0 335.4 jit_solution(8747419351665086077)
XLA Ops:
  11.3 2.3 multiply_reduce_fusion.1
  13.6 6.4 %convolution_convert_fusion.2 = bf16[768,1408]{1,0:T(8,128)(2,1)} fusion(bf16[192,1408]{1,0:T(8,128)(2,1)S(1)} %copy-done.12, bf16[1408,192]{0,1:T(8,128)(2,1)S(1)} %copy-done.13, bf16[768,1408]{1,0:T(8,128)(2,1)} %param.22, f32[1408]{0:T(1024)S(1)} %convert_element_type.106, f32[1408]{0:T(1024)S(1)} %convert_element_type.105, ...), kind=kOutput, calls=%fused_computation.31 | convolution fusion | flops 847773696 | bytes 5424896 | tf_op jit(solution)/shard_map/dot_general | solution.py:97
  20.0 7.6 %all-to-all-start = ((bf16[32,24,1408]{2,1,0:T(8,128)(2,1)}), bf16[32,24,1408]{2,1,0:T(8,128)(2,1)}, u32[]{:S(2)}, u32[]{:S(2)}) async-start(bf16[32,24,1408]{2,1,0:T(8,128)(2,1)} %bitcast.79), calls=%async_computation | async-start | bytes 4325376 | tf_op jit(solution)/shard_map/all_to_all | solution.py:100
  27.6 3.9 %convert_element_type.104 = f32[768,1408]{1,0:T(8,128)} convert(bf16[768,1408]{1,0:T(8,128)(2,1)} %param.22) | non-fusion elementwise | flops 1081344 | bytes 6488064 | tf_op jit(solution)/shard_map/convert_element_type | solution.py:91
  31.7 4.5 %reduce-window.19 = s32[8,8,2,128]{3,1,2,0:T(8,128)S(1)} reduce-window(s32[8,8,2,128]{3,1,2,0:T(8,128)S(1)} %convert_bitcast_fusion, s32[]{:T(128)} %constant.55.clone.1), window={size=1x1x1x128 pad=0_0x0_0x0_0x127_0}, to_apply=%region_4.6 | reduce-window | flops 2080768 | bytes 131076 | tf_op jit(solution)/shard_map/reduce-window.2
  36.5 21.2 %all-to-all-done = bf16[32,24,1408]{2,1,0:T(8,128)(2,1)} async-done(((bf16[32,24,1408]{2,1,0:T(8,128)(2,1)}), bf16[32,24,1408]{2,1,0:T(8,128)(2,1)}, u32[]{:S(2)}, u32[]{:S(2)}) %all-to-all-start) | async-done | bytes 2162720 | tf_op jit(solution)/shard_map/all_to_all | solution.py:100
  62.9 6.9 %all-to-all-start.1 = ((bf16[32,6,5632]{2,1,0:T(8,128)(2,1)}), bf16[32,6,5632]{2,1,0:T(8,128)(2,1)}, u32[]{:S(2)}, u32[]{:S(2)}) async-start(bf16[32,6,5632]{2,1,0:T(8,128)(2,1)} %broadcast_in_dim.132), calls=%async_computation.1 | async-start | bytes 5767168 | tf_op jit(solution)/shard_map/all_to_all | solution.py:108
  72.1 6.2 %scatter_custom_fusion = s32[192]{0:T(256)S(1)} fusion(s32[1536]{0:T(1024)S(1)} %compare_select_fusion, s32[1536]{0:T(1024)S(1)} %iota.44, s32[]{:T(128)} %constant.55.clone.1), kind=kCustom, calls=%fused_computation.171 | custom fusion | bytes 772 | tf_op jit(solution)/shard_map/scatter | solution.py:149
  79.8 32.3 %all-to-all-done.1 = bf16[32,6,5632]{2,1,0:T(8,128)(2,1)} async-done(((bf16[32,6,5632]{2,1,0:T(8,128)(2,1)}), bf16[32,6,5632]{2,1,0:T(8,128)(2,1)}, u32[]{:S(2)}, u32[]{:S(2)}) %all-to-all-start.1) | async-done | bytes 2162720 | tf_op jit(solution)/shard_map/all_to_all | solution.py:108
  112.1 4.4 %reshape.319 = bf16[192,5632]{1,0:T(8,128)(2,1)} reshape(bf16[32,6,5632]{2,1,0:T(8,128)(2,1)} %all-to-all-done.1) | data formatting | bytes 4325376 | tf_op jit(solution)/shard_map/reshape | solution.py:116
  116.4 2.4 fusion.11
  121.6 10.1 %all-to-all-start.2 = ((bf16[8,66,128]{2,1,0:T(8,128)(2,1)}), bf16[8,66,128]{2,1,0:T(8,128)(2,1)S(1)}, u32[]{:S(2)}, u32[]{:S(2)}) async-start(bf16[8,66,128]{2,1,0:T(8,128)(2,1)} %broadcast_select_fusion), calls=%async_computation.2 | async-start | bytes 294912 | tf_op jit(solution)/shard_map/all_to_all | solution.py:141
  131.8 9.5 %all-to-all-done.2 = bf16[8,66,128]{2,1,0:T(8,128)(2,1)S(1)} async-done(((bf16[8,66,128]{2,1,0:T(8,128)(2,1)}), bf16[8,66,128]{2,1,0:T(8,128)(2,1)S(1)}, u32[]{:S(2)}, u32[]{:S(2)}) %all-to-all-start.2) | async-done | bytes 135200 | tf_op jit(solution)/shard_map/all_to_all | solution.py:141
  143.7 6.7 %all-to-all-start.3 = ((bf16[32,192,128]{2,1,0:T(8,128)(2,1)}), bf16[32,192,128]{2,1,0:T(8,128)(2,1)S(1)}, u32[]{:S(2)}, u32[]{:S(2)}) async-start(bf16[32,192,128]{2,1,0:T(8,128)(2,1)} %broadcast_in_dim.137), calls=%async_computation.3 | async-start | bytes 3145728 | tf_op jit(solution)/shard_map/all_to_all | solution.py:152
  156.3 15.0 %all-to-all-done.3 = bf16[32,192,128]{2,1,0:T(8,128)(2,1)S(1)} async-done(((bf16[32,192,128]{2,1,0:T(8,128)(2,1)}), bf16[32,192,128]{2,1,0:T(8,128)(2,1)S(1)}, u32[]{:S(2)}, u32[]{:S(2)}) %all-to-all-start.3) | async-done | bytes 1572896 | tf_op jit(solution)/shard_map/all_to_all | solution.py:152
  171.7 7.8 %gather_fusion.2 = bf16[1024,4096]{1,0:T(8,128)(2,1)} fusion(bf16[193,4096]{1,0:T(8,128)(2,1)S(1)} %concatenate.15, s32[1024]{0:T(1024)S(1)} %fusion.76), kind=kCustom, calls=%fused_computation.4 | custom fusion | bytes 16781312 | tf_op jit(solution)/shard_map/jit(_take)/gather | solution.py:163
  179.6 12.9 %fusion.114 = (f32[1024,4096]{1,0:T(8,128)}, bf16[1024,4096]{1,0:T(8,128)(2,1)S(1)}) fusion(bf16[1024,4096]{1,0:T(8,128)(2,1)} %all-gather.2.cloned.1.call-done, bf16[1024,4096]{1,0:T(8,128)(2,1)} %gather_fusion.2, pred[1024]{0:T(1024)(128)(4,1)S(1)} %get-tuple-element.94, pred[1024]{0:T(1024)(128)(4,1)S(1)} %get-tuple-element.93), kind=kLoop, calls=%fused_computation.204 | loop fusion | flops 12582912 | bytes 41945088 | tf_op jit(solution)/shard_map/convert_element_type | solution.py:165
  195.7 10.4 %multiply_convert_fusion = bf16[1024,4096]{1,0:T(8,128)(2,1)} fusion(f32[4096]{0:T(1024)S(1)} %convert_element_type.118, f32[1024]{0:T(1024)S(1)} %add_rsqrt_fusion, bf16[1024,4096]{1,0:T(8,128)(2,1)} %copy-done.3), kind=kLoop, calls=%fused_computation.19 | loop fusion | flops 16777216 | bytes 16797696 | tf_op jit(solution)/shard_map/convert_element_type | solution.py:170
  206.1 6.4 %convolution_bitcast_fusion = f32[1024,1,128]{0,2,1:T(8,128)S(1)} fusion(bf16[1024,4096]{1,0:T(8,128)(2,1)} %multiply_convert_fusion, bf16[4096,128]{1,0:T(8,128)(2,1)S(1)} %copy-done.4), kind=kOutput, calls=%fused_computation.35 | convolution fusion | flops 1073741824 | bytes 9961472 | tf_op jit(solution)/shard_map/dot_general | solution.py:176
  212.6 2.9 convolution_bitcast_fusion.1
  217.3 5.9 %convolution_convert_fusion.3 = bf16[1024,128]{1,0:T(8,128)(2,1)S(1)} fusion(bf16[1024,4096]{1,0:T(8,128)(2,1)} %multiply_convert_fusion, bf16[4096,128]{1,0:T(8,128)(2,1)} %param.38), kind=kOutput, calls=%fused_computation.38 | convolution fusion | flops 1073872896 | bytes 9699328 | tf_op jit(solution)/shard_map/dot_general | solution.py:178
  223.3 3.4 %while.10 = (s32[]{:T(128)}, bf16[2,512,128]{2,1,0:T(8,128)(2,1)S(1)}, pred[2,512,1024]{2,1,0:T(32,128)(4,1)S(1)}, bf16[2,512,128]{2,1,0:T(8,128)(2,1)S(1)}, bf1...) while((s32[]{:T(128)}, bf16[2,512,128]{2,1,0:T(8,128)(2,1)S(1)}, ...), condition=%wide.region_18.20_spmd, body=%wide.region_15.19_spmd.sunk | while | flops 272694272 | bytes 7613521 | solution.py:187
  226.7 5.6 %convolution_convert_fusion.1 = bf16[1024,4096]{1,0:T(8,128)(2,1)} fusion(bf16[1024,128]{1,0:T(8,128)(2,1)S(1)} %bitcast.80, bf16[128,4096]{1,0:T(8,128)(2,1)S(1)} %copy-done.6), kind=kOutput, calls=%fused_computation.22 | convolution fusion | flops 1077936128 | bytes 9699328 | tf_op jit(solution)/shard_map/dot_general | solution.py:196
  232.3 94.4 %reduce-scatter.2.cloned.1.call-done = bf16[32,4096]{1,0:T(8,128)(2,1)} async-done(((bf16[1024,4096]{1,0:T(8,128)(2,1)}), bf16[32,4096]{1,0:T(8,128)(2,1)}) %reduce-scatter.2.cloned.1.call-update) | async-done | bytes 262160 | tf_op jit(solution)/shard_map/reduce_scatter | solution.py:195
  (125 shorter events, 35.7 us)
Async XLA Ops:
  6.5 109.9 %copy-start = (bf16[5632,128]{1,0:T(8,128)(2,1)S(1)}, bf16[5632,128]{1,0:T(8,128)(2,1)}, u32[]{:S(2)}) copy-start(bf16[5632,128]{1,0:T(8,128)(2,1)} %param.30) | copy-start | bytes 4325380
  6.5 7.1 %copy-start.13 = (bf16[1408,192]{0,1:T(8,128)(2,1)S(1)}, bf16[1408,192]{0,1:T(8,128)(2,1)}, u32[]{:S(2)}) copy-start(bf16[1408,192]{0,1:T(8,128)(2,1)} %param.25) | copy-start | bytes 1622020
  6.5 7.1 %copy-start.12 = (bf16[192,1408]{1,0:T(8,128)(2,1)S(1)}, bf16[192,1408]{1,0:T(8,128)(2,1)}, u32[]{:S(2)}) copy-start(bf16[192,1408]{1,0:T(8,128)(2,1)} %param.27) | copy-start | bytes 1622020
  6.5 173.0 %all-gather.2.cloned.1.call-start = ((), (), s32[]{:S(2)}) async-start(), calls=%async_computation.5 | async-start | bytes 8650752 | tf_op jit(solution)/shard_map/all_gather | solution.py:90
  20.0 37.8 %all-to-all-start = ((bf16[32,24,1408]{2,1,0:T(8,128)(2,1)}), bf16[32,24,1408]{2,1,0:T(8,128)(2,1)}, u32[]{:S(2)}, u32[]{:S(2)}) async-start(bf16[32,24,1408]{2,1,0:T(8,128)(2,1)} %bitcast.79), calls=%async_computation | async-start | bytes 4325376 | tf_op jit(solution)/shard_map/all_to_all | solution.py:100
  27.6 3.9 %copy-start.10 = (bf16[1408]{0:T(1024)(128)(2,1)S(1)}, bf16[1408]{0:T(1024)(128)(2,1)}, u32[]{:S(2)}) copy-start(bf16[1408]{0:T(1024)(128)(2,1)} %param.28) | copy-start | bytes 8452
  27.6 3.9 %copy-start.11 = (bf16[1408]{0:T(1024)(128)(2,1)S(1)}, bf16[1408]{0:T(1024)(128)(2,1)}, u32[]{:S(2)}) copy-start(bf16[1408]{0:T(1024)(128)(2,1)} %param.29) | copy-start | bytes 8452
  27.6 3.9 %copy-start.7 = (s32[1536]{0:T(1024)S(1)}, s32[1536]{0:T(1024)}, u32[]{:S(2)}) copy-start(s32[1536]{0:T(1024)} %param.32) | copy-start | bytes 18436
  61.1 8.9 %copy-start.14 = (bf16[128]{0:T(256)(128)(2,1)S(1)}, bf16[128]{0:T(256)(128)(2,1)}, u32[]{:S(2)}) copy-start(bf16[128]{0:T(256)(128)(2,1)} %param.31) | copy-start | bytes 772
  62.9 49.2 %all-to-all-start.1 = ((bf16[32,6,5632]{2,1,0:T(8,128)(2,1)}), bf16[32,6,5632]{2,1,0:T(8,128)(2,1)}, u32[]{:S(2)}, u32[]{:S(2)}) async-start(bf16[32,6,5632]{2,1,0:T(8,128)(2,1)} %broadcast_in_dim.132), calls=%async_computation.1 | async-start | bytes 5767168 | tf_op jit(solution)/shard_map/all_to_all | solution.py:108
  118.8 33.3 %copy-start.9 = (bf16[4096]{0:T(1024)(128)(2,1)S(1)}, bf16[4096]{0:T(1024)(128)(2,1)}, u32[]{:S(2)}) copy-start(bf16[4096]{0:T(1024)(128)(2,1)} %param.35) | copy-start | bytes 24580
  118.8 33.3 %copy-start.8 = (s32[1,1024]{1,0:T(1,128)S(1)}, s32[1,1024]{1,0:T(1,128)}, u32[]{:S(2)}) copy-start(s32[1,1024]{1,0:T(1,128)} %param.34) | copy-start | bytes 12292
  121.6 19.7 %all-to-all-start.2 = ((bf16[8,66,128]{2,1,0:T(8,128)(2,1)}), bf16[8,66,128]{2,1,0:T(8,128)(2,1)S(1)}, u32[]{:S(2)}, u32[]{:S(2)}) async-start(bf16[8,66,128]{2,1,0:T(8,128)(2,1)} %broadcast_select_fusion), calls=%async_computation.2 | async-start | bytes 294912 | tf_op jit(solution)/shard_map/all_to_all | solution.py:141
  143.7 27.6 %all-to-all-start.3 = ((bf16[32,192,128]{2,1,0:T(8,128)(2,1)}), bf16[32,192,128]{2,1,0:T(8,128)(2,1)S(1)}, u32[]{:S(2)}, u32[]{:S(2)}) async-start(bf16[32,192,128]{2,1,0:T(8,128)(2,1)} %broadcast_in_dim.137), calls=%async_computation.3 | async-start | bytes 3145728 | tf_op jit(solution)/shard_map/all_to_all | solution.py:152
  150.4 176.3 %reduce-scatter.2.cloned.1.call-start = ((), (), s32[]{:S(2)}) async-start(), calls=%async_computation.6 | async-start | bytes 8650752 | tf_op jit(solution)/shard_map/reduce_scatter | solution.py:195
  192.5 3.2 copy-start.3
  195.7 10.4 %copy-start.4 = (bf16[4096,128]{1,0:T(8,128)(2,1)S(1)}, bf16[4096,128]{1,0:T(8,128)(2,1)}, u32[]{:S(2)}) copy-start(bf16[4096,128]{1,0:T(8,128)(2,1)} %param.37) | copy-start | bytes 3145732
  206.1 6.4 %copy-start.2 = (bf16[1024,4096]{1,0:T(8,128)(2,1)S(1)}, bf16[1024,4096]{1,0:T(8,128)(2,1)}, u32[]{:S(2)}) copy-start(bf16[1024,4096]{1,0:T(8,128)(2,1)} %multiply_convert_fusion) | copy-start | bytes 25165828
  206.1 6.4 %copy-start.5 = (bf16[4096,128]{1,0:T(8,128)(2,1)S(1)}, bf16[4096,128]{1,0:T(8,128)(2,1)}, u32[]{:S(2)}) copy-start(bf16[4096,128]{1,0:T(8,128)(2,1)} %param.36) | copy-start | bytes 3145732
  223.3 3.4 %copy-start.6 = (bf16[128,4096]{1,0:T(8,128)(2,1)S(1)}, bf16[128,4096]{1,0:T(8,128)(2,1)}, u32[]{:S(2)}) copy-start(bf16[128,4096]{1,0:T(8,128)(2,1)} %param.39) | copy-start | bytes 3145732
  232.3 96.4 %copy-start.1 = (bf16[5632,128]{1,0:T(8,128)(2,1)S(1)}, bf16[5632,128]{1,0:T(8,128)(2,1)}, u32[]{:S(2)}) copy-start(bf16[5632,128]{1,0:T(8,128)(2,1)} %param.30) | copy-start | bytes 4325380
Sparse Core Ops, SparseCore 0:
  9.8 115.3 all-gather.1
  232.4 94.2 reduce-scatter.1

commit v4 on v3

--- a/solution.py
+++ b/solution.py
@@ -158,10 +158,11 @@
         .at[jnp.take(dest_local, pick)]
         .set(jnp.arange(image_count, dtype=jnp.int32))
     )
-    row_table = jnp.concatenate([mine_rows, jnp.zeros_like(mine_rows[:1])], axis=0)
-    features = jnp.where(
-        (lookup < image_count)[:, None], jnp.take(row_table, lookup, axis=0), gathered_text
-    )
+    choose = (lookup[:, None] == jnp.arange(image_count, dtype=jnp.int32)[None, :]).astype(
+        jnp.bfloat16
+    )
+    placed = jnp.dot(choose, mine_rows, preferred_element_type=jnp.float32).astype(jnp.bfloat16)
+    features = jnp.where((lookup < image_count)[:, None], placed, gathered_text)
     token_values = features.astype(jnp.float32)
     normed_tokens = (
         token_values
@@ -169,15 +170,12 @@
         * text_gain.astype(jnp.float32)
     ).astype(jnp.bfloat16)
     positions, allowed = causal_setup(segment_ids[0])
-    queries = rotate(
-        jnp.dot(normed_tokens, query_weight, preferred_element_type=jnp.float32), positions
-    ).astype(jnp.bfloat16)
-    keys_rot = rotate(
-        jnp.dot(normed_tokens, key_weight, preferred_element_type=jnp.float32), positions
-    ).astype(jnp.bfloat16)
-    values_here = jnp.dot(normed_tokens, value_weight, preferred_element_type=jnp.float32).astype(
-        jnp.bfloat16
-    )
+    head_cols = query_weight.shape[1]
+    qkv_weight = jnp.concatenate([query_weight, key_weight, value_weight], axis=1)
+    qkv = jnp.dot(normed_tokens, qkv_weight, preferred_element_type=jnp.float32)
+    queries = rotate(qkv[:, :head_cols], positions).astype(jnp.bfloat16)
+    keys_rot = rotate(qkv[:, head_cols : 2 * head_cols], positions).astype(jnp.bfloat16)
+    values_here = qkv[:, 2 * head_cols :].astype(jnp.bfloat16)
     block_rows = min(512, tok_grp)
     block_count = tok_grp // block_rows
 
@@ -198,7 +196,9 @@
         scatter_dimension=0,
         tiled=True,
     ).astype(jnp.float32)
-    residual = lax.dynamic_slice_in_dim(token_values, blk_index * out_share, out_share, 0)
+    residual = lax.dynamic_slice_in_dim(features, blk_index * out_share, out_share, 0).astype(
+        jnp.float32
+    )
     return (residual + summed_heads).astype(jnp.bfloat16)
 
 

time: 336 us -> 299 us (0.89)
  other arithmetic: 51.5 us -> 26.5 us
  local copies, waits for them, and re-layouts: 33.3 us -> 25.3 us
  matrix products: 31.9 us -> 28.3 us
    convert_element_type x3 -> x1, other arithmetic: 23.3 us -> 0.02 us  [body(): rotate(qkv[:, head_cols:2 * head_cols], positions).astype(jnp.bfloat16)]
    gather x1 -> x0, local copies, waits for them, and re-layouts: 7.82 us -> none  [body(): jnp.take(row_table, lookup, axis=0)]
    dot_general x3 -> x2, matrix products: 15.3 us -> 10.5 us  [the longest x1 6.63 us: body(): jnp.dot(choose, mine_rows, preferred_element_type=jnp.float32)]
  transfers between devices with their start and end apart: 6 -> 6, of which waited for: 5 -> 5; matrix products, arithmetic and copies ran while one was open for 19% -> 18% of each run, Pallas kernels for 0% -> 0%
where the time goes in v4:
time: 299 us; the launch traced here: 298 us
  waiting for transfers between devices  176 us (59%)
  matrix products  28.3 us (9%)
  starting transfers between devices  28.2 us (9%)
  other arithmetic  26.5 us (9%)
  local copies, waits for them, and re-layouts  25.3 us (8%)
  between operations  14 us (5%)
    reduce_scatter x1, waiting for transfers between devices, body(): lax.psum_scatter(jnp.dot(attn_out, out_weight, preferred_element_type=jnp...  94.4 us
    all_to_all x1, waiting for transfers between devices, body(): lax.all_to_all(jnp.broadcast_to(merged_here[None], (blk_count,) + merged_...  34.6 us
    all_to_all x1, waiting for transfers between devices, body(): lax.all_to_all(partial.reshape(blk_count, row_share, vis_width), 'blk', 0...  21.7 us
    all_to_all x1, waiting for transfers between devices, body(): lax.all_to_all(jnp.broadcast_to(mine_cols[None], (blk_count,) + mine_cols...  15 us
    all_to_all x1, waiting for transfers between devices, body(): lax.all_to_all(outgoing, 'req', split_axis=0, concat_axis=0, tiled=True)  9.46 us
    all_to_all x1, starting transfers between devices, body(): lax.all_to_all(partial.reshape(blk_count, row_share, vis_width), 'blk', 0...  7.58 us
    all_to_all x1, starting transfers between devices, body(): lax.all_to_all(outgoing, 'req', split_axis=0, concat_axis=0, tiled=True)  7.28 us
    all_to_all x1, starting transfers between devices, body(): lax.all_to_all(jnp.broadcast_to(merged_here[None], (blk_count,) + merged_...  7.12 us
  transfers between devices with their start and end apart: 6, of which 5 were waited for; matrix products, arithmetic and copies ran while one was open for 18% of the time, Pallas kernels for 0%

profile of v4, /device:TPU:8, one launch (start us, length us, event | category | flops | bytes accessed | tf_op | source)
XLA Modules:
  0.0 298.3 jit_solution(8643636575924972471)
XLA Ops:
  9.6 2.0 convert_reduce_fusion.2
  12.3 6.3 %convolution_convert_fusion.2 = bf16[768,1408]{1,0:T(8,128)(2,1)} fusion(bf16[192,1408]{1,0:T(8,128)(2,1)S(1)} %copy-done.13, bf16[1408,192]{0,1:T(8,128)(2,1)S(1)} %copy-done.14, bf16[768,1408]{1,0:T(8,128)(2,1)} %param.22, f32[1408]{0:T(1024)S(1)} %convert_element_type.111, f32[1408]{0:T(1024)S(1)} %convert_element_type.110, ...), kind=kOutput, calls=%fused_computation.36 | convolution fusion | flops 847773696 | bytes 5424896 | tf_op jit(solution)/shard_map/dot_general | solution.py:97
  18.6 7.6 %all-to-all-start = ((bf16[32,24,1408]{2,1,0:T(8,128)(2,1)}), bf16[32,24,1408]{2,1,0:T(8,128)(2,1)}, u32[]{:S(2)}, u32[]{:S(2)}) async-start(bf16[32,24,1408]{2,1,0:T(8,128)(2,1)} %bitcast.77), calls=%async_computation | async-start | bytes 4325376 | tf_op jit(solution)/shard_map/all_to_all | solution.py:100
  26.3 3.9 %convert_element_type.109 = f32[768,1408]{1,0:T(8,128)} convert(bf16[768,1408]{1,0:T(8,128)(2,1)} %param.22) | non-fusion elementwise | flops 1081344 | bytes 6488064 | tf_op jit(solution)/shard_map/convert_element_type | solution.py:91
  30.3 4.5 %reduce-window.19 = s32[8,8,2,128]{3,1,2,0:T(8,128)S(1)} reduce-window(s32[8,8,2,128]{3,1,2,0:T(8,128)S(1)} %convert_bitcast_fusion, s32[]{:T(128)} %constant.49.clone.1), window={size=1x1x1x128 pad=0_0x0_0x0_0x127_0}, to_apply=%region_4.6 | reduce-window | flops 2080768 | bytes 131076 | tf_op jit(solution)/shard_map/reduce-window.2
  35.2 21.7 %all-to-all-done = bf16[32,24,1408]{2,1,0:T(8,128)(2,1)} async-done(((bf16[32,24,1408]{2,1,0:T(8,128)(2,1)}), bf16[32,24,1408]{2,1,0:T(8,128)(2,1)}, u32[]{:S(2)}, u32[]{:S(2)}) %all-to-all-start) | async-done | bytes 2162720 | tf_op jit(solution)/shard_map/all_to_all | solution.py:100
  56.9 1.9 convert_reduce_fusion
  60.2 1.9 broadcast_in_dim.120
  62.1 7.1 %all-to-all-start.1 = ((bf16[32,6,5632]{2,1,0:T(8,128)(2,1)}), bf16[32,6,5632]{2,1,0:T(8,128)(2,1)}, u32[]{:S(2)}, u32[]{:S(2)}) async-start(bf16[32,6,5632]{2,1,0:T(8,128)(2,1)} %broadcast_in_dim.120), calls=%async_computation.1 | async-start | bytes 5767168 | tf_op jit(solution)/shard_map/all_to_all | solution.py:108
  71.5 6.2 %scatter_custom_fusion = s32[192]{0:T(256)S(1)} fusion(s32[1536]{0:T(1024)S(1)} %compare_select_fusion, s32[1536]{0:T(1024)S(1)} %iota.48, s32[]{:T(128)} %constant.49.clone.1), kind=kCustom, calls=%fused_computation.181 | custom fusion | bytes 772 | tf_op jit(solution)/shard_map/scatter | solution.py:149
  79.1 34.6 %all-to-all-done.1 = bf16[32,6,5632]{2,1,0:T(8,128)(2,1)} async-done(((bf16[32,6,5632]{2,1,0:T(8,128)(2,1)}), bf16[32,6,5632]{2,1,0:T(8,128)(2,1)}, u32[]{:S(2)}, u32[]{:S(2)}) %all-to-all-start.1) | async-done | bytes 2162720 | tf_op jit(solution)/shard_map/all_to_all | solution.py:108
  113.7 4.3 %reshape.315 = bf16[192,5632]{1,0:T(8,128)(2,1)} reshape(bf16[32,6,5632]{2,1,0:T(8,128)(2,1)} %all-to-all-done.1) | data formatting | bytes 4325376 | tf_op jit(solution)/shard_map/reshape | solution.py:116
  118.0 2.3 fusion.25
  120.4 1.9 gather_fusion
  123.2 7.3 %all-to-all-start.2 = ((bf16[8,66,128]{2,1,0:T(8,128)(2,1)}), bf16[8,66,128]{2,1,0:T(8,128)(2,1)S(1)}, u32[]{:S(2)}, u32[]{:S(2)}) async-start(bf16[8,66,128]{2,1,0:T(8,128)(2,1)} %broadcast_select_fusion), calls=%async_computation.2 | async-start | bytes 294912 | tf_op jit(solution)/shard_map/all_to_all | solution.py:141
  130.5 9.5 %all-to-all-done.2 = bf16[8,66,128]{2,1,0:T(8,128)(2,1)S(1)} async-done(((bf16[8,66,128]{2,1,0:T(8,128)(2,1)}), bf16[8,66,128]{2,1,0:T(8,128)(2,1)S(1)}, u32[]{:S(2)}, u32[]{:S(2)}) %all-to-all-start.2) | async-done | bytes 135200 | tf_op jit(solution)/shard_map/all_to_all | solution.py:141
  142.4 6.0 %all-to-all-start.3 = ((bf16[32,192,128]{2,1,0:T(8,128)(2,1)}), bf16[32,192,128]{2,1,0:T(8,128)(2,1)}, u32[]{:S(2)}, u32[]{:S(2)}) async-start(bf16[32,192,128]{2,1,0:T(8,128)(2,1)} %broadcast_in_dim.125), calls=%async_computation.3 | async-start | bytes 3145728 | tf_op jit(solution)/shard_map/all_to_all | solution.py:152
  154.4 15.0 %all-to-all-done.3 = bf16[32,192,128]{2,1,0:T(8,128)(2,1)} async-done(((bf16[32,192,128]{2,1,0:T(8,128)(2,1)}), bf16[32,192,128]{2,1,0:T(8,128)(2,1)}, u32[]{:S(2)}, u32[]{:S(2)}) %all-to-all-start.3) | async-done | bytes 1572896 | tf_op jit(solution)/shard_map/all_to_all | solution.py:152
  169.4 6.6 %fusion.7 = (f32[1024]{0:T(1024)S(1)}, bf16[1024,4096]{1,0:T(8,128)(2,1)S(1)}) fusion(bf16[1024,4096]{1,0:T(8,128)(2,1)} %all-gather.2.cloned.1.call-done, s32[1024]{0:T(1024)S(1)} %scatter_custom_fusion.1, pred[1024]{0:T(1024)(128)(4,1)S(1)} %broadcast_compare_fusion.1, bf16[32,192,128]{2,1,0:T(8,128)(2,1)} %all-to-all-done.3), kind=kOutput, calls=%fused_computation.20 | convolution fusion | flops 1631779840 | bytes 18359296 | tf_op jit(solution)/shard_map/dot_general | solution.py:164
  176.1 3.8 %fusion.10 = f32[1024,384]{0,1:T(8,128)S(1)} fusion(bf16[1024,4096]{1,0:T(8,128)(2,1)S(1)} %get-tuple-element.94, f32[4096]{0:T(1024)S(1)} %convert_element_type.125, f32[1024]{0:T(1024)S(1)} %add_rsqrt_fusion, bf16[4096,128]{1,0:T(8,128)(2,1)S(1)} %copy-done.10, bf16[4096,128]{1,0:T(8,128)(2,1)S(1)} %copy-done.11, bf16[4096,128]{1,0:T(8,128)(2,1)S(1)} %copy-done.12), kind=kOutput, calls=%fused_computation.23 | convolution fusion | flops 3247439872 | bytes 13127680 | tf_op jit(solution)/shard_map/dot_general | solution.py:175
  180.1 1.9 fusion.81
  183.5 4.8 %while.10 = (s32[]{:T(128)}, bf16[2,512,128]{2,1,0:T(8,128)(2,1)}, pred[2,512,1024]{2,1,0:T(32,128)(4,1)S(1)}, bf16[2,512,128]{2,1,0:T(8,128)(2,1)S(1)}, bf16[10...) while((s32[]{:T(128)}, bf16[2,512,128]{2,1,0:T(8,128)(2,1)}, ...), condition=%wide.region_18.20_spmd, body=%wide.region_15.19_spmd.sunk | while | flops 272694272 | bytes 9710729 | solution.py:185
  188.3 6.9 %convolution_convert_fusion.1 = bf16[1024,4096]{1,0:T(8,128)(2,1)} fusion(bf16[1024,128]{1,0:T(8,128)(2,1)} %bitcast.78, bf16[128,4096]{1,0:T(8,128)(2,1)} %param.39), kind=kOutput, calls=%fused_computation.27 | convolution fusion | flops 1077936128 | bytes 9699328 | tf_op jit(solution)/shard_map/dot_general | solution.py:194
  195.2 94.4 %reduce-scatter.2.cloned.1.call-done = bf16[32,4096]{1,0:T(8,128)(2,1)} async-done(((bf16[1024,4096]{1,0:T(8,128)(2,1)}), bf16[32,4096]{1,0:T(8,128)(2,1)}) %reduce-scatter.2.cloned.1.call-update) | async-done | bytes 262160 | tf_op jit(solution)/shard_map/reduce_scatter | solution.py:193
  (126 shorter events, 26.7 us)
Async XLA Ops:
  6.5 111.5 %copy-start = (bf16[5632,128]{1,0:T(8,128)(2,1)S(1)}, bf16[5632,128]{1,0:T(8,128)(2,1)}, u32[]{:S(2)}) copy-start(bf16[5632,128]{1,0:T(8,128)(2,1)} %param.30) | copy-start | bytes 4325380
  6.5 162.9 %all-gather.2.cloned.1.call-start = ((), (), s32[]{:S(2)}) async-start(), calls=%async_computation.5 | async-start | bytes 8650752 | tf_op jit(solution)/shard_map/all_gather | solution.py:90
  7.3 4.3 %copy-start.1 = (bf16[768,1408]{1,0:T(8,128)(2,1)S(1)}, bf16[768,1408]{1,0:T(8,128)(2,1)}, u32[]{:S(2)}) copy-start(bf16[768,1408]{1,0:T(8,128)(2,1)} %param.22) | copy-start | bytes 6488068
  7.3 5.0 %copy-start.13 = (bf16[192,1408]{1,0:T(8,128)(2,1)S(1)}, bf16[192,1408]{1,0:T(8,128)(2,1)}, u32[]{:S(2)}) copy-start(bf16[192,1408]{1,0:T(8,128)(2,1)} %param.27) | copy-start | bytes 1622020
  7.3 5.0 %copy-start.14 = (bf16[1408,192]{0,1:T(8,128)(2,1)S(1)}, bf16[1408,192]{0,1:T(8,128)(2,1)}, u32[]{:S(2)}) copy-start(bf16[1408,192]{0,1:T(8,128)(2,1)} %param.25) | copy-start | bytes 1622020
  18.6 38.3 %all-to-all-start = ((bf16[32,24,1408]{2,1,0:T(8,128)(2,1)}), bf16[32,24,1408]{2,1,0:T(8,128)(2,1)}, u32[]{:S(2)}, u32[]{:S(2)}) async-start(bf16[32,24,1408]{2,1,0:T(8,128)(2,1)} %bitcast.77), calls=%async_computation | async-start | bytes 4325376 | tf_op jit(solution)/shard_map/all_to_all | solution.py:100
  26.2 3.9 %copy-start.8 = (bf16[1408]{0:T(1024)(128)(2,1)S(1)}, bf16[1408]{0:T(1024)(128)(2,1)}, u32[]{:S(2)}) copy-start(bf16[1408]{0:T(1024)(128)(2,1)} %param.28) | copy-start | bytes 8452
  26.2 3.9 %copy-start.9 = (bf16[1408]{0:T(1024)(128)(2,1)S(1)}, bf16[1408]{0:T(1024)(128)(2,1)}, u32[]{:S(2)}) copy-start(bf16[1408]{0:T(1024)(128)(2,1)} %param.29) | copy-start | bytes 8452
  26.2 3.9 %copy-start.4 = (s32[1536]{0:T(1024)S(1)}, s32[1536]{0:T(1024)}, u32[]{:S(2)}) copy-start(s32[1536]{0:T(1024)} %param.32) | copy-start | bytes 18436
  62.1 7.2 %copy-start.15 = (bf16[128]{0:T(256)(128)(2,1)S(1)}, bf16[128]{0:T(256)(128)(2,1)}, u32[]{:S(2)}) copy-start(bf16[128]{0:T(256)(128)(2,1)} %param.31) | copy-start | bytes 772
  62.1 51.6 %all-to-all-start.1 = ((bf16[32,6,5632]{2,1,0:T(8,128)(2,1)}), bf16[32,6,5632]{2,1,0:T(8,128)(2,1)}, u32[]{:S(2)}, u32[]{:S(2)}) async-start(bf16[32,6,5632]{2,1,0:T(8,128)(2,1)} %broadcast_in_dim.120), calls=%async_computation.1 | async-start | bytes 5767168 | tf_op jit(solution)/shard_map/all_to_all | solution.py:108
  123.2 16.8 %all-to-all-start.2 = ((bf16[8,66,128]{2,1,0:T(8,128)(2,1)}), bf16[8,66,128]{2,1,0:T(8,128)(2,1)S(1)}, u32[]{:S(2)}, u32[]{:S(2)}) async-start(bf16[8,66,128]{2,1,0:T(8,128)(2,1)} %broadcast_select_fusion), calls=%async_computation.2 | async-start | bytes 294912 | tf_op jit(solution)/shard_map/all_to_all | solution.py:141
  140.0 10.1 %copy-start.6 = (bf16[4096]{0:T(1024)(128)(2,1)S(1)}, bf16[4096]{0:T(1024)(128)(2,1)}, u32[]{:S(2)}) copy-start(bf16[4096]{0:T(1024)(128)(2,1)} %param.35) | copy-start | bytes 24580
  140.0 10.1 %copy-start.5 = (s32[1,1024]{1,0:T(1,128)S(1)}, s32[1,1024]{1,0:T(1,128)}, u32[]{:S(2)}) copy-start(s32[1,1024]{1,0:T(1,128)} %param.34) | copy-start | bytes 12292
  142.4 27.0 %all-to-all-start.3 = ((bf16[32,192,128]{2,1,0:T(8,128)(2,1)}), bf16[32,192,128]{2,1,0:T(8,128)(2,1)}, u32[]{:S(2)}, u32[]{:S(2)}) async-start(bf16[32,192,128]{2,1,0:T(8,128)(2,1)} %broadcast_in_dim.125), calls=%async_computation.3 | async-start | bytes 3145728 | tf_op jit(solution)/shard_map/all_to_all | solution.py:152
  148.4 141.2 %reduce-scatter.2.cloned.1.call-start = ((), (), s32[]{:S(2)}) async-start(), calls=%async_computation.6 | async-start | bytes 8650752 | tf_op jit(solution)/shard_map/reduce_scatter | solution.py:193
  169.4 6.7 %copy-start.10 = (bf16[4096,128]{1,0:T(8,128)(2,1)S(1)}, bf16[4096,128]{1,0:T(8,128)(2,1)}, u32[]{:S(2)}) copy-start(bf16[4096,128]{1,0:T(8,128)(2,1)} %param.38) | copy-start | bytes 3145732
  169.4 6.7 %copy-start.11 = (bf16[4096,128]{1,0:T(8,128)(2,1)S(1)}, bf16[4096,128]{1,0:T(8,128)(2,1)}, u32[]{:S(2)}) copy-start(bf16[4096,128]{1,0:T(8,128)(2,1)} %param.37) | copy-start | bytes 3145732
  169.4 6.7 %copy-start.12 = (bf16[4096,128]{1,0:T(8,128)(2,1)S(1)}, bf16[4096,128]{1,0:T(8,128)(2,1)}, u32[]{:S(2)}) copy-start(bf16[4096,128]{1,0:T(8,128)(2,1)} %param.36) | copy-start | bytes 3145732
  176.0 3.9 %copy-start.7 = (bf16[1024,4096]{1,0:T(8,128)(2,1)}, bf16[1024,4096]{1,0:T(8,128)(2,1)S(1)}, u32[]{:S(2)}) copy-start(bf16[1024,4096]{1,0:T(8,128)(2,1)S(1)} %get-tuple-element.94) | copy-start | bytes 25165828
  183.5 1.1 copy-start.2
  185.2 0.7 copy-start.3
  185.9 1.1 copy-start.2
  187.6 0.7 copy-start.3
Sparse Core Ops, SparseCore 0:
  9.8 113.5 all-gather.1
  195.3 94.2 reduce-scatter.1

commit v5 on v4

--- a/solution.py
+++ b/solution.py
@@ -1,7 +1,7 @@
 import jax
 import jax.numpy as jnp
 from jax import lax
-from jax.sharding import PartitionSpec as P
+from jax.sharding import Mesh, PartitionSpec as P
 
 HEAD = 128
 
@@ -82,12 +82,15 @@
     value_weight,
     out_weight,
 ):
-    blk_count = lax.axis_size("blk")
+    pair_count = lax.axis_size("core")
+    blk_count = lax.axis_size("xy") * pair_count
     req_count = lax.axis_size("req")
-    blk_index = lax.axis_index("blk")
+    core_index = lax.axis_index("core")
+    blk_index = lax.axis_index("xy") * pair_count + core_index
     req_index = lax.axis_index("req")
     vis_width = patches.shape[1]
-    gathered_text = lax.all_gather(text_embed, "blk", axis=1, tiled=True)
+    gathered_text = lax.all_gather(text_embed, BLK, axis=1, tiled=True)
+    partner_weight = lax.ppermute(out_weight, "core", [(0, 1), (1, 0)])
     patch_rows = patches.astype(jnp.float32)
     normed = layer_norm(patch_rows, vis_ln_gain, vis_ln_bias).astype(jnp.bfloat16)
     pre_act = jnp.dot(normed, vis_up, preferred_element_type=jnp.float32) + vis_up_bias.astype(
@@ -98,7 +101,7 @@
     patch_count = patches.shape[0]
     row_share = patch_count // blk_count
     parts_here = lax.all_to_all(
-        partial.reshape(blk_count, row_share, vis_width), "blk", 0, 0, tiled=False
+        partial.reshape(blk_count, row_share, vis_width), BLK, 0, 0, tiled=False
     )
     summed = jnp.sum(parts_here.astype(jnp.float32), axis=0)
     own_rows = lax.dynamic_slice_in_dim(patch_rows, blk_index * row_share, row_share, 0)
@@ -107,7 +110,7 @@
     merged_here = normed.reshape(-1, 4 * vis_width)
     merged_all = lax.all_to_all(
         jnp.broadcast_to(merged_here[None], (blk_count,) + merged_here.shape),
-        "blk",
+        BLK,
         0,
         0,
         tiled=False,
@@ -150,7 +153,7 @@
     )
     mine_cols = jnp.take(incoming, jnp.take(arrival, pick), axis=0)
     mine_rows = lax.all_to_all(
-        jnp.broadcast_to(mine_cols[None], (blk_count,) + mine_cols.shape), "blk", 0, 0, tiled=False
+        jnp.broadcast_to(mine_cols[None], (blk_count,) + mine_cols.shape), BLK, 0, 0, tiled=False
     )
     mine_rows = mine_rows.transpose(1, 0, 2).reshape(image_count, -1)
     lookup = (
@@ -190,42 +193,57 @@
         ),
     ).reshape(tok_grp, -1)
     out_share = tok_grp // blk_count
-    summed_heads = lax.psum_scatter(
-        jnp.dot(attn_out, out_weight, preferred_element_type=jnp.float32).astype(jnp.bfloat16),
-        "blk",
-        scatter_dimension=0,
-        tiled=True,
-    ).astype(jnp.float32)
+    swap = [(0, 1), (1, 0)]
+    by_core = attn_out.reshape(blk_count // pair_count, pair_count, out_share, -1)
+    attn_mine = lax.dynamic_index_in_dim(by_core, core_index, 1, keepdims=False)
+    attn_other = lax.ppermute(
+        lax.dynamic_index_in_dim(by_core, 1 - core_index, 1, keepdims=False), "core", swap
+    )
+    pair_attn = jnp.concatenate([attn_mine, attn_other], axis=-1).reshape(
+        tok_grp // pair_count, -1
+    )
+    pair_weight = jnp.concatenate([out_weight, partner_weight], axis=0)
+    pair_sum = jnp.dot(pair_attn, pair_weight, preferred_element_type=jnp.float32).astype(
+        jnp.bfloat16
+    )
+    summed_heads = lax.psum_scatter(pair_sum, "xy", scatter_dimension=0, tiled=True).astype(
+        jnp.float32
+    )
     residual = lax.dynamic_slice_in_dim(features, blk_index * out_share, out_share, 0).astype(
         jnp.float32
     )
     return (residual + summed_heads).astype(jnp.bfloat16)
 
 
+BLK = ("xy", "core")
+
+
 def solution(mesh):
+    blk_size, req_size = mesh.devices.shape
+    pair_mesh = Mesh(mesh.devices.reshape(blk_size // 2, 2, req_size), ("xy", "core", "req"))
     return jax.shard_map(
         body,
-        mesh=mesh,
+        mesh=pair_mesh,
         in_specs=(
             P("req", None),
             P(),
             P(),
-            P(None, "blk"),
-            P("blk"),
-            P("blk", None),
-            P(),
-            P(),
-            P(None, "blk"),
-            P("blk"),
-            P(),
-            P("req", "blk"),
+            P(None, BLK),
+            P(BLK),
+            P(BLK, None),
+            P(),
+            P(),
+            P(None, BLK),
+            P(BLK),
+            P(),
+            P("req", BLK),
             P("req", None),
             P(),
-            P(None, "blk"),
-            P(None, "blk"),
-            P(None, "blk"),
-            P("blk", None),
+            P(None, BLK),
+            P(None, BLK),
+            P(None, BLK),
+            P(BLK, None),
         ),
-        out_specs=P(("req", "blk"), None),
+        out_specs=P(("req",) + BLK, None),
         check_vma=False,
     )

time: 299 us -> 283 us (0.946)
  waiting for transfers between devices: 176 us -> 160 us
    reduce_scatter x1, waiting for transfers between devices: 94.4 us -> 77.5 us  [body(): lax.psum_scatter(pair_sum, 'xy', scatter_dimension=0, tiled=True)]
  transfers between devices with their start and end apart: 6 -> 8, of which waited for: 5 -> 6; matrix products, arithmetic and copies ran while one was open for 18% -> 25% of each run, Pallas kernels for 0% -> 0%
where the time goes in v5:
time: 283 us; the launch traced here: 282 us
  waiting for transfers between devices  160 us (57%)
  starting transfers between devices  28.5 us (10%)
  other arithmetic  26.5 us (9%)
  local copies, waits for them, and re-layouts  26.3 us (9%)
  matrix products  26.2 us (9%)
  between operations  14 us (5%)
    reduce_scatter x1, waiting for transfers between devices, body(): lax.psum_scatter(pair_sum, 'xy', scatter_dimension=0, tiled=True)  77.5 us
    all_to_all x1, waiting for transfers between devices, body(): lax.all_to_all(jnp.broadcast_to(merged_here[None], (blk_count,) + merged_...  34.6 us
    all_to_all x1, waiting for transfers between devices, body(): lax.all_to_all(partial.reshape(blk_count, row_share, vis_width), BLK, 0,...  21.7 us
    all_to_all x1, waiting for transfers between devices, body(): lax.all_to_all(jnp.broadcast_to(mine_cols[None], (blk_count,) + mine_cols...  14.8 us
    all_to_all x1, waiting for transfers between devices, body(): lax.all_to_all(outgoing, 'req', split_axis=0, concat_axis=0, tiled=True)  9.46 us
    all_to_all x1, starting transfers between devices, body(): lax.all_to_all(partial.reshape(blk_count, row_share, vis_width), BLK, 0,...  7.58 us
    all_to_all x1, starting transfers between devices, body(): lax.all_to_all(outgoing, 'req', split_axis=0, concat_axis=0, tiled=True)  7.29 us
    all_to_all x1, starting transfers between devices, body(): lax.all_to_all(jnp.broadcast_to(merged_here[None], (blk_count,) + merged_...  7.13 us
  transfers between devices with their start and end apart: 8, of which 6 were waited for; matrix products, arithmetic and copies ran while one was open for 25% of the time, Pallas kernels for 0%

profile of v5, /device:TPU:8, one launch (start us, length us, event | category | flops | bytes accessed | tf_op | source)
XLA Modules:
  0.0 281.7 jit_solution(3486183406424662927)
XLA Ops:
  9.6 2.0 convert_reduce_fusion.2
  12.3 6.3 %convolution_convert_fusion.2 = bf16[768,1408]{1,0:T(8,128)(2,1)} fusion(bf16[192,1408]{1,0:T(8,128)(2,1)S(1)} %copy-done.13, bf16[1408,192]{0,1:T(8,128)(2,1)S(1)} %copy-done.14, bf16[768,1408]{1,0:T(8,128)(2,1)} %param.22, f32[1408]{0:T(1024)S(1)} %convert_element_type.111, f32[1408]{0:T(1024)S(1)} %convert_element_type.110, ...), kind=kOutput, calls=%fused_computation.36 | convolution fusion | flops 847773696 | bytes 5424896 | tf_op jit(solution)/shard_map/dot_general | solution.py:100
  18.6 7.6 %all-to-all-start = ((bf16[32,24,1408]{2,1,0:T(8,128)(2,1)}), bf16[32,24,1408]{2,1,0:T(8,128)(2,1)}, u32[]{:S(2)}, u32[]{:S(2)}) async-start(bf16[32,24,1408]{2,1,0:T(8,128)(2,1)} %bitcast.79), calls=%async_computation | async-start | bytes 4325376 | tf_op jit(solution)/shard_map/all_to_all | solution.py:103
  26.3 3.9 %convert_element_type.109 = f32[768,1408]{1,0:T(8,128)} convert(bf16[768,1408]{1,0:T(8,128)(2,1)} %param.22) | non-fusion elementwise | flops 1081344 | bytes 6488064 | tf_op jit(solution)/shard_map/convert_element_type | solution.py:94
  30.3 4.5 %reduce-window.19 = s32[8,8,2,128]{3,1,2,0:T(8,128)S(1)} reduce-window(s32[8,8,2,128]{3,1,2,0:T(8,128)S(1)} %convert_bitcast_fusion, s32[]{:T(128)} %constant.56.clone.1), window={size=1x1x1x128 pad=0_0x0_0x0_0x127_0}, to_apply=%region_4.6 | reduce-window | flops 2080768 | bytes 131076 | tf_op jit(solution)/shard_map/reduce-window.2
  35.2 21.7 %all-to-all-done = bf16[32,24,1408]{2,1,0:T(8,128)(2,1)} async-done(((bf16[32,24,1408]{2,1,0:T(8,128)(2,1)}), bf16[32,24,1408]{2,1,0:T(8,128)(2,1)}, u32[]{:S(2)}, u32[]{:S(2)}) %all-to-all-start) | async-done | bytes 2162720 | tf_op jit(solution)/shard_map/all_to_all | solution.py:103
  56.9 1.9 convert_reduce_fusion
  60.2 1.9 broadcast_in_dim.120
  62.1 7.1 %all-to-all-start.1 = ((bf16[32,6,5632]{2,1,0:T(8,128)(2,1)}), bf16[32,6,5632]{2,1,0:T(8,128)(2,1)}, u32[]{:S(2)}, u32[]{:S(2)}) async-start(bf16[32,6,5632]{2,1,0:T(8,128)(2,1)} %broadcast_in_dim.120), calls=%async_computation.1 | async-start | bytes 5767168 | tf_op jit(solution)/shard_map/all_to_all | solution.py:111
  71.5 6.2 %scatter_custom_fusion = s32[192]{0:T(256)S(1)} fusion(s32[1536]{0:T(1024)S(1)} %compare_select_fusion, s32[1536]{0:T(1024)S(1)} %iota.48, s32[]{:T(128)} %constant.56.clone.1), kind=kCustom, calls=%fused_computation.191 | custom fusion | bytes 772 | tf_op jit(solution)/shard_map/scatter | solution.py:152
  79.1 34.6 %all-to-all-done.1 = bf16[32,6,5632]{2,1,0:T(8,128)(2,1)} async-done(((bf16[32,6,5632]{2,1,0:T(8,128)(2,1)}), bf16[32,6,5632]{2,1,0:T(8,128)(2,1)}, u32[]{:S(2)}, u32[]{:S(2)}) %all-to-all-start.1) | async-done | bytes 2162720 | tf_op jit(solution)/shard_map/all_to_all | solution.py:111
  113.7 4.3 %reshape.316 = bf16[192,5632]{1,0:T(8,128)(2,1)} reshape(bf16[32,6,5632]{2,1,0:T(8,128)(2,1)} %all-to-all-done.1) | data formatting | bytes 4325376 | tf_op jit(solution)/shard_map/reshape | solution.py:119
  118.0 2.3 fusion.28
  120.4 1.9 gather_fusion
  123.2 7.3 %all-to-all-start.2 = ((bf16[8,66,128]{2,1,0:T(8,128)(2,1)}), bf16[8,66,128]{2,1,0:T(8,128)(2,1)S(1)}, u32[]{:S(2)}, u32[]{:S(2)}) async-start(bf16[8,66,128]{2,1,0:T(8,128)(2,1)} %broadcast_select_fusion), calls=%async_computation.2 | async-start | bytes 294912 | tf_op jit(solution)/shard_map/all_to_all | solution.py:144
  130.5 9.5 %all-to-all-done.2 = bf16[8,66,128]{2,1,0:T(8,128)(2,1)S(1)} async-done(((bf16[8,66,128]{2,1,0:T(8,128)(2,1)}), bf16[8,66,128]{2,1,0:T(8,128)(2,1)S(1)}, u32[]{:S(2)}, u32[]{:S(2)}) %all-to-all-start.2) | async-done | bytes 135200 | tf_op jit(solution)/shard_map/all_to_all | solution.py:144
  142.4 6.0 %all-to-all-start.3 = ((bf16[32,192,128]{2,1,0:T(8,128)(2,1)}), bf16[32,192,128]{2,1,0:T(8,128)(2,1)}, u32[]{:S(2)}, u32[]{:S(2)}) async-start(bf16[32,192,128]{2,1,0:T(8,128)(2,1)} %broadcast_in_dim.125), calls=%async_computation.3 | async-start | bytes 3145728 | tf_op jit(solution)/shard_map/all_to_all | solution.py:155
  154.6 14.8 %all-to-all-done.3 = bf16[32,192,128]{2,1,0:T(8,128)(2,1)} async-done(((bf16[32,192,128]{2,1,0:T(8,128)(2,1)}), bf16[32,192,128]{2,1,0:T(8,128)(2,1)}, u32[]{:S(2)}, u32[]{:S(2)}) %all-to-all-start.3) | async-done | bytes 1572896 | tf_op jit(solution)/shard_map/all_to_all | solution.py:155
  169.4 6.6 %fusion.7 = (f32[1024]{0:T(1024)S(1)}, bf16[1024,4096]{1,0:T(8,128)(2,1)S(1)}) fusion(bf16[1024,4096]{1,0:T(8,128)(2,1)} %all-gather.2.cloned.1.call-done, s32[1024]{0:T(1024)S(1)} %scatter_custom_fusion.1, pred[1024]{0:T(1024)(128)(4,1)S(1)} %broadcast_compare_fusion.1, bf16[32,192,128]{2,1,0:T(8,128)(2,1)} %all-to-all-done.3), kind=kOutput, calls=%fused_computation.20 | convolution fusion | flops 1631779840 | bytes 18359296 | tf_op jit(solution)/shard_map/dot_general | solution.py:167
  176.1 3.8 %fusion.10 = f32[1024,384]{0,1:T(8,128)S(1)} fusion(bf16[1024,4096]{1,0:T(8,128)(2,1)S(1)} %get-tuple-element.96, f32[4096]{0:T(1024)S(1)} %convert_element_type.125, f32[1024]{0:T(1024)S(1)} %add_rsqrt_fusion, bf16[4096,128]{1,0:T(8,128)(2,1)S(1)} %copy-done.10, bf16[4096,128]{1,0:T(8,128)(2,1)S(1)} %copy-done.11, bf16[4096,128]{1,0:T(8,128)(2,1)S(1)} %copy-done.12), kind=kOutput, calls=%fused_computation.23 | convolution fusion | flops 3247439872 | bytes 13127680 | tf_op jit(solution)/shard_map/dot_general | solution.py:178
  180.1 1.9 fusion.84
  183.5 4.8 %while.10 = (s32[]{:T(128)}, bf16[2,512,128]{2,1,0:T(8,128)(2,1)}, pred[2,512,1024]{2,1,0:T(32,128)(4,1)S(1)}, bf16[2,512,128]{2,1,0:T(8,128)(2,1)S(1)}, bf16[10...) while((s32[]{:T(128)}, bf16[2,512,128]{2,1,0:T(8,128)(2,1)}, ...), condition=%wide.region_18.20_spmd, body=%wide.region_15.19_spmd.sunk | while | flops 272694272 | bytes 9710729 | solution.py:188
  190.7 4.8 %convolution_convert_fusion.1 = bf16[512,4096]{1,0:T(8,128)(2,1)} fusion(bf16[128,4096]{1,0:T(8,128)(2,1)} %collective-permute-done.1, bf16[128,4096]{1,0:T(8,128)(2,1)} %param.39, bf16[512,128]{1,0:T(8,128)(2,1)S(1)} %bitcast.82, bf16[512,128]{1,0:T(8,128)(2,1)S(1)} %bitcast.80), kind=kOutput, calls=%fused_computation.27 | convolution fusion | flops 1080557568 | bytes 6553600 | tf_op jit(solution)/shard_map/dot_general | solution.py:206
  195.5 77.5 %reduce-scatter.2.cloned.1.call-done = bf16[32,4096]{1,0:T(8,128)(2,1)} async-done(((bf16[512,4096]{1,0:T(8,128)(2,1)}), bf16[32,4096]{1,0:T(8,128)(2,1)}) %reduce-scatter.2.cloned.1.call-update) | async-done | bytes 262160 | tf_op jit(solution)/shard_map/reduce_scatter | solution.py:209
  (131 shorter events, 29.3 us)
Async XLA Ops:
  6.5 111.5 %copy-start = (bf16[5632,128]{1,0:T(8,128)(2,1)S(1)}, bf16[5632,128]{1,0:T(8,128)(2,1)}, u32[]{:S(2)}) copy-start(bf16[5632,128]{1,0:T(8,128)(2,1)} %param.30) | copy-start | bytes 4325380
  6.5 162.8 %all-gather.2.cloned.1.call-start = ((), (), s32[]{:S(2)}) async-start(), calls=%async_computation.5 | async-start | bytes 8650752 | tf_op jit(solution)/shard_map/all_gather | solution.py:92
  7.3 4.3 %copy-start.1 = (bf16[768,1408]{1,0:T(8,128)(2,1)S(1)}, bf16[768,1408]{1,0:T(8,128)(2,1)}, u32[]{:S(2)}) copy-start(bf16[768,1408]{1,0:T(8,128)(2,1)} %param.22) | copy-start | bytes 6488068
  7.3 5.0 %copy-start.13 = (bf16[192,1408]{1,0:T(8,128)(2,1)S(1)}, bf16[192,1408]{1,0:T(8,128)(2,1)}, u32[]{:S(2)}) copy-start(bf16[192,1408]{1,0:T(8,128)(2,1)} %param.27) | copy-start | bytes 1622020
  7.3 5.0 %copy-start.14 = (bf16[1408,192]{0,1:T(8,128)(2,1)S(1)}, bf16[1408,192]{0,1:T(8,128)(2,1)}, u32[]{:S(2)}) copy-start(bf16[1408,192]{0,1:T(8,128)(2,1)} %param.25) | copy-start | bytes 1622020
  18.6 38.3 %all-to-all-start = ((bf16[32,24,1408]{2,1,0:T(8,128)(2,1)}), bf16[32,24,1408]{2,1,0:T(8,128)(2,1)}, u32[]{:S(2)}, u32[]{:S(2)}) async-start(bf16[32,24,1408]{2,1,0:T(8,128)(2,1)} %bitcast.79), calls=%async_computation | async-start | bytes 4325376 | tf_op jit(solution)/shard_map/all_to_all | solution.py:103
  26.2 3.9 %copy-start.8 = (bf16[1408]{0:T(1024)(128)(2,1)S(1)}, bf16[1408]{0:T(1024)(128)(2,1)}, u32[]{:S(2)}) copy-start(bf16[1408]{0:T(1024)(128)(2,1)} %param.28) | copy-start | bytes 8452
  26.2 3.9 %copy-start.9 = (bf16[1408]{0:T(1024)(128)(2,1)S(1)}, bf16[1408]{0:T(1024)(128)(2,1)}, u32[]{:S(2)}) copy-start(bf16[1408]{0:T(1024)(128)(2,1)} %param.29) | copy-start | bytes 8452
  26.2 3.9 %copy-start.4 = (s32[1536]{0:T(1024)S(1)}, s32[1536]{0:T(1024)}, u32[]{:S(2)}) copy-start(s32[1536]{0:T(1024)} %param.32) | copy-start | bytes 18436
  62.1 7.2 %copy-start.15 = (bf16[128]{0:T(256)(128)(2,1)S(1)}, bf16[128]{0:T(256)(128)(2,1)}, u32[]{:S(2)}) copy-start(bf16[128]{0:T(256)(128)(2,1)} %param.31) | copy-start | bytes 772
  62.1 51.6 %all-to-all-start.1 = ((bf16[32,6,5632]{2,1,0:T(8,128)(2,1)}), bf16[32,6,5632]{2,1,0:T(8,128)(2,1)}, u32[]{:S(2)}, u32[]{:S(2)}) async-start(bf16[32,6,5632]{2,1,0:T(8,128)(2,1)} %broadcast_in_dim.120), calls=%async_computation.1 | async-start | bytes 5767168 | tf_op jit(solution)/shard_map/all_to_all | solution.py:111
  123.2 16.8 %all-to-all-start.2 = ((bf16[8,66,128]{2,1,0:T(8,128)(2,1)}), bf16[8,66,128]{2,1,0:T(8,128)(2,1)S(1)}, u32[]{:S(2)}, u32[]{:S(2)}) async-start(bf16[8,66,128]{2,1,0:T(8,128)(2,1)} %broadcast_select_fusion), calls=%async_computation.2 | async-start | bytes 294912 | tf_op jit(solution)/shard_map/all_to_all | solution.py:144
  140.0 10.3 %copy-start.6 = (bf16[4096]{0:T(1024)(128)(2,1)S(1)}, bf16[4096]{0:T(1024)(128)(2,1)}, u32[]{:S(2)}) copy-start(bf16[4096]{0:T(1024)(128)(2,1)} %param.35) | copy-start | bytes 24580
  140.0 10.3 %copy-start.5 = (s32[1,1024]{1,0:T(1,128)S(1)}, s32[1,1024]{1,0:T(1,128)}, u32[]{:S(2)}) copy-start(s32[1,1024]{1,0:T(1,128)} %param.34) | copy-start | bytes 12292
  142.4 27.0 %all-to-all-start.3 = ((bf16[32,192,128]{2,1,0:T(8,128)(2,1)}), bf16[32,192,128]{2,1,0:T(8,128)(2,1)}, u32[]{:S(2)}, u32[]{:S(2)}) async-start(bf16[32,192,128]{2,1,0:T(8,128)(2,1)} %broadcast_in_dim.125), calls=%async_computation.3 | async-start | bytes 3145728 | tf_op jit(solution)/shard_map/all_to_all | solution.py:155
  148.4 124.6 %reduce-scatter.2.cloned.1.call-start = ((), (), s32[]{:S(2)}) async-start(), calls=%async_computation.6 | async-start | bytes 4456448 | tf_op jit(solution)/shard_map/reduce_scatter | solution.py:209
  148.4 40.9 %collective-permute-start.1 = (bf16[128,4096]{1,0:T(8,128)(2,1)}, bf16[128,4096]{1,0:T(8,128)(2,1)}, u32[]{:S(2)}, u32[]{:S(2)}) collective-permute-start(bf16[128,4096]{1,0:T(8,128)(2,1)} %param.39), channel_id=1, source_target_pairs={{0,8},{8,0},{1,9},{9,1},{2,10},{10,2},{3,11},{11,3},{4,12},{12,4},... | collective-permute-start | bytes 3145736 | tf_op jit(solution)/shard_map/ppermute | solution.py:93
  169.4 6.7 %copy-start.10 = (bf16[4096,128]{1,0:T(8,128)(2,1)S(1)}, bf16[4096,128]{1,0:T(8,128)(2,1)}, u32[]{:S(2)}) copy-start(bf16[4096,128]{1,0:T(8,128)(2,1)} %param.38) | copy-start | bytes 3145732
  169.4 6.7 %copy-start.11 = (bf16[4096,128]{1,0:T(8,128)(2,1)S(1)}, bf16[4096,128]{1,0:T(8,128)(2,1)}, u32[]{:S(2)}) copy-start(bf16[4096,128]{1,0:T(8,128)(2,1)} %param.37) | copy-start | bytes 3145732
  169.4 6.7 %copy-start.12 = (bf16[4096,128]{1,0:T(8,128)(2,1)S(1)}, bf16[4096,128]{1,0:T(8,128)(2,1)}, u32[]{:S(2)}) copy-start(bf16[4096,128]{1,0:T(8,128)(2,1)} %param.36) | copy-start | bytes 3145732
  176.0 3.9 %copy-start.7 = (bf16[1024,4096]{1,0:T(8,128)(2,1)}, bf16[1024,4096]{1,0:T(8,128)(2,1)S(1)}, u32[]{:S(2)}) copy-start(bf16[1024,4096]{1,0:T(8,128)(2,1)S(1)} %get-tuple-element.96) | copy-start | bytes 25165828
  183.5 1.1 copy-start.2
  185.9 1.1 copy-start.2
  189.3 1.4 collective-permute-start
  (2 other events, 1.4 us)
Sparse Core Ops, SparseCore 0:
  9.8 113.5 all-gather.1
  195.6 77.3 reduce-scatter.1

commit v6 on v5

--- a/solution.py
+++ b/solution.py
@@ -206,9 +206,11 @@
     pair_sum = jnp.dot(pair_attn, pair_weight, preferred_element_type=jnp.float32).astype(
         jnp.bfloat16
     )
-    summed_heads = lax.psum_scatter(pair_sum, "xy", scatter_dimension=0, tiled=True).astype(
-        jnp.float32
-    )
+    chip_count = blk_count // pair_count
+    sums_here = lax.all_to_all(
+        pair_sum.reshape(chip_count, out_share, -1), "xy", 0, 0, tiled=False
+    )
+    summed_heads = jnp.sum(sums_here.astype(jnp.float32), axis=0)
     residual = lax.dynamic_slice_in_dim(features, blk_index * out_share, out_share, 0).astype(
         jnp.float32
     )

time: 283 us -> 278 us (0.982)
  the two profiles are of different devices: /device:TPU:8 before, /device:TPU:20 now
where the time goes in v6:
time: 278 us; the launch traced here: 277 us
  waiting for transfers between devices  136 us (49%)
  starting transfers between devices  43.9 us (16%)
  other arithmetic  30.8 us (11%)
  local copies, waits for them, and re-layouts  26.4 us (9%)
  matrix products  26.2 us (9%)
  between operations  14 us (5%)
    all_to_all x1, waiting for transfers between devices, body(): lax.all_to_all(pair_sum.reshape(chip_count, out_share, -1), 'xy', 0, 0, t...  61.4 us
    all_to_all x1, waiting for transfers between devices, body(): lax.all_to_all(jnp.broadcast_to(merged_here[None], (blk_count,) + merged_...  32.1 us
    all_to_all x1, waiting for transfers between devices, body(): lax.all_to_all(partial.reshape(blk_count, row_share, vis_width), BLK, 0,...  18.7 us
    all_to_all x1, waiting for transfers between devices, body(): lax.all_to_all(jnp.broadcast_to(mine_cols[None], (blk_count,) + mine_cols...  12.3 us
    all_to_all x1, starting transfers between devices, body(): lax.all_to_all(jnp.broadcast_to(mine_cols[None], (blk_count,) + mine_cols...  9.9 us
    all_to_all x1, waiting for transfers between devices, body(): lax.all_to_all(outgoing, 'req', split_axis=0, concat_axis=0, tiled=True)  9.72 us
    all_to_all x1, starting transfers between devices, body(): lax.all_to_all(jnp.broadcast_to(merged_here[None], (blk_count,) + merged_...  9.6 us
    all_to_all x1, starting transfers between devices, body(): lax.all_to_all(pair_sum.reshape(chip_count, out_share, -1), 'xy', 0, 0, t...  9.05 us
  transfers between devices with their start and end apart: 8, of which 6 were waited for; matrix products, arithmetic and copies ran while one was open for 26% of the time, Pallas kernels for 0%

profile of v6, /device:TPU:20, one launch (start us, length us, event | category | flops | bytes accessed | tf_op | source)
XLA Modules:
  0.0 277.5 jit_solution(18419885766093517492)
XLA Ops:
  9.3 2.0 convert_reduce_fusion.3
  11.3 2.3 multiply_reduce_fusion
  13.6 6.3 %convolution_convert_fusion.2 = bf16[768,1408]{1,0:T(8,128)(2,1)} fusion(bf16[192,1408]{1,0:T(8,128)(2,1)S(1)} %copy-done.12, bf16[1408,192]{0,1:T(8,128)(2,1)S(1)} %copy-done.13, bf16[768,1408]{1,0:T(8,128)(2,1)} %param.22, f32[1408]{0:T(1024)S(1)} %convert_element_type.111, f32[1408]{0:T(1024)S(1)} %convert_element_type.110, ...), kind=kOutput, calls=%fused_computation.37 | convolution fusion | flops 847773696 | bytes 5424896 | tf_op jit(solution)/shard_map/dot_general | solution.py:100
  20.0 7.4 %all-to-all-start = ((bf16[32,24,1408]{2,1,0:T(8,128)(2,1)}), bf16[32,24,1408]{2,1,0:T(8,128)(2,1)}, u32[]{:S(2)}, u32[]{:S(2)}) async-start(bf16[32,24,1408]{2,1,0:T(8,128)(2,1)} %bitcast.81), calls=%async_computation | async-start | bytes 4325376 | tf_op jit(solution)/shard_map/all_to_all | solution.py:103
  27.4 3.9 %convert_element_type.109 = f32[768,1408]{1,0:T(8,128)} convert(bf16[768,1408]{1,0:T(8,128)(2,1)} %param.22) | non-fusion elementwise | flops 1081344 | bytes 6488064 | tf_op jit(solution)/shard_map/convert_element_type | solution.py:94
  31.5 4.5 %reduce-window.19 = s32[8,8,2,128]{3,1,2,0:T(8,128)S(1)} reduce-window(s32[8,8,2,128]{3,1,2,0:T(8,128)S(1)} %convert_bitcast_fusion, s32[]{:T(128)} %constant.56.clone.1), window={size=1x1x1x128 pad=0_0x0_0x0_0x127_0}, to_apply=%region_4.6 | reduce-window | flops 2080768 | bytes 131076 | tf_op jit(solution)/shard_map/reduce-window.2
  36.4 18.7 %all-to-all-done = bf16[32,24,1408]{2,1,0:T(8,128)(2,1)} async-done(((bf16[32,24,1408]{2,1,0:T(8,128)(2,1)}), bf16[32,24,1408]{2,1,0:T(8,128)(2,1)}, u32[]{:S(2)}, u32[]{:S(2)}) %all-to-all-start) | async-done | bytes 2162720 | tf_op jit(solution)/shard_map/all_to_all | solution.py:103
  55.0 1.9 convert_reduce_fusion.1
  60.2 9.6 %all-to-all-start.1 = ((bf16[32,6,5632]{2,1,0:T(8,128)(2,1)}), bf16[32,6,5632]{2,1,0:T(8,128)(2,1)}, u32[]{:S(2)}, u32[]{:S(2)}) async-start(bf16[32,6,5632]{2,1,0:T(8,128)(2,1)} %broadcast_in_dim.120), calls=%async_computation.1 | async-start | bytes 5767168 | tf_op jit(solution)/shard_map/all_to_all | solution.py:111
  72.1 6.2 %scatter_custom_fusion = s32[192]{0:T(256)S(1)} fusion(s32[1536]{0:T(1024)S(1)} %compare_select_fusion, s32[1536]{0:T(1024)S(1)} %iota.48, s32[]{:T(128)} %constant.56.clone.1), kind=kCustom, calls=%fused_computation.192 | custom fusion | bytes 772 | tf_op jit(solution)/shard_map/scatter | solution.py:152
  79.8 32.1 %all-to-all-done.1 = bf16[32,6,5632]{2,1,0:T(8,128)(2,1)} async-done(((bf16[32,6,5632]{2,1,0:T(8,128)(2,1)}), bf16[32,6,5632]{2,1,0:T(8,128)(2,1)}, u32[]{:S(2)}, u32[]{:S(2)}) %all-to-all-start.1) | async-done | bytes 2162720 | tf_op jit(solution)/shard_map/all_to_all | solution.py:111
  111.9 4.4 %reshape.319 = bf16[192,5632]{1,0:T(8,128)(2,1)} reshape(bf16[32,6,5632]{2,1,0:T(8,128)(2,1)} %all-to-all-done.1) | data formatting | bytes 4325376 | tf_op jit(solution)/shard_map/reshape | solution.py:119
  116.2 2.3 fusion.28
  121.4 7.1 %all-to-all-start.2 = ((bf16[8,66,128]{2,1,0:T(8,128)(2,1)}), bf16[8,66,128]{2,1,0:T(8,128)(2,1)S(1)}, u32[]{:S(2)}, u32[]{:S(2)}) async-start(bf16[8,66,128]{2,1,0:T(8,128)(2,1)} %broadcast_select_fusion), calls=%async_computation.2 | async-start | bytes 294912 | tf_op jit(solution)/shard_map/all_to_all | solution.py:144
  128.5 9.7 %all-to-all-done.2 = bf16[8,66,128]{2,1,0:T(8,128)(2,1)S(1)} async-done(((bf16[8,66,128]{2,1,0:T(8,128)(2,1)}), bf16[8,66,128]{2,1,0:T(8,128)(2,1)S(1)}, u32[]{:S(2)}, u32[]{:S(2)}) %all-to-all-start.2) | async-done | bytes 135200 | tf_op jit(solution)/shard_map/all_to_all | solution.py:144
  140.7 9.9 %all-to-all-start.3 = ((bf16[32,192,128]{2,1,0:T(8,128)(2,1)}), bf16[32,192,128]{2,1,0:T(8,128)(2,1)}, u32[]{:S(2)}, u32[]{:S(2)}) async-start(bf16[32,192,128]{2,1,0:T(8,128)(2,1)} %broadcast_in_dim.125), calls=%async_computation.3 | async-start | bytes 3145728 | tf_op jit(solution)/shard_map/all_to_all | solution.py:155
  156.8 12.3 %all-to-all-done.3 = bf16[32,192,128]{2,1,0:T(8,128)(2,1)} async-done(((bf16[32,192,128]{2,1,0:T(8,128)(2,1)}), bf16[32,192,128]{2,1,0:T(8,128)(2,1)}, u32[]{:S(2)}, u32[]{:S(2)}) %all-to-all-start.3) | async-done | bytes 1572896 | tf_op jit(solution)/shard_map/all_to_all | solution.py:155
  169.1 6.6 %fusion.7 = (f32[1024]{0:T(1024)S(1)}, bf16[1024,4096]{1,0:T(8,128)(2,1)S(1)}) fusion(bf16[1024,4096]{1,0:T(8,128)(2,1)} %all-gather.2.cloned.1.call-done, s32[1024]{0:T(1024)S(1)} %scatter_custom_fusion.1, pred[1024]{0:T(1024)(128)(4,1)S(1)} %broadcast_compare_fusion.1, bf16[32,192,128]{2,1,0:T(8,128)(2,1)} %all-to-all-done.3), kind=kOutput, calls=%fused_computation.20 | convolution fusion | flops 1631779840 | bytes 18359296 | tf_op jit(solution)/shard_map/dot_general | solution.py:167
  175.8 3.8 %fusion.10 = f32[1024,384]{0,1:T(8,128)S(1)} fusion(bf16[1024,4096]{1,0:T(8,128)(2,1)S(1)} %get-tuple-element.96, f32[4096]{0:T(1024)S(1)} %convert_element_type.125, f32[1024]{0:T(1024)S(1)} %add_rsqrt_fusion, bf16[4096,128]{1,0:T(8,128)(2,1)S(1)} %copy-done.9, bf16[4096,128]{1,0:T(8,128)(2,1)S(1)} %copy-done.10, bf16[4096,128]{1,0:T(8,128)(2,1)S(1)} %copy-done.11), kind=kOutput, calls=%fused_computation.23 | convolution fusion | flops 3247439872 | bytes 13127680 | tf_op jit(solution)/shard_map/dot_general | solution.py:178
  183.2 4.8 %while.10 = (s32[]{:T(128)}, bf16[2,512,128]{2,1,0:T(8,128)(2,1)}, pred[2,512,1024]{2,1,0:T(32,128)(4,1)S(1)}, bf16[2,512,128]{2,1,0:T(8,128)(2,1)S(1)}, bf16[10...) while((s32[]{:T(128)}, bf16[2,512,128]{2,1,0:T(8,128)(2,1)}, ...), condition=%wide.region_18.20_spmd, body=%wide.region_15.19_spmd.sunk | while | flops 272694272 | bytes 9710729 | solution.py:188
  190.7 4.8 %convolution_convert_fusion.1 = bf16[512,4096]{1,0:T(8,128)(2,1)} fusion(bf16[128,4096]{1,0:T(8,128)(2,1)} %collective-permute-done.1, bf16[128,4096]{1,0:T(8,128)(2,1)} %param.39, bf16[512,128]{1,0:T(8,128)(2,1)S(1)} %bitcast.84, bf16[512,128]{1,0:T(8,128)(2,1)S(1)} %bitcast.82), kind=kOutput, calls=%fused_computation.28 | convolution fusion | flops 1080557568 | bytes 6553600 | tf_op jit(solution)/shard_map/dot_general | solution.py:206
  195.5 9.1 %all-to-all-start.4 = ((bf16[16,32,4096]{2,1,0:T(8,128)(2,1)}), bf16[16,32,4096]{2,1,0:T(8,128)(2,1)}, u32[]{:S(2)}, u32[]{:S(2)}) async-start(bf16[16,32,4096]{2,1,0:T(8,128)(2,1)} %bitcast.79), calls=%async_computation.4 | async-start | bytes 8388608 | tf_op jit(solution)/shard_map/all_to_all | solution.py:210
  204.5 61.4 %all-to-all-done.4 = bf16[16,32,4096]{2,1,0:T(8,128)(2,1)} async-done(((bf16[16,32,4096]{2,1,0:T(8,128)(2,1)}), bf16[16,32,4096]{2,1,0:T(8,128)(2,1)}, u32[]{:S(2)}, u32[]{:S(2)}) %all-to-all-start.4) | async-done | bytes 4194336 | tf_op jit(solution)/shard_map/all_to_all | solution.py:210
  265.9 3.0 %convert_reduce_fusion = f32[32,4096]{1,0:T(8,128)S(1)} fusion(bf16[16,32,4096]{2,1,0:T(8,128)(2,1)} %all-to-all-done.4), kind=kLoop, calls=%fused_computation.24 | loop fusion | flops 4063232 | bytes 4718592 | tf_op jit(solution)/shard_map/reduce_sum | solution.py:213
  (129 shorter events, 34.1 us)
Async XLA Ops:
  6.5 109.7 %copy-start = (bf16[5632,128]{1,0:T(8,128)(2,1)S(1)}, bf16[5632,128]{1,0:T(8,128)(2,1)}, u32[]{:S(2)}) copy-start(bf16[5632,128]{1,0:T(8,128)(2,1)} %param.30) | copy-start | bytes 4325380
  6.5 7.1 %copy-start.13 = (bf16[1408,192]{0,1:T(8,128)(2,1)S(1)}, bf16[1408,192]{0,1:T(8,128)(2,1)}, u32[]{:S(2)}) copy-start(bf16[1408,192]{0,1:T(8,128)(2,1)} %param.25) | copy-start | bytes 1622020
  6.5 7.1 %copy-start.12 = (bf16[192,1408]{1,0:T(8,128)(2,1)S(1)}, bf16[192,1408]{1,0:T(8,128)(2,1)}, u32[]{:S(2)}) copy-start(bf16[192,1408]{1,0:T(8,128)(2,1)} %param.27) | copy-start | bytes 1622020
  6.5 162.6 %all-gather.2.cloned.1.call-start = ((), (), s32[]{:S(2)}) async-start(), calls=%async_computation.5 | async-start | bytes 8650752 | tf_op jit(solution)/shard_map/all_gather | solution.py:92
  20.0 35.1 %all-to-all-start = ((bf16[32,24,1408]{2,1,0:T(8,128)(2,1)}), bf16[32,24,1408]{2,1,0:T(8,128)(2,1)}, u32[]{:S(2)}, u32[]{:S(2)}) async-start(bf16[32,24,1408]{2,1,0:T(8,128)(2,1)} %bitcast.81), calls=%async_computation | async-start | bytes 4325376 | tf_op jit(solution)/shard_map/all_to_all | solution.py:103
  27.4 3.9 %copy-start.7 = (bf16[1408]{0:T(1024)(128)(2,1)S(1)}, bf16[1408]{0:T(1024)(128)(2,1)}, u32[]{:S(2)}) copy-start(bf16[1408]{0:T(1024)(128)(2,1)} %param.28) | copy-start | bytes 8452
  27.4 3.9 %copy-start.8 = (bf16[1408]{0:T(1024)(128)(2,1)S(1)}, bf16[1408]{0:T(1024)(128)(2,1)}, u32[]{:S(2)}) copy-start(bf16[1408]{0:T(1024)(128)(2,1)} %param.29) | copy-start | bytes 8452
  27.4 3.9 %copy-start.3 = (s32[1536]{0:T(1024)S(1)}, s32[1536]{0:T(1024)}, u32[]{:S(2)}) copy-start(s32[1536]{0:T(1024)} %param.32) | copy-start | bytes 18436
  58.4 11.6 %copy-start.14 = (bf16[128]{0:T(256)(128)(2,1)S(1)}, bf16[128]{0:T(256)(128)(2,1)}, u32[]{:S(2)}) copy-start(bf16[128]{0:T(256)(128)(2,1)} %param.31) | copy-start | bytes 772
  60.2 51.6 %all-to-all-start.1 = ((bf16[32,6,5632]{2,1,0:T(8,128)(2,1)}), bf16[32,6,5632]{2,1,0:T(8,128)(2,1)}, u32[]{:S(2)}, u32[]{:S(2)}) async-start(bf16[32,6,5632]{2,1,0:T(8,128)(2,1)} %broadcast_in_dim.120), calls=%async_computation.1 | async-start | bytes 5767168 | tf_op jit(solution)/shard_map/all_to_all | solution.py:111
  118.6 33.9 %copy-start.5 = (bf16[4096]{0:T(1024)(128)(2,1)S(1)}, bf16[4096]{0:T(1024)(128)(2,1)}, u32[]{:S(2)}) copy-start(bf16[4096]{0:T(1024)(128)(2,1)} %param.35) | copy-start | bytes 24580
  118.6 33.9 %copy-start.4 = (s32[1,1024]{1,0:T(1,128)S(1)}, s32[1,1024]{1,0:T(1,128)}, u32[]{:S(2)}) copy-start(s32[1,1024]{1,0:T(1,128)} %param.34) | copy-start | bytes 12292
  121.4 16.9 %all-to-all-start.2 = ((bf16[8,66,128]{2,1,0:T(8,128)(2,1)}), bf16[8,66,128]{2,1,0:T(8,128)(2,1)S(1)}, u32[]{:S(2)}, u32[]{:S(2)}) async-start(bf16[8,66,128]{2,1,0:T(8,128)(2,1)} %broadcast_select_fusion), calls=%async_computation.2 | async-start | bytes 294912 | tf_op jit(solution)/shard_map/all_to_all | solution.py:144
  140.7 28.4 %all-to-all-start.3 = ((bf16[32,192,128]{2,1,0:T(8,128)(2,1)}), bf16[32,192,128]{2,1,0:T(8,128)(2,1)}, u32[]{:S(2)}, u32[]{:S(2)}) async-start(bf16[32,192,128]{2,1,0:T(8,128)(2,1)} %broadcast_in_dim.125), calls=%async_computation.3 | async-start | bytes 3145728 | tf_op jit(solution)/shard_map/all_to_all | solution.py:155
  150.6 38.9 %collective-permute-start.1 = (bf16[128,4096]{1,0:T(8,128)(2,1)}, bf16[128,4096]{1,0:T(8,128)(2,1)}, u32[]{:S(2)}, u32[]{:S(2)}) collective-permute-start(bf16[128,4096]{1,0:T(8,128)(2,1)} %param.39), channel_id=1, source_target_pairs={{0,8},{8,0},{1,9},{9,1},{2,10},{10,2},{3,11},{11,3},{4,12},{12,4},... | collective-permute-start | bytes 3145736 | tf_op jit(solution)/shard_map/ppermute | solution.py:93
  169.1 6.7 %copy-start.9 = (bf16[4096,128]{1,0:T(8,128)(2,1)S(1)}, bf16[4096,128]{1,0:T(8,128)(2,1)}, u32[]{:S(2)}) copy-start(bf16[4096,128]{1,0:T(8,128)(2,1)} %param.38) | copy-start | bytes 3145732
  169.1 6.7 %copy-start.10 = (bf16[4096,128]{1,0:T(8,128)(2,1)S(1)}, bf16[4096,128]{1,0:T(8,128)(2,1)}, u32[]{:S(2)}) copy-start(bf16[4096,128]{1,0:T(8,128)(2,1)} %param.37) | copy-start | bytes 3145732
  169.1 6.7 %copy-start.11 = (bf16[4096,128]{1,0:T(8,128)(2,1)S(1)}, bf16[4096,128]{1,0:T(8,128)(2,1)}, u32[]{:S(2)}) copy-start(bf16[4096,128]{1,0:T(8,128)(2,1)} %param.36) | copy-start | bytes 3145732
  175.8 3.9 %copy-start.6 = (bf16[1024,4096]{1,0:T(8,128)(2,1)}, bf16[1024,4096]{1,0:T(8,128)(2,1)S(1)}, u32[]{:S(2)}) copy-start(bf16[1024,4096]{1,0:T(8,128)(2,1)S(1)} %get-tuple-element.96) | copy-start | bytes 25165828
  183.2 1.1 copy-start.1
  184.9 0.7 copy-start.2
  185.6 1.1 copy-start.1
  189.0 1.7 collective-permute-start
  195.5 70.5 %all-to-all-start.4 = ((bf16[16,32,4096]{2,1,0:T(8,128)(2,1)}), bf16[16,32,4096]{2,1,0:T(8,128)(2,1)}, u32[]{:S(2)}, u32[]{:S(2)}) async-start(bf16[16,32,4096]{2,1,0:T(8,128)(2,1)} %bitcast.79), calls=%async_computation.4 | async-start | bytes 8388608 | tf_op jit(solution)/shard_map/all_to_all | solution.py:210
  (1 other events, 0.7 us)
Sparse Core Ops, SparseCore 0:
  9.8 112.8 all-gather.1

commit v7 on v6

--- a/solution.py
+++ b/solution.py
@@ -82,15 +82,20 @@
     value_weight,
     out_weight,
 ):
-    pair_count = lax.axis_size("core")
-    blk_count = lax.axis_size("xy") * pair_count
+    pair_count = lax.axis_size("quad")
+    blk_count = lax.axis_size("grp") * pair_count
     req_count = lax.axis_size("req")
-    core_index = lax.axis_index("core")
-    blk_index = lax.axis_index("xy") * pair_count + core_index
+    core_index = lax.axis_index("quad")
+    blk_index = lax.axis_index("grp") * pair_count + core_index
     req_index = lax.axis_index("req")
     vis_width = patches.shape[1]
     gathered_text = lax.all_gather(text_embed, BLK, axis=1, tiled=True)
-    partner_weight = lax.ppermute(out_weight, "core", [(0, 1), (1, 0)])
+    quad_weights = [out_weight] + [
+        lax.ppermute(
+            out_weight, "quad", [(j, (j + shift) % pair_count) for j in range(pair_count)]
+        )
+        for shift in range(1, pair_count)
+    ]
     patch_rows = patches.astype(jnp.float32)
     normed = layer_norm(patch_rows, vis_ln_gain, vis_ln_bias).astype(jnp.bfloat16)
     pre_act = jnp.dot(normed, vis_up, preferred_element_type=jnp.float32) + vis_up_bias.astype(
@@ -193,22 +198,18 @@
         ),
     ).reshape(tok_grp, -1)
     out_share = tok_grp // blk_count
-    swap = [(0, 1), (1, 0)]
     by_core = attn_out.reshape(blk_count // pair_count, pair_count, out_share, -1)
-    attn_mine = lax.dynamic_index_in_dim(by_core, core_index, 1, keepdims=False)
-    attn_other = lax.ppermute(
-        lax.dynamic_index_in_dim(by_core, 1 - core_index, 1, keepdims=False), "core", swap
-    )
-    pair_attn = jnp.concatenate([attn_mine, attn_other], axis=-1).reshape(
-        tok_grp // pair_count, -1
-    )
-    pair_weight = jnp.concatenate([out_weight, partner_weight], axis=0)
+    from_quad = lax.all_to_all(by_core.transpose(1, 0, 2, 3), "quad", 0, 0, tiled=False)
+    sources = (core_index - jnp.arange(pair_count, dtype=jnp.int32)) % pair_count
+    in_order = jnp.take(from_quad, sources, axis=0)
+    pair_attn = in_order.transpose(1, 2, 0, 3).reshape(tok_grp // pair_count, -1)
+    pair_weight = jnp.concatenate(quad_weights, axis=0)
     pair_sum = jnp.dot(pair_attn, pair_weight, preferred_element_type=jnp.float32).astype(
         jnp.bfloat16
     )
     chip_count = blk_count // pair_count
     sums_here = lax.all_to_all(
-        pair_sum.reshape(chip_count, out_share, -1), "xy", 0, 0, tiled=False
+        pair_sum.reshape(chip_count, out_share, -1), "grp", 0, 0, tiled=False
     )
     summed_heads = jnp.sum(sums_here.astype(jnp.float32), axis=0)
     residual = lax.dynamic_slice_in_dim(features, blk_index * out_share, out_share, 0).astype(
@@ -217,12 +218,12 @@
     return (residual + summed_heads).astype(jnp.bfloat16)
 
 
-BLK = ("xy", "core")
+BLK = ("grp", "quad")
 
 
 def solution(mesh):
     blk_size, req_size = mesh.devices.shape
-    pair_mesh = Mesh(mesh.devices.reshape(blk_size // 2, 2, req_size), ("xy", "core", "req"))
+    pair_mesh = Mesh(mesh.devices.reshape(blk_size // 4, 4, req_size), ("grp", "quad", "req"))
     return jax.shard_map(
         body,
         mesh=pair_mesh,

time: 278 us -> 272 us (0.978)
  the two profiles are of different devices: /device:TPU:20 before, /device:TPU:8 now
where the time goes in v7:
time: 272 us; the launch traced here: 269 us
  waiting for transfers between devices  129 us (47%)
  starting transfers between devices  43.5 us (16%)
  other arithmetic  28.2 us (10%)
  local copies, waits for them, and re-layouts  28 us (10%)
  matrix products  26.3 us (10%)
  between operations  14 us (5%)
    all_to_all x1, waiting for transfers between devices, body(): lax.all_to_all(jnp.broadcast_to(merged_here[None], (blk_count,) + merged_...  34.3 us
    all_to_all x1, waiting for transfers between devices, body(): lax.all_to_all(pair_sum.reshape(chip_count, out_share, -1), 'grp', 0, 0,...  31.6 us
    all_to_all x1, waiting for transfers between devices, body(): lax.all_to_all(partial.reshape(blk_count, row_share, vis_width), BLK, 0,...  21.2 us
    all_to_all x1, waiting for transfers between devices, body(): lax.all_to_all(by_core.transpose(1, 0, 2, 3), 'quad', 0, 0, tiled=False)  18.8 us
    all_to_all x1, waiting for transfers between devices, body(): lax.all_to_all(jnp.broadcast_to(mine_cols[None], (blk_count,) + mine_cols...  12.9 us
    all_to_all x1, waiting for transfers between devices, body(): lax.all_to_all(outgoing, 'req', split_axis=0, concat_axis=0, tiled=True)  9.65 us
    all_to_all x1, starting transfers between devices, body(): lax.all_to_all(outgoing, 'req', split_axis=0, concat_axis=0, tiled=True)  7.74 us
    all_to_all x1, starting transfers between devices, body(): lax.all_to_all(partial.reshape(blk_count, row_share, vis_width), BLK, 0,...  7.58 us
  transfers between devices with their start and end apart: 10, of which 6 were waited for; matrix products, arithmetic and copies ran while one was open for 28% of the time, Pallas kernels for 0%

profile of v7, /device:TPU:8, one launch (start us, length us, event | category | flops | bytes accessed | tf_op | source)
XLA Modules:
  0.0 269.2 jit_solution(9878292730928788900)
XLA Ops:
  9.3 2.0 convert_reduce_fusion.3
  11.3 2.3 multiply_reduce_fusion
  13.6 6.3 %convolution_convert_fusion.2 = bf16[768,1408]{1,0:T(8,128)(2,1)} fusion(bf16[192,1408]{1,0:T(8,128)(2,1)S(1)} %copy-done.12, bf16[1408,192]{0,1:T(8,128)(2,1)S(1)} %copy-done.13, bf16[768,1408]{1,0:T(8,128)(2,1)} %param.22, f32[1408]{0:T(1024)S(1)} %convert_element_type.111, f32[1408]{0:T(1024)S(1)} %convert_element_type.110, ...), kind=kOutput, calls=%fused_computation.45 | convolution fusion | flops 847773696 | bytes 5424896 | tf_op jit(solution)/shard_map/dot_general | solution.py:105
  20.0 7.6 %all-to-all-start = ((bf16[32,24,1408]{2,1,0:T(8,128)(2,1)}), bf16[32,24,1408]{2,1,0:T(8,128)(2,1)}, u32[]{:S(2)}, u32[]{:S(2)}) async-start(bf16[32,24,1408]{2,1,0:T(8,128)(2,1)} %bitcast.88), calls=%async_computation | async-start | bytes 4325376 | tf_op jit(solution)/shard_map/all_to_all | solution.py:108
  27.6 3.9 %convert_element_type.109 = f32[768,1408]{1,0:T(8,128)} convert(bf16[768,1408]{1,0:T(8,128)(2,1)} %param.22) | non-fusion elementwise | flops 1081344 | bytes 6488064 | tf_op jit(solution)/shard_map/convert_element_type | solution.py:99
  31.6 4.5 %reduce-window.19 = s32[8,8,2,128]{3,1,2,0:T(8,128)S(1)} reduce-window(s32[8,8,2,128]{3,1,2,0:T(8,128)S(1)} %convert_bitcast_fusion, s32[]{:T(128)} %constant.70.clone.1), window={size=1x1x1x128 pad=0_0x0_0x0_0x127_0}, to_apply=%region_4.6 | reduce-window | flops 2080768 | bytes 131076 | tf_op jit(solution)/shard_map/reduce-window.2
  36.5 21.2 %all-to-all-done = bf16[32,24,1408]{2,1,0:T(8,128)(2,1)} async-done(((bf16[32,24,1408]{2,1,0:T(8,128)(2,1)}), bf16[32,24,1408]{2,1,0:T(8,128)(2,1)}, u32[]{:S(2)}, u32[]{:S(2)}) %all-to-all-start) | async-done | bytes 2162720 | tf_op jit(solution)/shard_map/all_to_all | solution.py:108
  62.9 7.0 %all-to-all-start.1 = ((bf16[32,6,5632]{2,1,0:T(8,128)(2,1)}), bf16[32,6,5632]{2,1,0:T(8,128)(2,1)}, u32[]{:S(2)}, u32[]{:S(2)}) async-start(bf16[32,6,5632]{2,1,0:T(8,128)(2,1)} %broadcast_in_dim.130), calls=%async_computation.1 | async-start | bytes 5767168 | tf_op jit(solution)/shard_map/all_to_all | solution.py:116
  72.2 6.2 %scatter_custom_fusion = s32[192]{0:T(256)S(1)} fusion(s32[1536]{0:T(1024)S(1)} %compare_select_fusion, s32[1536]{0:T(1024)S(1)} %iota.54, s32[]{:T(128)} %constant.70.clone.1), kind=kCustom, calls=%fused_computation.207 | custom fusion | bytes 772 | tf_op jit(solution)/shard_map/scatter | solution.py:157
  79.8 34.3 %all-to-all-done.1 = bf16[32,6,5632]{2,1,0:T(8,128)(2,1)} async-done(((bf16[32,6,5632]{2,1,0:T(8,128)(2,1)}), bf16[32,6,5632]{2,1,0:T(8,128)(2,1)}, u32[]{:S(2)}, u32[]{:S(2)}) %all-to-all-start.1) | async-done | bytes 2162720 | tf_op jit(solution)/shard_map/all_to_all | solution.py:116
  114.1 4.3 %reshape.372 = bf16[192,5632]{1,0:T(8,128)(2,1)} reshape(bf16[32,6,5632]{2,1,0:T(8,128)(2,1)} %all-to-all-done.1) | data formatting | bytes 4325376 | tf_op jit(solution)/shard_map/reshape | solution.py:124
  118.4 2.3 fusion.32
  123.6 7.7 %all-to-all-start.2 = ((bf16[8,66,128]{2,1,0:T(8,128)(2,1)}), bf16[8,66,128]{2,1,0:T(8,128)(2,1)S(1)}, u32[]{:S(2)}, u32[]{:S(2)}) async-start(bf16[8,66,128]{2,1,0:T(8,128)(2,1)} %broadcast_select_fusion), calls=%async_computation.2 | async-start | bytes 294912 | tf_op jit(solution)/shard_map/all_to_all | solution.py:149
  131.4 9.6 %all-to-all-done.2 = bf16[8,66,128]{2,1,0:T(8,128)(2,1)S(1)} async-done(((bf16[8,66,128]{2,1,0:T(8,128)(2,1)}), bf16[8,66,128]{2,1,0:T(8,128)(2,1)S(1)}, u32[]{:S(2)}, u32[]{:S(2)}) %all-to-all-start.2) | async-done | bytes 135200 | tf_op jit(solution)/shard_map/all_to_all | solution.py:149
  143.4 7.3 %all-to-all-start.3 = ((bf16[32,192,128]{2,1,0:T(8,128)(2,1)}), bf16[32,192,128]{2,1,0:T(8,128)(2,1)}, u32[]{:S(2)}, u32[]{:S(2)}) async-start(bf16[32,192,128]{2,1,0:T(8,128)(2,1)} %broadcast_in_dim.135), calls=%async_computation.3 | async-start | bytes 3145728 | tf_op jit(solution)/shard_map/all_to_all | solution.py:160
  158.8 12.9 %all-to-all-done.3 = bf16[32,192,128]{2,1,0:T(8,128)(2,1)} async-done(((bf16[32,192,128]{2,1,0:T(8,128)(2,1)}), bf16[32,192,128]{2,1,0:T(8,128)(2,1)}, u32[]{:S(2)}, u32[]{:S(2)}) %all-to-all-start.3) | async-done | bytes 1572896 | tf_op jit(solution)/shard_map/all_to_all | solution.py:160
  171.8 6.6 %fusion.7 = (f32[1024]{0:T(1024)S(1)}, bf16[1024,4096]{1,0:T(8,128)(2,1)S(1)}) fusion(bf16[1024,4096]{1,0:T(8,128)(2,1)} %all-gather.2.cloned.1.call-done, s32[1024]{0:T(1024)S(1)} %scatter_custom_fusion.1, pred[1024]{0:T(1024)(128)(4,1)S(1)} %broadcast_compare_fusion.1, bf16[32,192,128]{2,1,0:T(8,128)(2,1)} %all-to-all-done.3), kind=kOutput, calls=%fused_computation.21 | convolution fusion | flops 1631779840 | bytes 18359296 | tf_op jit(solution)/shard_map/dot_general | solution.py:172
  178.4 3.8 %fusion.10 = f32[1024,384]{0,1:T(8,128)S(1)} fusion(bf16[1024,4096]{1,0:T(8,128)(2,1)S(1)} %get-tuple-element.106, f32[4096]{0:T(1024)S(1)} %convert_element_type.125, f32[1024]{0:T(1024)S(1)} %add_rsqrt_fusion, bf16[4096,128]{1,0:T(8,128)(2,1)S(1)} %copy-done.9, bf16[4096,128]{1,0:T(8,128)(2,1)S(1)} %copy-done.10, bf16[4096,128]{1,0:T(8,128)(2,1)S(1)} %copy-done.11), kind=kOutput, calls=%fused_computation.24 | convolution fusion | flops 3247439872 | bytes 13127680 | tf_op jit(solution)/shard_map/dot_general | solution.py:183
  185.8 4.8 %while.10 = (s32[]{:T(128)}, bf16[2,512,128]{2,1,0:T(8,128)(2,1)}, pred[2,512,1024]{2,1,0:T(32,128)(4,1)S(1)}, bf16[2,512,128]{2,1,0:T(8,128)(2,1)S(1)}, bf16[10...) while((s32[]{:T(128)}, bf16[2,512,128]{2,1,0:T(8,128)(2,1)}, ...), condition=%wide.region_18.20_spmd, body=%wide.region_15.19_spmd.sunk | while | flops 272694272 | bytes 9710729 | solution.py:193
  192.3 5.6 %all-to-all-start.4 = ((bf16[4,8,32,128]{3,2,1,0:T(8,128)(2,1)}), bf16[4,8,32,128]{3,2,1,0:T(8,128)(2,1)S(1)}, u32[]{:S(2)}, u32[]{:S(2)}) async-start(bf16[4,8,32,128]{3,2,1,0:T(8,128)(2,1)} %bitcast.76), calls=%async_computation.4 | async-start | bytes 524288 | tf_op jit(solution)/shard_map/all_to_all | solution.py:202
  198.0 18.8 %all-to-all-done.4 = bf16[4,8,32,128]{3,2,1,0:T(8,128)(2,1)S(1)} async-done(((bf16[4,8,32,128]{3,2,1,0:T(8,128)(2,1)}), bf16[4,8,32,128]{3,2,1,0:T(8,128)(2,1)S(1)}, u32[]{:S(2)}, u32[]{:S(2)}) %all-to-all-start.4) | async-done | bytes 262176 | tf_op jit(solution)/shard_map/all_to_all | solution.py:202
  217.7 4.8 %convolution_convert_fusion.1 = bf16[256,4096]{1,0:T(8,128)(2,1)} fusion(bf16[128,4096]{1,0:T(8,128)(2,1)} %collective-permute-done.2, bf16[128,4096]{1,0:T(8,128)(2,1)} %collective-permute-done.1, bf16[128,4096]{1,0:T(8,128)(2,1)} %collective-permute-done, bf16[128,4096]{1,0:T(8,128)(2,1)} %param.39, bf16[32,8,4,128]{3,2,1,0:T(4,128)(2,1)S(1)} %bitcast.91), kind=kOutput, calls=%fused_computation.28 | convolution fusion | flops 1091567616 | bytes 6553600 | tf_op jit(solution)/shard_map/dot_general | solution.py:207
  222.5 6.2 %all-to-all-start.5 = ((bf16[8,32,4096]{2,1,0:T(8,128)(2,1)}), bf16[8,32,4096]{2,1,0:T(8,128)(2,1)S(1)}, u32[]{:S(2)}, u32[]{:S(2)}) async-start(bf16[8,32,4096]{2,1,0:T(8,128)(2,1)} %bitcast.89), calls=%async_computation.5 | async-start | bytes 4194304 | tf_op jit(solution)/shard_map/all_to_all | solution.py:211
  228.8 31.6 %all-to-all-done.5 = bf16[8,32,4096]{2,1,0:T(8,128)(2,1)S(1)} async-done(((bf16[8,32,4096]{2,1,0:T(8,128)(2,1)}), bf16[8,32,4096]{2,1,0:T(8,128)(2,1)S(1)}, u32[]{:S(2)}, u32[]{:S(2)}) %all-to-all-start.5) | async-done | bytes 2097184 | tf_op jit(solution)/shard_map/all_to_all | solution.py:211
  (139 shorter events, 38.2 us)
Async XLA Ops:
  6.5 111.9 %copy-start = (bf16[5632,128]{1,0:T(8,128)(2,1)S(1)}, bf16[5632,128]{1,0:T(8,128)(2,1)}, u32[]{:S(2)}) copy-start(bf16[5632,128]{1,0:T(8,128)(2,1)} %param.30) | copy-start | bytes 4325380
  6.5 7.1 %copy-start.13 = (bf16[1408,192]{0,1:T(8,128)(2,1)S(1)}, bf16[1408,192]{0,1:T(8,128)(2,1)}, u32[]{:S(2)}) copy-start(bf16[1408,192]{0,1:T(8,128)(2,1)} %param.25) | copy-start | bytes 1622020
  6.5 7.1 %copy-start.12 = (bf16[192,1408]{1,0:T(8,128)(2,1)S(1)}, bf16[192,1408]{1,0:T(8,128)(2,1)}, u32[]{:S(2)}) copy-start(bf16[192,1408]{1,0:T(8,128)(2,1)} %param.27) | copy-start | bytes 1622020
  6.5 165.2 %all-gather.2.cloned.1.call-start = ((), (), s32[]{:S(2)}) async-start(), calls=%async_computation.6 | async-start | bytes 8650752 | tf_op jit(solution)/shard_map/all_gather | solution.py:92
  20.0 37.8 %all-to-all-start = ((bf16[32,24,1408]{2,1,0:T(8,128)(2,1)}), bf16[32,24,1408]{2,1,0:T(8,128)(2,1)}, u32[]{:S(2)}, u32[]{:S(2)}) async-start(bf16[32,24,1408]{2,1,0:T(8,128)(2,1)} %bitcast.88), calls=%async_computation | async-start | bytes 4325376 | tf_op jit(solution)/shard_map/all_to_all | solution.py:108
  27.5 3.9 %copy-start.7 = (bf16[1408]{0:T(1024)(128)(2,1)S(1)}, bf16[1408]{0:T(1024)(128)(2,1)}, u32[]{:S(2)}) copy-start(bf16[1408]{0:T(1024)(128)(2,1)} %param.28) | copy-start | bytes 8452
  27.6 3.9 %copy-start.8 = (bf16[1408]{0:T(1024)(128)(2,1)S(1)}, bf16[1408]{0:T(1024)(128)(2,1)}, u32[]{:S(2)}) copy-start(bf16[1408]{0:T(1024)(128)(2,1)} %param.29) | copy-start | bytes 8452
  27.6 3.9 %copy-start.3 = (s32[1536]{0:T(1024)S(1)}, s32[1536]{0:T(1024)}, u32[]{:S(2)}) copy-start(s32[1536]{0:T(1024)} %param.32) | copy-start | bytes 18436
  61.0 8.9 %copy-start.14 = (bf16[128]{0:T(256)(128)(2,1)S(1)}, bf16[128]{0:T(256)(128)(2,1)}, u32[]{:S(2)}) copy-start(bf16[128]{0:T(256)(128)(2,1)} %param.31) | copy-start | bytes 772
  62.9 51.2 %all-to-all-start.1 = ((bf16[32,6,5632]{2,1,0:T(8,128)(2,1)}), bf16[32,6,5632]{2,1,0:T(8,128)(2,1)}, u32[]{:S(2)}, u32[]{:S(2)}) async-start(bf16[32,6,5632]{2,1,0:T(8,128)(2,1)} %broadcast_in_dim.130), calls=%async_computation.1 | async-start | bytes 5767168 | tf_op jit(solution)/shard_map/all_to_all | solution.py:116
  120.8 33.4 %copy-start.5 = (bf16[4096]{0:T(1024)(128)(2,1)S(1)}, bf16[4096]{0:T(1024)(128)(2,1)}, u32[]{:S(2)}) copy-start(bf16[4096]{0:T(1024)(128)(2,1)} %param.35) | copy-start | bytes 24580
  120.8 33.5 %copy-start.4 = (s32[1,1024]{1,0:T(1,128)S(1)}, s32[1,1024]{1,0:T(1,128)}, u32[]{:S(2)}) copy-start(s32[1,1024]{1,0:T(1,128)} %param.34) | copy-start | bytes 12292
  123.6 17.4 %all-to-all-start.2 = ((bf16[8,66,128]{2,1,0:T(8,128)(2,1)}), bf16[8,66,128]{2,1,0:T(8,128)(2,1)S(1)}, u32[]{:S(2)}, u32[]{:S(2)}) async-start(bf16[8,66,128]{2,1,0:T(8,128)(2,1)} %broadcast_select_fusion), calls=%async_computation.2 | async-start | bytes 294912 | tf_op jit(solution)/shard_map/all_to_all | solution.py:149
  143.4 28.3 %all-to-all-start.3 = ((bf16[32,192,128]{2,1,0:T(8,128)(2,1)}), bf16[32,192,128]{2,1,0:T(8,128)(2,1)}, u32[]{:S(2)}, u32[]{:S(2)}) async-start(bf16[32,192,128]{2,1,0:T(8,128)(2,1)} %broadcast_in_dim.135), calls=%async_computation.3 | async-start | bytes 3145728 | tf_op jit(solution)/shard_map/all_to_all | solution.py:160
  150.8 66.9 %collective-permute-start = (bf16[128,4096]{1,0:T(8,128)(2,1)}, bf16[128,4096]{1,0:T(8,128)(2,1)}, u32[]{:S(2)}, u32[]{:S(2)}) collective-permute-start(bf16[128,4096]{1,0:T(8,128)(2,1)} %param.39), channel_id=1, source_target_pairs={{0,8},{8,16},{16,24},{24,0},{1,9},{9,17},{17,25},{25,1},{2,10},{10... | collective-permute-start | bytes 3145736 | tf_op jit(solution)/shard_map/ppermute | solution.py:94
  151.1 66.6 %collective-permute-start.1 = (bf16[128,4096]{1,0:T(8,128)(2,1)}, bf16[128,4096]{1,0:T(8,128)(2,1)}, u32[]{:S(2)}, u32[]{:S(2)}) collective-permute-start(bf16[128,4096]{1,0:T(8,128)(2,1)} %param.39), channel_id=1, source_target_pairs={{0,16},{8,24},{16,0},{24,8},{1,17},{9,25},{17,1},{25,9},{2,18},{10... | collective-permute-start | bytes 3145736 | tf_op jit(solution)/shard_map/ppermute | solution.py:94
  151.5 66.2 %collective-permute-start.2 = (bf16[128,4096]{1,0:T(8,128)(2,1)}, bf16[128,4096]{1,0:T(8,128)(2,1)}, u32[]{:S(2)}, u32[]{:S(2)}) collective-permute-start(bf16[128,4096]{1,0:T(8,128)(2,1)} %param.39), channel_id=1, source_target_pairs={{0,24},{8,0},{16,8},{24,16},{1,25},{9,1},{17,9},{25,17},{2,26},{10... | collective-permute-start | bytes 3145736 | tf_op jit(solution)/shard_map/ppermute | solution.py:94
  171.7 6.7 %copy-start.9 = (bf16[4096,128]{1,0:T(8,128)(2,1)S(1)}, bf16[4096,128]{1,0:T(8,128)(2,1)}, u32[]{:S(2)}) copy-start(bf16[4096,128]{1,0:T(8,128)(2,1)} %param.38) | copy-start | bytes 3145732
  171.7 6.7 %copy-start.10 = (bf16[4096,128]{1,0:T(8,128)(2,1)S(1)}, bf16[4096,128]{1,0:T(8,128)(2,1)}, u32[]{:S(2)}) copy-start(bf16[4096,128]{1,0:T(8,128)(2,1)} %param.37) | copy-start | bytes 3145732
  171.7 6.7 %copy-start.11 = (bf16[4096,128]{1,0:T(8,128)(2,1)S(1)}, bf16[4096,128]{1,0:T(8,128)(2,1)}, u32[]{:S(2)}) copy-start(bf16[4096,128]{1,0:T(8,128)(2,1)} %param.36) | copy-start | bytes 3145732
  178.4 3.9 %copy-start.6 = (bf16[1024,4096]{1,0:T(8,128)(2,1)}, bf16[1024,4096]{1,0:T(8,128)(2,1)S(1)}, u32[]{:S(2)}) copy-start(bf16[1024,4096]{1,0:T(8,128)(2,1)S(1)} %get-tuple-element.106) | copy-start | bytes 25165828
  185.8 1.1 copy-start.1
  192.3 24.4 %all-to-all-start.4 = ((bf16[4,8,32,128]{3,2,1,0:T(8,128)(2,1)}), bf16[4,8,32,128]{3,2,1,0:T(8,128)(2,1)S(1)}, u32[]{:S(2)}, u32[]{:S(2)}) async-start(bf16[4,8,32,128]{3,2,1,0:T(8,128)(2,1)} %bitcast.76), calls=%async_computation.4 | async-start | bytes 524288 | tf_op jit(solution)/shard_map/all_to_all | solution.py:202
  222.5 37.8 %all-to-all-start.5 = ((bf16[8,32,4096]{2,1,0:T(8,128)(2,1)}), bf16[8,32,4096]{2,1,0:T(8,128)(2,1)S(1)}, u32[]{:S(2)}, u32[]{:S(2)}) async-start(bf16[8,32,4096]{2,1,0:T(8,128)(2,1)} %bitcast.89), calls=%async_computation.5 | async-start | bytes 4194304 | tf_op jit(solution)/shard_map/all_to_all | solution.py:211
  (3 other events, 2.5 us)
Sparse Core Ops, SparseCore 0:
  9.8 114.3 all-gather.1

commit v8 on v7

--- a/solution.py
+++ b/solution.py
@@ -199,9 +199,19 @@
     ).reshape(tok_grp, -1)
     out_share = tok_grp // blk_count
     by_core = attn_out.reshape(blk_count // pair_count, pair_count, out_share, -1)
-    from_quad = lax.all_to_all(by_core.transpose(1, 0, 2, 3), "quad", 0, 0, tiled=False)
-    sources = (core_index - jnp.arange(pair_count, dtype=jnp.int32)) % pair_count
-    in_order = jnp.take(from_quad, sources, axis=0)
+    in_order = jnp.stack(
+        [lax.dynamic_index_in_dim(by_core, core_index, 1, keepdims=False)]
+        + [
+            lax.ppermute(
+                lax.dynamic_index_in_dim(
+                    by_core, (core_index + shift) % pair_count, 1, keepdims=False
+                ),
+                "quad",
+                [(j, (j + shift) % pair_count) for j in range(pair_count)],
+            )
+            for shift in range(1, pair_count)
+        ]
+    )
     pair_attn = in_order.transpose(1, 2, 0, 3).reshape(tok_grp // pair_count, -1)
     pair_weight = jnp.concatenate(quad_weights, axis=0)
     pair_sum = jnp.dot(pair_attn, pair_weight, preferred_element_type=jnp.float32).astype(

time: 272 us -> 273 us (level)
  waiting for transfers between devices: 129 us -> 134 us
  starting transfers between devices: 43.5 us -> 40.6 us
    ppermute x0 -> x3, waiting for transfers between devices: none -> 22.8 us  [body(): lax.ppermute(lax.dynamic_index_in_dim(by_core, (core_index + shift) % pai...]
    all_to_all x1 -> x0, waiting for transfers between devices: 18.8 us -> none  [body(): lax.all_to_all(by_core.transpose(1, 0, 2, 3), 'quad', 0, 0, tiled=False)]
    all_to_all x1 -> x0, starting transfers between devices: 5.64 us -> none  [body(): lax.all_to_all(by_core.transpose(1, 0, 2, 3), 'quad', 0, 0, tiled=False)]
  transfers between devices with their start and end apart: 10 -> 12, of which waited for: 6 -> 8; matrix products, arithmetic and copies ran while one was open for 28% -> 27% of each run, Pallas kernels for 0% -> 0%
where the time goes in v8:
time: 273 us; the launch traced here: 270 us
  waiting for transfers between devices  134 us (49%)
  starting transfers between devices  40.6 us (15%)
  other arithmetic  28.1 us (10%)
  local copies, waits for them, and re-layouts  26.5 us (10%)
  matrix products  26.3 us (10%)
  between operations  14 us (5%)
    all_to_all x1, waiting for transfers between devices, body(): lax.all_to_all(jnp.broadcast_to(merged_here[None], (blk_count,) + merged_...  34.3 us
    all_to_all x1, waiting for transfers between devices, body(): lax.all_to_all(pair_sum.reshape(chip_count, out_share, -1), 'grp', 0, 0,...  32.5 us
    ppermute x3, waiting for transfers between devices, body(): lax.ppermute(lax.dynamic_index_in_dim(by_core, (core_index + shift) % pai...  22.8 us
    all_to_all x1, waiting for transfers between devices, body(): lax.all_to_all(partial.reshape(blk_count, row_share, vis_width), BLK, 0,...  21.2 us
    all_to_all x1, waiting for transfers between devices, body(): lax.all_to_all(jnp.broadcast_to(mine_cols[None], (blk_count,) + mine_cols...  13.1 us
    all_to_all x1, waiting for transfers between devices, body(): lax.all_to_all(outgoing, 'req', split_axis=0, concat_axis=0, tiled=True)  9.65 us
    all_to_all x1, starting transfers between devices, body(): lax.all_to_all(outgoing, 'req', split_axis=0, concat_axis=0, tiled=True)  7.74 us
    all_to_all x1, starting transfers between devices, body(): lax.all_to_all(partial.reshape(blk_count, row_share, vis_width), BLK, 0,...  7.58 us
  transfers between devices with their start and end apart: 12, of which 8 were waited for; matrix products, arithmetic and copies ran while one was open for 27% of the time, Pallas kernels for 0%

profile of v8, /device:TPU:8, one launch (start us, length us, event | category | flops | bytes accessed | tf_op | source)
XLA Modules:
  0.0 269.9 jit_solution(1359147385702358832)
XLA Ops:
  9.3 2.0 convert_reduce_fusion.3
  11.3 2.3 multiply_reduce_fusion
  13.6 6.3 %convolution_convert_fusion.2 = bf16[768,1408]{1,0:T(8,128)(2,1)} fusion(bf16[192,1408]{1,0:T(8,128)(2,1)S(1)} %copy-done.12, bf16[1408,192]{0,1:T(8,128)(2,1)S(1)} %copy-done.13, bf16[768,1408]{1,0:T(8,128)(2,1)} %param.22, f32[1408]{0:T(1024)S(1)} %convert_element_type.111, f32[1408]{0:T(1024)S(1)} %convert_element_type.110, ...), kind=kOutput, calls=%fused_computation.44 | convolution fusion | flops 847773696 | bytes 5424896 | tf_op jit(solution)/shard_map/dot_general | solution.py:105
  20.0 7.6 %all-to-all-start = ((bf16[32,24,1408]{2,1,0:T(8,128)(2,1)}), bf16[32,24,1408]{2,1,0:T(8,128)(2,1)}, u32[]{:S(2)}, u32[]{:S(2)}) async-start(bf16[32,24,1408]{2,1,0:T(8,128)(2,1)} %bitcast.94), calls=%async_computation | async-start | bytes 4325376 | tf_op jit(solution)/shard_map/all_to_all | solution.py:108
  27.6 3.9 %convert_element_type.109 = f32[768,1408]{1,0:T(8,128)} convert(bf16[768,1408]{1,0:T(8,128)(2,1)} %param.22) | non-fusion elementwise | flops 1081344 | bytes 6488064 | tf_op jit(solution)/shard_map/convert_element_type | solution.py:99
  31.6 4.5 %reduce-window.19 = s32[8,8,2,128]{3,1,2,0:T(8,128)S(1)} reduce-window(s32[8,8,2,128]{3,1,2,0:T(8,128)S(1)} %convert_bitcast_fusion, s32[]{:T(128)} %constant.91.clone.1), window={size=1x1x1x128 pad=0_0x0_0x0_0x127_0}, to_apply=%region_4.6 | reduce-window | flops 2080768 | bytes 131076 | tf_op jit(solution)/shard_map/reduce-window.2
  36.5 21.2 %all-to-all-done = bf16[32,24,1408]{2,1,0:T(8,128)(2,1)} async-done(((bf16[32,24,1408]{2,1,0:T(8,128)(2,1)}), bf16[32,24,1408]{2,1,0:T(8,128)(2,1)}, u32[]{:S(2)}, u32[]{:S(2)}) %all-to-all-start) | async-done | bytes 2162720 | tf_op jit(solution)/shard_map/all_to_all | solution.py:108
  62.9 7.0 %all-to-all-start.1 = ((bf16[32,6,5632]{2,1,0:T(8,128)(2,1)}), bf16[32,6,5632]{2,1,0:T(8,128)(2,1)}, u32[]{:S(2)}, u32[]{:S(2)}) async-start(bf16[32,6,5632]{2,1,0:T(8,128)(2,1)} %broadcast_in_dim.120), calls=%async_computation.1 | async-start | bytes 5767168 | tf_op jit(solution)/shard_map/all_to_all | solution.py:116
  72.2 6.2 %scatter_custom_fusion = s32[192]{0:T(256)S(1)} fusion(s32[1536]{0:T(1024)S(1)} %compare_select_fusion, s32[1536]{0:T(1024)S(1)} %iota.48, s32[]{:T(128)} %constant.91.clone.1), kind=kCustom, calls=%fused_computation.198 | custom fusion | bytes 772 | tf_op jit(solution)/shard_map/scatter | solution.py:157
  79.8 34.3 %all-to-all-done.1 = bf16[32,6,5632]{2,1,0:T(8,128)(2,1)} async-done(((bf16[32,6,5632]{2,1,0:T(8,128)(2,1)}), bf16[32,6,5632]{2,1,0:T(8,128)(2,1)}, u32[]{:S(2)}, u32[]{:S(2)}) %all-to-all-start.1) | async-done | bytes 2162720 | tf_op jit(solution)/shard_map/all_to_all | solution.py:116
  114.1 4.3 %reshape.319 = bf16[192,5632]{1,0:T(8,128)(2,1)} reshape(bf16[32,6,5632]{2,1,0:T(8,128)(2,1)} %all-to-all-done.1) | data formatting | bytes 4325376 | tf_op jit(solution)/shard_map/reshape | solution.py:124
  118.4 2.3 fusion.32
  123.6 7.7 %all-to-all-start.2 = ((bf16[8,66,128]{2,1,0:T(8,128)(2,1)}), bf16[8,66,128]{2,1,0:T(8,128)(2,1)S(1)}, u32[]{:S(2)}, u32[]{:S(2)}) async-start(bf16[8,66,128]{2,1,0:T(8,128)(2,1)} %broadcast_select_fusion), calls=%async_computation.2 | async-start | bytes 294912 | tf_op jit(solution)/shard_map/all_to_all | solution.py:149
  131.4 9.6 %all-to-all-done.2 = bf16[8,66,128]{2,1,0:T(8,128)(2,1)S(1)} async-done(((bf16[8,66,128]{2,1,0:T(8,128)(2,1)}), bf16[8,66,128]{2,1,0:T(8,128)(2,1)S(1)}, u32[]{:S(2)}, u32[]{:S(2)}) %all-to-all-start.2) | async-done | bytes 135200 | tf_op jit(solution)/shard_map/all_to_all | solution.py:149
  143.4 7.3 %all-to-all-start.3 = ((bf16[32,192,128]{2,1,0:T(8,128)(2,1)}), bf16[32,192,128]{2,1,0:T(8,128)(2,1)}, u32[]{:S(2)}, u32[]{:S(2)}) async-start(bf16[32,192,128]{2,1,0:T(8,128)(2,1)} %broadcast_in_dim.125), calls=%async_computation.3 | async-start | bytes 3145728 | tf_op jit(solution)/shard_map/all_to_all | solution.py:160
  158.6 13.1 %all-to-all-done.3 = bf16[32,192,128]{2,1,0:T(8,128)(2,1)} async-done(((bf16[32,192,128]{2,1,0:T(8,128)(2,1)}), bf16[32,192,128]{2,1,0:T(8,128)(2,1)}, u32[]{:S(2)}, u32[]{:S(2)}) %all-to-all-start.3) | async-done | bytes 1572896 | tf_op jit(solution)/shard_map/all_to_all | solution.py:160
  171.8 6.6 %fusion.7 = (f32[1024]{0:T(1024)S(1)}, bf16[1024,4096]{1,0:T(8,128)(2,1)S(1)}) fusion(bf16[1024,4096]{1,0:T(8,128)(2,1)} %all-gather.2.cloned.1.call-done, s32[1024]{0:T(1024)S(1)} %scatter_custom_fusion.1, pred[1024]{0:T(1024)(128)(4,1)S(1)} %broadcast_compare_fusion.1, bf16[32,192,128]{2,1,0:T(8,128)(2,1)} %all-to-all-done.3), kind=kOutput, calls=%fused_computation.20 | convolution fusion | flops 1631779840 | bytes 18359296 | tf_op jit(solution)/shard_map/dot_general | solution.py:172
  178.4 3.8 %fusion.10 = f32[1024,384]{0,1:T(8,128)S(1)} fusion(bf16[1024,4096]{1,0:T(8,128)(2,1)S(1)} %get-tuple-element.110, f32[4096]{0:T(1024)S(1)} %convert_element_type.125, f32[1024]{0:T(1024)S(1)} %add_rsqrt_fusion, bf16[4096,128]{1,0:T(8,128)(2,1)S(1)} %copy-done.9, bf16[4096,128]{1,0:T(8,128)(2,1)S(1)} %copy-done.10, bf16[4096,128]{1,0:T(8,128)(2,1)S(1)} %copy-done.11), kind=kOutput, calls=%fused_computation.23 | convolution fusion | flops 3247439872 | bytes 13127680 | tf_op jit(solution)/shard_map/dot_general | solution.py:183
  185.8 4.8 %while.10 = (s32[]{:T(128)}, bf16[2,512,128]{2,1,0:T(8,128)(2,1)}, pred[2,512,1024]{2,1,0:T(32,128)(4,1)S(1)}, bf16[2,512,128]{2,1,0:T(8,128)(2,1)S(1)}, bf16[10...) while((s32[]{:T(128)}, bf16[2,512,128]{2,1,0:T(8,128)(2,1)}, ...), condition=%wide.region_18.20_spmd, body=%wide.region_15.19_spmd.sunk | while | flops 272694272 | bytes 9710729 | solution.py:193
  191.7 2.4 collective-permute-start.1
  194.1 20.9 %collective-permute-done = bf16[8,32,128]{2,1,0:T(8,128)(2,1)S(1)} collective-permute-done((bf16[8,32,128]{2,1,0:T(8,128)(2,1)S(1)}, bf16[8,32,128]{2,1,0:T(8,128)(2,1)S(1)}, u32[]{:S(2)}, u32[]{:S(2)}) %collective-permute-start) | collective-permute-done | bytes 65568 | tf_op jit(solution)/shard_map/ppermute | solution.py:205
  217.1 4.8 %convolution_convert_fusion.1 = bf16[256,4096]{1,0:T(8,128)(2,1)} fusion(bf16[128,4096]{1,0:T(8,128)(2,1)} %collective-permute-done.5, bf16[128,4096]{1,0:T(8,128)(2,1)} %collective-permute-done.4, bf16[128,4096]{1,0:T(8,128)(2,1)} %collective-permute-done.3, bf16[128,4096]{1,0:T(8,128)(2,1)} %param.39, bf16[32,8,4,128]{3,2,1,0:T(4,128)(2,1)S(1)} %bitcast.97), kind=kOutput, calls=%fused_computation.27 | convolution fusion | flops 1091567616 | bytes 6553600 | tf_op jit(solution)/shard_map/dot_general | solution.py:217
  222.0 6.6 %all-to-all-start.4 = ((bf16[8,32,4096]{2,1,0:T(8,128)(2,1)}), bf16[8,32,4096]{2,1,0:T(8,128)(2,1)S(1)}, u32[]{:S(2)}, u32[]{:S(2)}) async-start(bf16[8,32,4096]{2,1,0:T(8,128)(2,1)} %bitcast.95), calls=%async_computation.4 | async-start | bytes 4194304 | tf_op jit(solution)/shard_map/all_to_all | solution.py:221
  228.5 32.5 %all-to-all-done.4 = bf16[8,32,4096]{2,1,0:T(8,128)(2,1)S(1)} async-done(((bf16[8,32,4096]{2,1,0:T(8,128)(2,1)}), bf16[8,32,4096]{2,1,0:T(8,128)(2,1)S(1)}, u32[]{:S(2)}, u32[]{:S(2)}) %all-to-all-start.4) | async-done | bytes 2097184 | tf_op jit(solution)/shard_map/all_to_all | solution.py:221
  (139 shorter events, 38.5 us)
Async XLA Ops:
  6.5 111.9 %copy-start = (bf16[5632,128]{1,0:T(8,128)(2,1)S(1)}, bf16[5632,128]{1,0:T(8,128)(2,1)}, u32[]{:S(2)}) copy-start(bf16[5632,128]{1,0:T(8,128)(2,1)} %param.30) | copy-start | bytes 4325380
  6.5 7.1 %copy-start.13 = (bf16[1408,192]{0,1:T(8,128)(2,1)S(1)}, bf16[1408,192]{0,1:T(8,128)(2,1)}, u32[]{:S(2)}) copy-start(bf16[1408,192]{0,1:T(8,128)(2,1)} %param.25) | copy-start | bytes 1622020
  6.5 7.1 %copy-start.12 = (bf16[192,1408]{1,0:T(8,128)(2,1)S(1)}, bf16[192,1408]{1,0:T(8,128)(2,1)}, u32[]{:S(2)}) copy-start(bf16[192,1408]{1,0:T(8,128)(2,1)} %param.27) | copy-start | bytes 1622020
  6.5 165.2 %all-gather.2.cloned.1.call-start = ((), (), s32[]{:S(2)}) async-start(), calls=%async_computation.5 | async-start | bytes 8650752 | tf_op jit(solution)/shard_map/all_gather | solution.py:92
  20.0 37.8 %all-to-all-start = ((bf16[32,24,1408]{2,1,0:T(8,128)(2,1)}), bf16[32,24,1408]{2,1,0:T(8,128)(2,1)}, u32[]{:S(2)}, u32[]{:S(2)}) async-start(bf16[32,24,1408]{2,1,0:T(8,128)(2,1)} %bitcast.94), calls=%async_computation | async-start | bytes 4325376 | tf_op jit(solution)/shard_map/all_to_all | solution.py:108
  27.5 3.9 %copy-start.7 = (bf16[1408]{0:T(1024)(128)(2,1)S(1)}, bf16[1408]{0:T(1024)(128)(2,1)}, u32[]{:S(2)}) copy-start(bf16[1408]{0:T(1024)(128)(2,1)} %param.28) | copy-start | bytes 8452
  27.6 3.9 %copy-start.8 = (bf16[1408]{0:T(1024)(128)(2,1)S(1)}, bf16[1408]{0:T(1024)(128)(2,1)}, u32[]{:S(2)}) copy-start(bf16[1408]{0:T(1024)(128)(2,1)} %param.29) | copy-start | bytes 8452
  27.6 3.9 %copy-start.3 = (s32[1536]{0:T(1024)S(1)}, s32[1536]{0:T(1024)}, u32[]{:S(2)}) copy-start(s32[1536]{0:T(1024)} %param.32) | copy-start | bytes 18436
  61.0 8.9 %copy-start.14 = (bf16[128]{0:T(256)(128)(2,1)S(1)}, bf16[128]{0:T(256)(128)(2,1)}, u32[]{:S(2)}) copy-start(bf16[128]{0:T(256)(128)(2,1)} %param.31) | copy-start | bytes 772
  62.9 51.2 %all-to-all-start.1 = ((bf16[32,6,5632]{2,1,0:T(8,128)(2,1)}), bf16[32,6,5632]{2,1,0:T(8,128)(2,1)}, u32[]{:S(2)}, u32[]{:S(2)}) async-start(bf16[32,6,5632]{2,1,0:T(8,128)(2,1)} %broadcast_in_dim.120), calls=%async_computation.1 | async-start | bytes 5767168 | tf_op jit(solution)/shard_map/all_to_all | solution.py:116
  120.8 33.4 %copy-start.5 = (bf16[4096]{0:T(1024)(128)(2,1)S(1)}, bf16[4096]{0:T(1024)(128)(2,1)}, u32[]{:S(2)}) copy-start(bf16[4096]{0:T(1024)(128)(2,1)} %param.35) | copy-start | bytes 24580
  120.8 33.5 %copy-start.4 = (s32[1,1024]{1,0:T(1,128)S(1)}, s32[1,1024]{1,0:T(1,128)}, u32[]{:S(2)}) copy-start(s32[1,1024]{1,0:T(1,128)} %param.34) | copy-start | bytes 12292
  123.6 17.4 %all-to-all-start.2 = ((bf16[8,66,128]{2,1,0:T(8,128)(2,1)}), bf16[8,66,128]{2,1,0:T(8,128)(2,1)S(1)}, u32[]{:S(2)}, u32[]{:S(2)}) async-start(bf16[8,66,128]{2,1,0:T(8,128)(2,1)} %broadcast_select_fusion), calls=%async_computation.2 | async-start | bytes 294912 | tf_op jit(solution)/shard_map/all_to_all | solution.py:149
  143.4 28.3 %all-to-all-start.3 = ((bf16[32,192,128]{2,1,0:T(8,128)(2,1)}), bf16[32,192,128]{2,1,0:T(8,128)(2,1)}, u32[]{:S(2)}, u32[]{:S(2)}) async-start(bf16[32,192,128]{2,1,0:T(8,128)(2,1)} %broadcast_in_dim.125), calls=%async_computation.3 | async-start | bytes 3145728 | tf_op jit(solution)/shard_map/all_to_all | solution.py:160
  150.8 66.4 %collective-permute-start.3 = (bf16[128,4096]{1,0:T(8,128)(2,1)}, bf16[128,4096]{1,0:T(8,128)(2,1)}, u32[]{:S(2)}, u32[]{:S(2)}) collective-permute-start(bf16[128,4096]{1,0:T(8,128)(2,1)} %param.39), channel_id=1, source_target_pairs={{0,8},{8,16},{16,24},{24,0},{1,9},{9,17},{17,25},{25,1},{2,10},{10... | collective-permute-start | bytes 3145736 | tf_op jit(solution)/shard_map/ppermute | solution.py:94
  151.1 66.0 %collective-permute-start.4 = (bf16[128,4096]{1,0:T(8,128)(2,1)}, bf16[128,4096]{1,0:T(8,128)(2,1)}, u32[]{:S(2)}, u32[]{:S(2)}) collective-permute-start(bf16[128,4096]{1,0:T(8,128)(2,1)} %param.39), channel_id=1, source_target_pairs={{0,16},{8,24},{16,0},{24,8},{1,17},{9,25},{17,1},{25,9},{2,18},{10... | collective-permute-start | bytes 3145736 | tf_op jit(solution)/shard_map/ppermute | solution.py:94
  151.5 65.6 %collective-permute-start.5 = (bf16[128,4096]{1,0:T(8,128)(2,1)}, bf16[128,4096]{1,0:T(8,128)(2,1)}, u32[]{:S(2)}, u32[]{:S(2)}) collective-permute-start(bf16[128,4096]{1,0:T(8,128)(2,1)} %param.39), channel_id=1, source_target_pairs={{0,24},{8,0},{16,8},{24,16},{1,25},{9,1},{17,9},{25,17},{2,26},{10... | collective-permute-start | bytes 3145736 | tf_op jit(solution)/shard_map/ppermute | solution.py:94
  171.7 6.7 %copy-start.9 = (bf16[4096,128]{1,0:T(8,128)(2,1)S(1)}, bf16[4096,128]{1,0:T(8,128)(2,1)}, u32[]{:S(2)}) copy-start(bf16[4096,128]{1,0:T(8,128)(2,1)} %param.38) | copy-start | bytes 3145732
  171.7 6.7 %copy-start.10 = (bf16[4096,128]{1,0:T(8,128)(2,1)S(1)}, bf16[4096,128]{1,0:T(8,128)(2,1)}, u32[]{:S(2)}) copy-start(bf16[4096,128]{1,0:T(8,128)(2,1)} %param.37) | copy-start | bytes 3145732
  171.7 6.7 %copy-start.11 = (bf16[4096,128]{1,0:T(8,128)(2,1)S(1)}, bf16[4096,128]{1,0:T(8,128)(2,1)}, u32[]{:S(2)}) copy-start(bf16[4096,128]{1,0:T(8,128)(2,1)} %param.36) | copy-start | bytes 3145732
  191.6 23.3 %collective-permute-start = (bf16[8,32,128]{2,1,0:T(8,128)(2,1)S(1)}, bf16[8,32,128]{2,1,0:T(8,128)(2,1)S(1)}, u32[]{:S(2)}, u32[]{:S(2)}) collective-permute-start(bf16[8,32,128]{2,1,0:T(8,128)(2,1)S(1)} %get-tuple-element.104), channel_id=1, source_target_pairs={{0,8},{8,16},{16,24},{24,0},{1,9},{9,17},{17,25},{25,1},{2,10},{10... | collective-permute-start | bytes 196616 | tf_op jit(solution)/shard_map/ppermute | solution.py:205
  191.7 24.1 %collective-permute-start.1 = (bf16[8,32,128]{2,1,0:T(8,128)(2,1)S(1)}, bf16[8,32,128]{2,1,0:T(8,128)(2,1)S(1)}, u32[]{:S(2)}, u32[]{:S(2)}) collective-permute-start(bf16[8,32,128]{2,1,0:T(8,128)(2,1)S(1)} %get-tuple-element.103), channel_id=1, source_target_pairs={{0,16},{8,24},{16,0},{24,8},{1,17},{9,25},{17,1},{25,9},{2,18},{10... | collective-permute-start | bytes 196616 | tf_op jit(solution)/shard_map/ppermute | solution.py:205
  215.0 1.9 collective-permute-start.2
  222.0 39.0 %all-to-all-start.4 = ((bf16[8,32,4096]{2,1,0:T(8,128)(2,1)}), bf16[8,32,4096]{2,1,0:T(8,128)(2,1)S(1)}, u32[]{:S(2)}, u32[]{:S(2)}) async-start(bf16[8,32,4096]{2,1,0:T(8,128)(2,1)} %bitcast.95), calls=%async_computation.4 | async-start | bytes 4194304 | tf_op jit(solution)/shard_map/all_to_all | solution.py:221
  (5 other events, 7.5 us)
Sparse Core Ops, SparseCore 0:
  9.8 114.3 all-gather.1

commit v9 on v7

--- a/solution.py
+++ b/solution.py
@@ -166,21 +166,22 @@
         .at[jnp.take(dest_local, pick)]
         .set(jnp.arange(image_count, dtype=jnp.int32))
     )
-    choose = (lookup[:, None] == jnp.arange(image_count, dtype=jnp.int32)[None, :]).astype(
-        jnp.bfloat16
-    )
-    placed = jnp.dot(choose, mine_rows, preferred_element_type=jnp.float32).astype(jnp.bfloat16)
-    features = jnp.where((lookup < image_count)[:, None], placed, gathered_text)
-    token_values = features.astype(jnp.float32)
-    normed_tokens = (
-        token_values
-        * lax.rsqrt(jnp.mean(token_values * token_values, axis=-1, keepdims=True) + 1e-05)
-        * text_gain.astype(jnp.float32)
-    ).astype(jnp.bfloat16)
+    def rms_normed(rows):
+        row_values = rows.astype(jnp.float32)
+        return (
+            row_values
+            * lax.rsqrt(jnp.mean(row_values * row_values, axis=-1, keepdims=True) + 1e-05)
+            * text_gain.astype(jnp.float32)
+        ).astype(jnp.bfloat16)
+
     positions, allowed = causal_setup(segment_ids[0])
     head_cols = query_weight.shape[1]
     qkv_weight = jnp.concatenate([query_weight, key_weight, value_weight], axis=1)
-    qkv = jnp.dot(normed_tokens, qkv_weight, preferred_element_type=jnp.float32)
+    qkv_text = jnp.dot(rms_normed(gathered_text), qkv_weight, preferred_element_type=jnp.float32)
+    qkv_image = jnp.dot(rms_normed(mine_rows), qkv_weight, preferred_element_type=jnp.float32)
+    is_image = (lookup < image_count)[:, None]
+    qkv_table = jnp.concatenate([qkv_image, jnp.zeros_like(qkv_image[:1])], axis=0)
+    qkv = jnp.where(is_image, jnp.take(qkv_table, lookup, axis=0), qkv_text)
     queries = rotate(qkv[:, :head_cols], positions).astype(jnp.bfloat16)
     keys_rot = rotate(qkv[:, head_cols : 2 * head_cols], positions).astype(jnp.bfloat16)
     values_here = qkv[:, 2 * head_cols :].astype(jnp.bfloat16)
@@ -212,9 +213,13 @@
         pair_sum.reshape(chip_count, out_share, -1), "grp", 0, 0, tiled=False
     )
     summed_heads = jnp.sum(sums_here.astype(jnp.float32), axis=0)
-    residual = lax.dynamic_slice_in_dim(features, blk_index * out_share, out_share, 0).astype(
-        jnp.float32
-    )
+    own_lookup = lax.dynamic_slice_in_dim(lookup, blk_index * out_share, out_share, 0)
+    image_table = jnp.concatenate([mine_rows, jnp.zeros_like(mine_rows[:1])], axis=0)
+    residual = jnp.where(
+        (own_lookup < image_count)[:, None],
+        jnp.take(image_table, own_lookup, axis=0),
+        lax.dynamic_slice_in_dim(gathered_text, blk_index * out_share, out_share, 0),
+    ).astype(jnp.float32)
     return (residual + summed_heads).astype(jnp.bfloat16)
 
 

time: 272 us -> 302 us (1.11)
  local copies, waits for them, and re-layouts: 28 us -> 43.8 us
  waiting for transfers between devices: 129 us -> 137 us
  other arithmetic: 28.2 us -> 35.5 us
    all_to_all x1, waiting for transfers between devices: 21.2 us -> 54.5 us  [body(): lax.all_to_all(partial.reshape(blk_count, row_share, vis_width), BLK, 0,...]
    all_to_all x1, waiting for transfers between devices: 18.8 us -> 4.35 us  [body(): lax.all_to_all(by_core.transpose(1, 0, 2, 3), 'quad', 0, 0, tiled=False)]
    all_to_all x1, waiting for transfers between devices: 34.3 us -> 21.6 us  [body(): lax.all_to_all(jnp.broadcast_to(merged_here[None], (blk_count,) + merged_...]
    gather x0 -> x3, local copies, waits for them, and re-layouts: none -> 8.55 us  [the longest x2 7.85 us: body(): qkv = jnp.where(is_image, jnp.take(qkv_table, lookup, axis=0), qkv_text)]
    reduce_sum x0 -> x2, other arithmetic: none -> 5.62 us  [rms_normed(): jnp.mean(row_values * row_values, axis=-1, keepdims=True) + 1e-05]
    unnamed x27 -> x33, local copies, waits for them, and re-layouts: 0.66 us -> 4.61 us
    all_to_all x1, waiting for transfers between devices: 12.9 us -> 16.3 us  [body(): lax.all_to_all(jnp.broadcast_to(mine_cols[None], (blk_count,) + mine_cols...]
  transfers between devices with their start and end apart: 10 -> 10, of which waited for: 6 -> 6; matrix products, arithmetic and copies ran while one was open for 28% -> 31% of each run, Pallas kernels for 0% -> 0%
where the time goes in v9:
time: 302 us; the launch traced here: 301 us
  waiting for transfers between devices  137 us (45%)
  starting transfers between devices  45.1 us (15%)
  local copies, waits for them, and re-layouts  43.8 us (15%)
  other arithmetic  35.5 us (12%)
  matrix products  24.9 us (8%)
  between operations  14.1 us (5%)
    all_to_all x1, waiting for transfers between devices, body(): lax.all_to_all(partial.reshape(blk_count, row_share, vis_width), BLK, 0,...  54.5 us
    all_to_all x1, waiting for transfers between devices, body(): lax.all_to_all(pair_sum.reshape(chip_count, out_share, -1), 'grp', 0, 0,...  30.6 us
    all_to_all x1, waiting for transfers between devices, body(): lax.all_to_all(jnp.broadcast_to(merged_here[None], (blk_count,) + merged_...  21.6 us
    all_to_all x1, waiting for transfers between devices, body(): lax.all_to_all(jnp.broadcast_to(mine_cols[None], (blk_count,) + mine_cols...  16.3 us
    all_to_all x1, starting transfers between devices, body(): lax.all_to_all(outgoing, 'req', split_axis=0, concat_axis=0, tiled=True)  9.98 us
    all_to_all x1, starting transfers between devices, body(): lax.all_to_all(jnp.broadcast_to(merged_here[None], (blk_count,) + merged_...  9.56 us
    all_to_all x1, waiting for transfers between devices, body(): lax.all_to_all(outgoing, 'req', split_axis=0, concat_axis=0, tiled=True)  9.19 us
    gather x2, local copies, waits for them, and re-layouts, body(): qkv = jnp.where(is_image, jnp.take(qkv_table, lookup, axis=0), qkv_text)  7.85 us
  transfers between devices with their start and end apart: 10, of which 6 were waited for; matrix products, arithmetic and copies ran while one was open for 31% of the time, Pallas kernels for 0%

profile of v9, /device:TPU:8, one launch (start us, length us, event | category | flops | bytes accessed | tf_op | source)
XLA Modules:
  0.0 300.6 jit_solution(6349801644750890403)
XLA Ops:
  15.7 6.3 %convolution_convert_fusion.2 = bf16[768,1408]{1,0:T(8,128)(2,1)} fusion(bf16[192,1408]{1,0:T(8,128)(2,1)S(1)} %copy-done.15, bf16[1408,192]{0,1:T(8,128)(2,1)S(1)} %copy-done.16, bf16[768,1408]{1,0:T(8,128)(2,1)} %param.22, f32[1408]{0:T(1024)S(1)} %convert_element_type.117, f32[1408]{0:T(1024)S(1)} %convert_element_type.116, ...), kind=kOutput, calls=%fused_computation.46 | convolution fusion | flops 847773696 | bytes 5424896 | tf_op jit(solution)/shard_map/dot_general | solution.py:105
  22.1 6.7 %all-to-all-start = ((bf16[32,24,1408]{2,1,0:T(8,128)(2,1)}), bf16[32,24,1408]{2,1,0:T(8,128)(2,1)}, u32[]{:S(2)}, u32[]{:S(2)}) async-start(bf16[32,24,1408]{2,1,0:T(8,128)(2,1)} %bitcast.93), calls=%async_computation | async-start | bytes 4325376 | tf_op jit(solution)/shard_map/all_to_all | solution.py:108
  28.8 3.9 %convert_element_type.115 = f32[768,1408]{1,0:T(8,128)} convert(bf16[768,1408]{1,0:T(8,128)(2,1)} %param.22) | non-fusion elementwise | flops 1081344 | bytes 6488064 | tf_op jit(solution)/shard_map/convert_element_type | solution.py:99
  32.9 4.5 %reduce-window.19 = s32[8,8,2,128]{3,1,2,0:T(8,128)S(1)} reduce-window(s32[8,8,2,128]{3,1,2,0:T(8,128)S(1)} %convert_bitcast_fusion, s32[]{:T(128)} %constant.97.clone.1), window={size=1x1x1x128 pad=0_0x0_0x0_0x127_0}, to_apply=%region_4.6 | reduce-window | flops 2080768 | bytes 131076 | tf_op jit(solution)/shard_map/reduce-window.2
  39.8 54.5 %all-to-all-done = bf16[32,24,1408]{2,1,0:T(8,128)(2,1)} async-done(((bf16[32,24,1408]{2,1,0:T(8,128)(2,1)}), bf16[32,24,1408]{2,1,0:T(8,128)(2,1)}, u32[]{:S(2)}, u32[]{:S(2)}) %all-to-all-start) | async-done | bytes 2162720 | tf_op jit(solution)/shard_map/all_to_all | solution.py:108
  99.5 9.6 %all-to-all-start.1 = ((bf16[32,6,5632]{2,1,0:T(8,128)(2,1)}), bf16[32,6,5632]{2,1,0:T(8,128)(2,1)}, u32[]{:S(2)}, u32[]{:S(2)}) async-start(bf16[32,6,5632]{2,1,0:T(8,128)(2,1)} %broadcast_in_dim.166), calls=%async_computation.1 | async-start | bytes 5767168 | tf_op jit(solution)/shard_map/all_to_all | solution.py:116
  109.3 6.3 %scatter_custom_fusion = s32[192]{0:T(256)S(1)} fusion(s32[1536]{0:T(1024)S(1)} %compare_select_fusion, s32[1536]{0:T(1024)S(1)} %iota.50, s32[]{:T(128)} %constant.97.clone.1), kind=kCustom, calls=%fused_computation.216 | custom fusion | bytes 772 | tf_op jit(solution)/shard_map/scatter | solution.py:157
  123.6 21.6 %all-to-all-done.1 = bf16[32,6,5632]{2,1,0:T(8,128)(2,1)} async-done(((bf16[32,6,5632]{2,1,0:T(8,128)(2,1)}), bf16[32,6,5632]{2,1,0:T(8,128)(2,1)}, u32[]{:S(2)}, u32[]{:S(2)}) %all-to-all-start.1) | async-done | bytes 2162720 | tf_op jit(solution)/shard_map/all_to_all | solution.py:116
  145.2 4.3 %reshape.390 = bf16[192,5632]{1,0:T(8,128)(2,1)} reshape(bf16[32,6,5632]{2,1,0:T(8,128)(2,1)} %all-to-all-done.1) | data formatting | bytes 4325376 | tf_op jit(solution)/shard_map/reshape | solution.py:124
  154.7 10.0 %all-to-all-start.2 = ((bf16[8,66,128]{2,1,0:T(8,128)(2,1)}), bf16[8,66,128]{2,1,0:T(8,128)(2,1)S(1)}, u32[]{:S(2)}, u32[]{:S(2)}) async-start(bf16[8,66,128]{2,1,0:T(8,128)(2,1)} %broadcast_select_fusion), calls=%async_computation.2 | async-start | bytes 294912 | tf_op jit(solution)/shard_map/all_to_all | solution.py:149
  164.7 9.2 %all-to-all-done.2 = bf16[8,66,128]{2,1,0:T(8,128)(2,1)S(1)} async-done(((bf16[8,66,128]{2,1,0:T(8,128)(2,1)}), bf16[8,66,128]{2,1,0:T(8,128)(2,1)S(1)}, u32[]{:S(2)}, u32[]{:S(2)}) %all-to-all-start.2) | async-done | bytes 135200 | tf_op jit(solution)/shard_map/all_to_all | solution.py:149
  176.4 5.2 %all-to-all-start.3 = ((bf16[32,192,128]{2,1,0:T(8,128)(2,1)}), bf16[32,192,128]{2,1,0:T(8,128)(2,1)S(1)}, u32[]{:S(2)}, u32[]{:S(2)}) async-start(bf16[32,192,128]{2,1,0:T(8,128)(2,1)} %broadcast_in_dim.171), calls=%async_computation.3 | async-start | bytes 3145728 | tf_op jit(solution)/shard_map/all_to_all | solution.py:160
  186.3 16.3 %all-to-all-done.3 = bf16[32,192,128]{2,1,0:T(8,128)(2,1)S(1)} async-done(((bf16[32,192,128]{2,1,0:T(8,128)(2,1)}), bf16[32,192,128]{2,1,0:T(8,128)(2,1)S(1)}, u32[]{:S(2)}, u32[]{:S(2)}) %all-to-all-start.3) | async-done | bytes 1572896 | tf_op jit(solution)/shard_map/all_to_all | solution.py:160
  203.0 2.9 fusion.24
  206.0 4.8 %gather_fusion.3 = f32[1024,384]{1,0:T(8,128)} fusion(f32[193,384]{1,0:T(8,128)S(1)} %concatenate.26, s32[1024]{0:T(1024)S(1)} %fusion.97), kind=kCustom, calls=%fused_computation.5 | custom fusion | bytes 3149824 | tf_op jit(solution)/shard_map/jit(_take)/gather | solution.py:184
  210.8 3.1 %copy.58 = f32[1024,384]{0,1:T(8,128)} copy(f32[1024,384]{1,0:T(8,128)} %gather_fusion.3) | data formatting | bytes 3145728 | tf_op jit(solution)/shard_map/jit(_take)/gather | solution.py:184
  213.9 5.2 %fusion.7 = f32[1024]{0:T(1024)S(1)} fusion(bf16[1024,4096]{1,0:T(8,128)(2,1)} %all-gather.2.cloned.1.call-done), kind=kLoop, calls=%fused_computation.23 | loop fusion | flops 12581888 | bytes 8392704 | tf_op jit(solution)/shard_map/reduce_sum | solution.py:173
  219.6 6.1 %select_select_fusion = f32[1024,384]{0,1:T(8,128)S(1)} fusion(f32[1024,384]{0,1:T(8,128)} %copy.58, bf16[4096,384]{1,0:T(8,128)(2,1)} %constant_dynamic-update-slice_fusion, bf16[1024,4096]{1,0:T(8,128)(2,1)S(1)} %copy-done.4, f32[4096]{0:T(1024)S(1)} %convert_element_type.131, f32[1024]{0:T(1024)S(1)} %add_rsqrt_fusion, ...), kind=kOutput, calls=%fused_computation.53 | convolution fusion | flops 3238789120 | bytes 14702592 | tf_op jit(solution)/shard_map/dot_general | solution.py:180
  231.5 4.8 %while.10 = (s32[]{:T(128)}, bf16[2,512,128]{2,1,0:T(8,128)(2,1)}, pred[2,512,1024]{2,1,0:T(32,128)(4,1)S(1)}, bf16[2,512,128]{2,1,0:T(8,128)(2,1)S(1)}, bf16[10...) while((s32[]{:T(128)}, bf16[2,512,128]{2,1,0:T(8,128)(2,1)}, ...), condition=%wide.region_19.21_spmd, body=%wide.region_16.20_spmd.sunk | while | flops 272694272 | bytes 10759333 | solution.py:194
  238.1 5.6 %all-to-all-start.4 = ((bf16[4,8,32,128]{3,2,1,0:T(8,128)(2,1)}), bf16[4,8,32,128]{3,2,1,0:T(8,128)(2,1)S(1)}, u32[]{:S(2)}, u32[]{:S(2)}) async-start(bf16[4,8,32,128]{3,2,1,0:T(8,128)(2,1)} %bitcast.81), calls=%async_computation.4 | async-start | bytes 524288 | tf_op jit(solution)/shard_map/all_to_all | solution.py:203
  243.7 4.3 %all-to-all-done.4 = bf16[4,8,32,128]{3,2,1,0:T(8,128)(2,1)S(1)} async-done(((bf16[4,8,32,128]{3,2,1,0:T(8,128)(2,1)}), bf16[4,8,32,128]{3,2,1,0:T(8,128)(2,1)S(1)}, u32[]{:S(2)}, u32[]{:S(2)}) %all-to-all-start.4) | async-done | bytes 262176 | tf_op jit(solution)/shard_map/all_to_all | solution.py:203
  249.0 4.8 %convolution_convert_fusion.1 = bf16[256,4096]{1,0:T(8,128)(2,1)} fusion(bf16[128,4096]{1,0:T(8,128)(2,1)} %collective-permute-done.2, bf16[128,4096]{1,0:T(8,128)(2,1)} %collective-permute-done.1, bf16[128,4096]{1,0:T(8,128)(2,1)} %collective-permute-done, bf16[128,4096]{1,0:T(8,128)(2,1)} %param.39, bf16[32,8,4,128]{3,2,1,0:T(4,128)(2,1)S(1)} %bitcast.96), kind=kOutput, calls=%fused_computation.29 | convolution fusion | flops 1091567616 | bytes 6553600 | tf_op jit(solution)/shard_map/dot_general | solution.py:208
  253.8 4.4 %all-to-all-start.5 = ((bf16[8,32,4096]{2,1,0:T(8,128)(2,1)}), bf16[8,32,4096]{2,1,0:T(8,128)(2,1)}, u32[]{:S(2)}, u32[]{:S(2)}) async-start(bf16[8,32,4096]{2,1,0:T(8,128)(2,1)} %bitcast.94), calls=%async_computation.5 | async-start | bytes 4194304 | tf_op jit(solution)/shard_map/all_to_all | solution.py:212
  259.4 30.6 %all-to-all-done.5 = bf16[8,32,4096]{2,1,0:T(8,128)(2,1)} async-done(((bf16[8,32,4096]{2,1,0:T(8,128)(2,1)}), bf16[8,32,4096]{2,1,0:T(8,128)(2,1)}, u32[]{:S(2)}, u32[]{:S(2)}) %all-to-all-start.5) | async-done | bytes 2097184 | tf_op jit(solution)/shard_map/all_to_all | solution.py:212
  (161 shorter events, 56.3 us)
Async XLA Ops:
  6.5 143.0 %copy-start = (bf16[5632,128]{1,0:T(8,128)(2,1)S(1)}, bf16[5632,128]{1,0:T(8,128)(2,1)}, u32[]{:S(2)}) copy-start(bf16[5632,128]{1,0:T(8,128)(2,1)} %param.30) | copy-start | bytes 4325380
  6.5 207.3 %all-gather.2.cloned.1.call-start = ((), (), s32[]{:S(2)}) async-start(), calls=%async_computation.6 | async-start | bytes 8650752 | tf_op jit(solution)/shard_map/all_gather | solution.py:92
  7.3 7.7 %copy-start.2 = (bf16[768,1408]{1,0:T(8,128)(2,1)S(1)}, bf16[768,1408]{1,0:T(8,128)(2,1)}, u32[]{:S(2)}) copy-start(bf16[768,1408]{1,0:T(8,128)(2,1)} %param.22) | copy-start | bytes 6488068
  7.3 8.5 %copy-start.15 = (bf16[192,1408]{1,0:T(8,128)(2,1)S(1)}, bf16[192,1408]{1,0:T(8,128)(2,1)}, u32[]{:S(2)}) copy-start(bf16[192,1408]{1,0:T(8,128)(2,1)} %param.27) | copy-start | bytes 1622020
  7.3 8.5 %copy-start.16 = (bf16[1408,192]{0,1:T(8,128)(2,1)S(1)}, bf16[1408,192]{0,1:T(8,128)(2,1)}, u32[]{:S(2)}) copy-start(bf16[1408,192]{0,1:T(8,128)(2,1)} %param.25) | copy-start | bytes 1622020
  7.3 241.7 %collective-permute-start = (bf16[128,4096]{1,0:T(8,128)(2,1)}, bf16[128,4096]{1,0:T(8,128)(2,1)}, u32[]{:S(2)}, u32[]{:S(2)}) collective-permute-start(bf16[128,4096]{1,0:T(8,128)(2,1)} %param.39), channel_id=1, source_target_pairs={{0,8},{8,16},{16,24},{24,0},{1,9},{9,17},{17,25},{25,1},{2,10},{10... | collective-permute-start | bytes 3145736 | tf_op jit(solution)/shard_map/ppermute | solution.py:94
  7.4 241.6 %collective-permute-start.1 = (bf16[128,4096]{1,0:T(8,128)(2,1)}, bf16[128,4096]{1,0:T(8,128)(2,1)}, u32[]{:S(2)}, u32[]{:S(2)}) collective-permute-start(bf16[128,4096]{1,0:T(8,128)(2,1)} %param.39), channel_id=1, source_target_pairs={{0,16},{8,24},{16,0},{24,8},{1,17},{9,25},{17,1},{25,9},{2,18},{10... | collective-permute-start | bytes 3145736 | tf_op jit(solution)/shard_map/ppermute | solution.py:94
  9.6 239.4 %collective-permute-start.2 = (bf16[128,4096]{1,0:T(8,128)(2,1)}, bf16[128,4096]{1,0:T(8,128)(2,1)}, u32[]{:S(2)}, u32[]{:S(2)}) collective-permute-start(bf16[128,4096]{1,0:T(8,128)(2,1)} %param.39), channel_id=1, source_target_pairs={{0,24},{8,0},{16,8},{24,16},{1,25},{9,1},{17,9},{25,17},{2,26},{10... | collective-permute-start | bytes 3145736 | tf_op jit(solution)/shard_map/ppermute | solution.py:94
  22.1 72.2 %all-to-all-start = ((bf16[32,24,1408]{2,1,0:T(8,128)(2,1)}), bf16[32,24,1408]{2,1,0:T(8,128)(2,1)}, u32[]{:S(2)}, u32[]{:S(2)}) async-start(bf16[32,24,1408]{2,1,0:T(8,128)(2,1)} %bitcast.93), calls=%async_computation | async-start | bytes 4325376 | tf_op jit(solution)/shard_map/all_to_all | solution.py:108
  28.8 3.9 %copy-start.13 = (bf16[1408]{0:T(1024)(128)(2,1)S(1)}, bf16[1408]{0:T(1024)(128)(2,1)}, u32[]{:S(2)}) copy-start(bf16[1408]{0:T(1024)(128)(2,1)} %param.28) | copy-start | bytes 8452
  28.8 3.9 %copy-start.14 = (bf16[1408]{0:T(1024)(128)(2,1)S(1)}, bf16[1408]{0:T(1024)(128)(2,1)}, u32[]{:S(2)}) copy-start(bf16[1408]{0:T(1024)(128)(2,1)} %param.29) | copy-start | bytes 8452
  28.8 3.9 %copy-start.10 = (s32[1536]{0:T(1024)S(1)}, s32[1536]{0:T(1024)}, u32[]{:S(2)}) copy-start(s32[1536]{0:T(1024)} %param.32) | copy-start | bytes 18436
  99.5 9.6 %copy-start.17 = (bf16[128]{0:T(256)(128)(2,1)S(1)}, bf16[128]{0:T(256)(128)(2,1)}, u32[]{:S(2)}) copy-start(bf16[128]{0:T(256)(128)(2,1)} %param.31) | copy-start | bytes 772
  99.5 19.6 %copy-start.11 = (s32[1,1024]{1,0:T(1,128)S(1)}, s32[1,1024]{1,0:T(1,128)}, u32[]{:S(2)}) copy-start(s32[1,1024]{1,0:T(1,128)} %param.34) | copy-start | bytes 12292
  99.5 45.7 %all-to-all-start.1 = ((bf16[32,6,5632]{2,1,0:T(8,128)(2,1)}), bf16[32,6,5632]{2,1,0:T(8,128)(2,1)}, u32[]{:S(2)}, u32[]{:S(2)}) async-start(bf16[32,6,5632]{2,1,0:T(8,128)(2,1)} %broadcast_in_dim.166), calls=%async_computation.1 | async-start | bytes 5767168 | tf_op jit(solution)/shard_map/all_to_all | solution.py:116
  149.5 15.1 %copy-start.12 = (bf16[4096]{0:T(1024)(128)(2,1)S(1)}, bf16[4096]{0:T(1024)(128)(2,1)}, u32[]{:S(2)}) copy-start(bf16[4096]{0:T(1024)(128)(2,1)} %param.35) | copy-start | bytes 24580
  153.8 27.8 %copy-start.5 = (bf16[4096,128]{1,0:T(8,128)(2,1)S(1)}, bf16[4096,128]{1,0:T(8,128)(2,1)}, u32[]{:S(2)}) copy-start(bf16[4096,128]{1,0:T(8,128)(2,1)} %param.36) | copy-start | bytes 3145732
  154.7 19.2 %all-to-all-start.2 = ((bf16[8,66,128]{2,1,0:T(8,128)(2,1)}), bf16[8,66,128]{2,1,0:T(8,128)(2,1)S(1)}, u32[]{:S(2)}, u32[]{:S(2)}) async-start(bf16[8,66,128]{2,1,0:T(8,128)(2,1)} %broadcast_select_fusion), calls=%async_computation.2 | async-start | bytes 294912 | tf_op jit(solution)/shard_map/all_to_all | solution.py:149
  176.4 26.3 %all-to-all-start.3 = ((bf16[32,192,128]{2,1,0:T(8,128)(2,1)}), bf16[32,192,128]{2,1,0:T(8,128)(2,1)S(1)}, u32[]{:S(2)}, u32[]{:S(2)}) async-start(bf16[32,192,128]{2,1,0:T(8,128)(2,1)} %broadcast_in_dim.171), calls=%async_computation.3 | async-start | bytes 3145728 | tf_op jit(solution)/shard_map/all_to_all | solution.py:160
  213.9 5.8 %copy-start.4 = (bf16[1024,4096]{1,0:T(8,128)(2,1)S(1)}, bf16[1024,4096]{1,0:T(8,128)(2,1)}, u32[]{:S(2)}) copy-start(bf16[1024,4096]{1,0:T(8,128)(2,1)} %all-gather.2.cloned.1.call-done) | copy-start | bytes 25165828
  225.8 5.8 %copy-start.3 = (pred[2,512,1024]{2,1,0:T(32,128)(4,1)S(1)}, pred[2,512,1024]{2,1,0:T(32,128)(4,1)}, u32[]{:S(2)}) copy-start(pred[2,512,1024]{2,1,0:T(32,128)(4,1)} %fusion.21) | copy-start | bytes 3145732
  238.1 10.0 %all-to-all-start.4 = ((bf16[4,8,32,128]{3,2,1,0:T(8,128)(2,1)}), bf16[4,8,32,128]{3,2,1,0:T(8,128)(2,1)S(1)}, u32[]{:S(2)}, u32[]{:S(2)}) async-start(bf16[4,8,32,128]{3,2,1,0:T(8,128)(2,1)} %bitcast.81), calls=%async_computation.4 | async-start | bytes 524288 | tf_op jit(solution)/shard_map/all_to_all | solution.py:203
  253.8 36.2 %all-to-all-start.5 = ((bf16[8,32,4096]{2,1,0:T(8,128)(2,1)}), bf16[8,32,4096]{2,1,0:T(8,128)(2,1)}, u32[]{:S(2)}, u32[]{:S(2)}) async-start(bf16[8,32,4096]{2,1,0:T(8,128)(2,1)} %bitcast.94), calls=%async_computation.5 | async-start | bytes 4194304 | tf_op jit(solution)/shard_map/all_to_all | solution.py:212
  258.5 35.2 %copy-start.1 = (bf16[5632,128]{1,0:T(8,128)(2,1)S(1)}, bf16[5632,128]{1,0:T(8,128)(2,1)}, u32[]{:S(2)}) copy-start(bf16[5632,128]{1,0:T(8,128)(2,1)} %param.30) | copy-start | bytes 4325380
  (7 other events, 9.3 us)
Sparse Core Ops, SparseCore 0:
  9.8 95.0 all-gather.1

commit v10 on v7

--- a/solution.py
+++ b/solution.py
@@ -89,7 +89,6 @@
     blk_index = lax.axis_index("grp") * pair_count + core_index
     req_index = lax.axis_index("req")
     vis_width = patches.shape[1]
-    gathered_text = lax.all_gather(text_embed, BLK, axis=1, tiled=True)
     quad_weights = [out_weight] + [
         lax.ppermute(
             out_weight, "quad", [(j, (j + shift) % pair_count) for j in range(pair_count)]
@@ -120,6 +119,8 @@
         0,
         tiled=False,
     )
+    late_text, merged_all = lax.optimization_barrier((text_embed, merged_all))
+    gathered_text = lax.all_gather(late_text, BLK, axis=1, tiled=True)
     image_cols = jnp.dot(
         merged_all.reshape(-1, 4 * vis_width), merge_proj, preferred_element_type=jnp.float32
     )

time: 272 us -> 275 us (1.011)
  blocking collectives: 0 us -> 41.1 us
  waiting for transfers between devices: 129 us -> 104 us
  starting transfers between devices: 43.5 us -> 33.8 us
    all_to_all x0 -> x1, blocking collectives: none -> 41.1 us  [body(): lax.all_to_all(jnp.broadcast_to(merged_here[None], (blk_count,) + merged_...]
    all_to_all x1 -> x0, waiting for transfers between devices: 34.3 us -> none  [body(): lax.all_to_all(jnp.broadcast_to(merged_here[None], (blk_count,) + merged_...]
    all_to_all x1 -> x0, starting transfers between devices: 6.98 us -> none  [body(): lax.all_to_all(jnp.broadcast_to(merged_here[None], (blk_count,) + merged_...]
    all_to_all x1, waiting for transfers between devices: 12.9 us -> 18.5 us  [body(): lax.all_to_all(jnp.broadcast_to(mine_cols[None], (blk_count,) + mine_cols...]
    all_gather x1, waiting for transfers between devices: 0.01 us -> 3.74 us  [body(): gathered_text = lax.all_gather(late_text, BLK, axis=1, tiled=True)]
  transfers between devices with their start and end apart: 10 -> 9, of which waited for: 6 -> 6; matrix products, arithmetic and copies ran while one was open for 28% -> 21% of each run, Pallas kernels for 0% -> 0%
where the time goes in v10:
time: 275 us; the launch traced here: 272 us
  waiting for transfers between devices  104 us (38%)
  blocking collectives  41.1 us (15%)
  starting transfers between devices  33.8 us (12%)
  local copies, waits for them, and re-layouts  26.4 us (10%)
  matrix products  26.4 us (10%)
  other arithmetic  26.3 us (10%)
  between operations  14.1 us (5%)
    all_to_all x1, blocking collectives, body(): lax.all_to_all(jnp.broadcast_to(merged_here[None], (blk_count,) + merged_...  41.1 us
    all_to_all x1, waiting for transfers between devices, body(): lax.all_to_all(pair_sum.reshape(chip_count, out_share, -1), 'grp', 0, 0,...  31.4 us
    all_to_all x1, waiting for transfers between devices, body(): lax.all_to_all(partial.reshape(blk_count, row_share, vis_width), BLK, 0,...  23.6 us
    all_to_all x1, waiting for transfers between devices, body(): lax.all_to_all(jnp.broadcast_to(mine_cols[None], (blk_count,) + mine_cols...  18.5 us
    all_to_all x1, waiting for transfers between devices, body(): lax.all_to_all(by_core.transpose(1, 0, 2, 3), 'quad', 0, 0, tiled=False)  16.7 us
    all_to_all x1, waiting for transfers between devices, body(): lax.all_to_all(outgoing, 'req', split_axis=0, concat_axis=0, tiled=True)  9.63 us
    all_to_all x1, starting transfers between devices, body(): lax.all_to_all(outgoing, 'req', split_axis=0, concat_axis=0, tiled=True)  8.42 us
    all_to_all x1, starting transfers between devices, body(): lax.all_to_all(partial.reshape(blk_count, row_share, vis_width), BLK, 0,...  7.58 us
  transfers between devices with their start and end apart: 9, of which 6 were waited for; matrix products, arithmetic and copies ran while one was open for 21% of the time, Pallas kernels for 0%

profile of v10, /device:TPU:8, one launch (start us, length us, event | category | flops | bytes accessed | tf_op | source)
XLA Modules:
  0.0 271.6 jit_solution(10426985669489029149)
XLA Ops:
  6.6 2.1 convert_reduce_fusion.3
  8.7 2.3 multiply_reduce_fusion
  11.1 6.4 %convolution_convert_fusion.2 = bf16[768,1408]{1,0:T(8,128)(2,1)} fusion(bf16[192,1408]{1,0:T(8,128)(2,1)S(1)} %copy-done.14, bf16[1408,192]{0,1:T(8,128)(2,1)S(1)} %copy-done.15, bf16[768,1408]{1,0:T(8,128)(2,1)} %param.22, f32[1408]{0:T(1024)S(1)} %convert_element_type.111, f32[1408]{0:T(1024)S(1)} %convert_element_type.110, ...), kind=kOutput, calls=%fused_computation.45 | convolution fusion | flops 847773696 | bytes 5424896 | tf_op jit(solution)/shard_map/dot_general | solution.py:104
  17.5 7.6 %all-to-all-start = ((bf16[32,24,1408]{2,1,0:T(8,128)(2,1)}), bf16[32,24,1408]{2,1,0:T(8,128)(2,1)}, u32[]{:S(2)}, u32[]{:S(2)}) async-start(bf16[32,24,1408]{2,1,0:T(8,128)(2,1)} %bitcast.88), calls=%async_computation | async-start | bytes 4325376 | tf_op jit(solution)/shard_map/all_to_all | solution.py:107
  25.1 3.9 %convert_element_type.109 = f32[768,1408]{1,0:T(8,128)} convert(bf16[768,1408]{1,0:T(8,128)(2,1)} %param.22) | non-fusion elementwise | flops 1081344 | bytes 6488064 | tf_op jit(solution)/shard_map/convert_element_type | solution.py:98
  29.0 23.6 %all-to-all-done = bf16[32,24,1408]{2,1,0:T(8,128)(2,1)} async-done(((bf16[32,24,1408]{2,1,0:T(8,128)(2,1)}), bf16[32,24,1408]{2,1,0:T(8,128)(2,1)}, u32[]{:S(2)}, u32[]{:S(2)}) %all-to-all-start) | async-done | bytes 2162720 | tf_op jit(solution)/shard_map/all_to_all | solution.py:107
  56.2 41.1 %all_to_all.34 = bf16[32,6,5632]{2,1,0:T(8,128)(2,1)} all-to-all(bf16[32,6,5632]{2,1,0:T(8,128)(2,1)S(1)} %broadcast_in_dim.130), channel_id=1, replica_groups=mesh['grp'=8,'quad'=4,'req'=8] {'grp','quad'}, dimensions={0} | all-to-all | bytes 4325376 | tf_op jit(solution)/shard_map/all_to_all | solution.py:115
  97.5 4.5 %reduce-window.19 = s32[8,8,2,128]{3,1,2,0:T(8,128)S(1)} reduce-window(s32[8,8,2,128]{3,1,2,0:T(8,128)S(1)} %convert_bitcast_fusion, s32[]{:T(128)} %constant.70.clone.1), window={size=1x1x1x128 pad=0_0x0_0x0_0x127_0}, to_apply=%region_4.6 | reduce-window | flops 2080768 | bytes 131076 | tf_op jit(solution)/shard_map/reduce-window.2
  104.6 6.2 %scatter_custom_fusion = s32[192]{0:T(256)S(1)} fusion(s32[1536]{0:T(1024)S(1)} %compare_select_fusion, s32[1536]{0:T(1024)S(1)} %iota.54, s32[]{:T(128)} %constant.70.clone.1), kind=kCustom, calls=%fused_computation.207 | custom fusion | bytes 772 | tf_op jit(solution)/shard_map/scatter | solution.py:158
  112.2 4.3 %reshape.372 = bf16[192,5632]{1,0:T(8,128)(2,1)} reshape(bf16[32,6,5632]{2,1,0:T(8,128)(2,1)} %all_to_all.34) | data formatting | bytes 4325376 | tf_op jit(solution)/shard_map/reshape | solution.py:125
  116.5 2.4 fusion.32
  121.7 8.4 %all-to-all-start.2 = ((bf16[8,66,128]{2,1,0:T(8,128)(2,1)}), bf16[8,66,128]{2,1,0:T(8,128)(2,1)S(1)}, u32[]{:S(2)}, u32[]{:S(2)}) async-start(bf16[8,66,128]{2,1,0:T(8,128)(2,1)} %broadcast_select_fusion), calls=%async_computation.2 | async-start | bytes 294912 | tf_op jit(solution)/shard_map/all_to_all | solution.py:150
  130.2 9.6 %all-to-all-done.2 = bf16[8,66,128]{2,1,0:T(8,128)(2,1)S(1)} async-done(((bf16[8,66,128]{2,1,0:T(8,128)(2,1)}), bf16[8,66,128]{2,1,0:T(8,128)(2,1)S(1)}, u32[]{:S(2)}, u32[]{:S(2)}) %all-to-all-start.2) | async-done | bytes 135200 | tf_op jit(solution)/shard_map/all_to_all | solution.py:150
  142.2 6.2 %all-to-all-start.3 = ((bf16[32,192,128]{2,1,0:T(8,128)(2,1)}), bf16[32,192,128]{2,1,0:T(8,128)(2,1)}, u32[]{:S(2)}, u32[]{:S(2)}) async-start(bf16[32,192,128]{2,1,0:T(8,128)(2,1)} %broadcast_in_dim.135), calls=%async_computation.3 | async-start | bytes 3145728 | tf_op jit(solution)/shard_map/all_to_all | solution.py:161
  156.6 18.5 %all-to-all-done.3 = bf16[32,192,128]{2,1,0:T(8,128)(2,1)} async-done(((bf16[32,192,128]{2,1,0:T(8,128)(2,1)}), bf16[32,192,128]{2,1,0:T(8,128)(2,1)}, u32[]{:S(2)}, u32[]{:S(2)}) %all-to-all-start.3) | async-done | bytes 1572896 | tf_op jit(solution)/shard_map/all_to_all | solution.py:161
  175.1 3.7 %all-gather.2.cloned.1.call-done = bf16[1024,4096]{1,0:T(8,128)(2,1)} async-done(((bf16[1024,128]{1,0:T(8,128)(2,1)}), bf16[1024,4096]{1,0:T(8,128)(2,1)}) %all-gather.2.cloned.1.call-update) | async-done | bytes 8388624 | tf_op jit(solution)/shard_map/all_gather | solution.py:123
  178.8 6.6 %fusion.7 = (f32[1024]{0:T(1024)S(1)}, bf16[1024,4096]{1,0:T(8,128)(2,1)S(1)}) fusion(bf16[1024,4096]{1,0:T(8,128)(2,1)} %all-gather.2.cloned.1.call-done, s32[1024]{0:T(1024)S(1)} %scatter_custom_fusion.1, pred[1024]{0:T(1024)(128)(4,1)S(1)} %broadcast_compare_fusion.1, bf16[32,192,128]{2,1,0:T(8,128)(2,1)} %all-to-all-done.3), kind=kOutput, calls=%fused_computation.21 | convolution fusion | flops 1631779840 | bytes 18359296 | tf_op jit(solution)/shard_map/dot_general | solution.py:173
  185.5 3.8 %fusion.10 = f32[1024,384]{0,1:T(8,128)S(1)} fusion(bf16[1024,4096]{1,0:T(8,128)(2,1)S(1)} %get-tuple-element.110, f32[4096]{0:T(1024)S(1)} %convert_element_type.125, f32[1024]{0:T(1024)S(1)} %add_rsqrt_fusion, bf16[4096,128]{1,0:T(8,128)(2,1)S(1)} %copy-done.11, bf16[4096,128]{1,0:T(8,128)(2,1)S(1)} %copy-done.12, bf16[4096,128]{1,0:T(8,128)(2,1)S(1)} %copy-done.13), kind=kOutput, calls=%fused_computation.24 | convolution fusion | flops 3247439872 | bytes 13127680 | tf_op jit(solution)/shard_map/dot_general | solution.py:184
  192.9 4.8 %while.10 = (s32[]{:T(128)}, bf16[2,512,128]{2,1,0:T(8,128)(2,1)}, pred[2,512,1024]{2,1,0:T(32,128)(4,1)S(1)}, bf16[2,512,128]{2,1,0:T(8,128)(2,1)S(1)}, bf16[10...) while((s32[]{:T(128)}, bf16[2,512,128]{2,1,0:T(8,128)(2,1)}, ...), condition=%wide.region_18.20_spmd, body=%wide.region_15.19_spmd.sunk | while | flops 272694272 | bytes 9710729 | solution.py:194
  199.4 4.6 %all-to-all-start.4 = ((bf16[4,8,32,128]{3,2,1,0:T(8,128)(2,1)}), bf16[4,8,32,128]{3,2,1,0:T(8,128)(2,1)S(1)}, u32[]{:S(2)}, u32[]{:S(2)}) async-start(bf16[4,8,32,128]{3,2,1,0:T(8,128)(2,1)} %bitcast.76), calls=%async_computation.4 | async-start | bytes 524288 | tf_op jit(solution)/shard_map/all_to_all | solution.py:203
  204.1 16.7 %all-to-all-done.4 = bf16[4,8,32,128]{3,2,1,0:T(8,128)(2,1)S(1)} async-done(((bf16[4,8,32,128]{3,2,1,0:T(8,128)(2,1)}), bf16[4,8,32,128]{3,2,1,0:T(8,128)(2,1)S(1)}, u32[]{:S(2)}, u32[]{:S(2)}) %all-to-all-start.4) | async-done | bytes 262176 | tf_op jit(solution)/shard_map/all_to_all | solution.py:203
  221.7 4.8 %convolution_convert_fusion.1 = bf16[256,4096]{1,0:T(8,128)(2,1)} fusion(bf16[128,4096]{1,0:T(8,128)(2,1)} %collective-permute-done.2, bf16[128,4096]{1,0:T(8,128)(2,1)} %collective-permute-done.1, bf16[128,4096]{1,0:T(8,128)(2,1)} %collective-permute-done, bf16[128,4096]{1,0:T(8,128)(2,1)} %param.39, bf16[32,8,4,128]{3,2,1,0:T(4,128)(2,1)S(1)} %bitcast.91), kind=kOutput, calls=%fused_computation.28 | convolution fusion | flops 1091567616 | bytes 6553600 | tf_op jit(solution)/shard_map/dot_general | solution.py:208
  226.6 4.8 %all-to-all-start.5 = ((bf16[8,32,4096]{2,1,0:T(8,128)(2,1)}), bf16[8,32,4096]{2,1,0:T(8,128)(2,1)S(1)}, u32[]{:S(2)}, u32[]{:S(2)}) async-start(bf16[8,32,4096]{2,1,0:T(8,128)(2,1)} %bitcast.89), calls=%async_computation.5 | async-start | bytes 4194304 | tf_op jit(solution)/shard_map/all_to_all | solution.py:212
  231.3 31.4 %all-to-all-done.5 = bf16[8,32,4096]{2,1,0:T(8,128)(2,1)S(1)} async-done(((bf16[8,32,4096]{2,1,0:T(8,128)(2,1)}), bf16[8,32,4096]{2,1,0:T(8,128)(2,1)S(1)}, u32[]{:S(2)}, u32[]{:S(2)}) %all-to-all-start.5) | async-done | bytes 2097184 | tf_op jit(solution)/shard_map/all_to_all | solution.py:212
  (144 shorter events, 33.9 us)
Async XLA Ops:
  6.5 110.0 %copy-start = (bf16[5632,128]{1,0:T(8,128)(2,1)S(1)}, bf16[5632,128]{1,0:T(8,128)(2,1)}, u32[]{:S(2)}) copy-start(bf16[5632,128]{1,0:T(8,128)(2,1)} %param.30) | copy-start | bytes 4325380
  6.5 4.5 %copy-start.7 = (bf16[1408]{0:T(1024)(128)(2,1)S(1)}, bf16[1408]{0:T(1024)(128)(2,1)}, u32[]{:S(2)}) copy-start(bf16[1408]{0:T(1024)(128)(2,1)} %param.23) | copy-start | bytes 8452
  6.5 4.5 %copy-start.8 = (bf16[1408]{0:T(1024)(128)(2,1)S(1)}, bf16[1408]{0:T(1024)(128)(2,1)}, u32[]{:S(2)}) copy-start(bf16[1408]{0:T(1024)(128)(2,1)} %param.24) | copy-start | bytes 8452
  6.5 4.5 %copy-start.16 = (bf16[192]{0:T(256)(128)(2,1)S(1)}, bf16[192]{0:T(256)(128)(2,1)}, u32[]{:S(2)}) copy-start(bf16[192]{0:T(256)(128)(2,1)} %param.26) | copy-start | bytes 1156
  6.5 4.5 %copy-start.15 = (bf16[1408,192]{0,1:T(8,128)(2,1)S(1)}, bf16[1408,192]{0,1:T(8,128)(2,1)}, u32[]{:S(2)}) copy-start(bf16[1408,192]{0,1:T(8,128)(2,1)} %param.25) | copy-start | bytes 1622020
  6.5 4.5 %copy-start.14 = (bf16[192,1408]{1,0:T(8,128)(2,1)S(1)}, bf16[192,1408]{1,0:T(8,128)(2,1)}, u32[]{:S(2)}) copy-start(bf16[192,1408]{1,0:T(8,128)(2,1)} %param.27) | copy-start | bytes 1622020
  17.5 35.2 %all-to-all-start = ((bf16[32,24,1408]{2,1,0:T(8,128)(2,1)}), bf16[32,24,1408]{2,1,0:T(8,128)(2,1)}, u32[]{:S(2)}, u32[]{:S(2)}) async-start(bf16[32,24,1408]{2,1,0:T(8,128)(2,1)} %bitcast.88), calls=%async_computation | async-start | bytes 4325376 | tf_op jit(solution)/shard_map/all_to_all | solution.py:107
  25.0 3.9 %copy-start.9 = (bf16[1408]{0:T(1024)(128)(2,1)S(1)}, bf16[1408]{0:T(1024)(128)(2,1)}, u32[]{:S(2)}) copy-start(bf16[1408]{0:T(1024)(128)(2,1)} %param.28) | copy-start | bytes 8452
  25.1 3.9 %copy-start.10 = (bf16[1408]{0:T(1024)(128)(2,1)S(1)}, bf16[1408]{0:T(1024)(128)(2,1)}, u32[]{:S(2)}) copy-start(bf16[1408]{0:T(1024)(128)(2,1)} %param.29) | copy-start | bytes 8452
  25.1 153.8 %all-gather.2.cloned.1.call-start = ((), (), s32[]{:S(2)}) async-start(), calls=%async_computation.6 | async-start | bytes 8650752 | tf_op jit(solution)/shard_map/all_gather | solution.py:123
  56.0 41.3 %copy-start.17 = (bf16[128]{0:T(256)(128)(2,1)S(1)}, bf16[128]{0:T(256)(128)(2,1)}, u32[]{:S(2)}) copy-start(bf16[128]{0:T(256)(128)(2,1)} %param.31) | copy-start | bytes 772
  56.0 41.4 %copy-start.3 = (s32[1536]{0:T(1024)S(1)}, s32[1536]{0:T(1024)}, u32[]{:S(2)}) copy-start(s32[1536]{0:T(1024)} %param.32) | copy-start | bytes 18436
  118.9 33.1 %copy-start.5 = (bf16[4096]{0:T(1024)(128)(2,1)S(1)}, bf16[4096]{0:T(1024)(128)(2,1)}, u32[]{:S(2)}) copy-start(bf16[4096]{0:T(1024)(128)(2,1)} %param.35) | copy-start | bytes 24580
  118.9 33.1 %copy-start.4 = (s32[1,1024]{1,0:T(1,128)S(1)}, s32[1,1024]{1,0:T(1,128)}, u32[]{:S(2)}) copy-start(s32[1,1024]{1,0:T(1,128)} %param.34) | copy-start | bytes 12292
  121.7 18.1 %all-to-all-start.2 = ((bf16[8,66,128]{2,1,0:T(8,128)(2,1)}), bf16[8,66,128]{2,1,0:T(8,128)(2,1)S(1)}, u32[]{:S(2)}, u32[]{:S(2)}) async-start(bf16[8,66,128]{2,1,0:T(8,128)(2,1)} %broadcast_select_fusion), calls=%async_computation.2 | async-start | bytes 294912 | tf_op jit(solution)/shard_map/all_to_all | solution.py:150
  142.2 32.9 %all-to-all-start.3 = ((bf16[32,192,128]{2,1,0:T(8,128)(2,1)}), bf16[32,192,128]{2,1,0:T(8,128)(2,1)}, u32[]{:S(2)}, u32[]{:S(2)}) async-start(bf16[32,192,128]{2,1,0:T(8,128)(2,1)} %broadcast_in_dim.135), calls=%async_computation.3 | async-start | bytes 3145728 | tf_op jit(solution)/shard_map/all_to_all | solution.py:161
  148.4 73.3 %collective-permute-start = (bf16[128,4096]{1,0:T(8,128)(2,1)}, bf16[128,4096]{1,0:T(8,128)(2,1)}, u32[]{:S(2)}, u32[]{:S(2)}) collective-permute-start(bf16[128,4096]{1,0:T(8,128)(2,1)} %param.39), channel_id=1, source_target_pairs={{0,8},{8,16},{16,24},{24,0},{1,9},{9,17},{17,25},{25,1},{2,10},{10... | collective-permute-start | bytes 3145736 | tf_op jit(solution)/shard_map/ppermute | solution.py:93
  148.8 72.9 %collective-permute-start.1 = (bf16[128,4096]{1,0:T(8,128)(2,1)}, bf16[128,4096]{1,0:T(8,128)(2,1)}, u32[]{:S(2)}, u32[]{:S(2)}) collective-permute-start(bf16[128,4096]{1,0:T(8,128)(2,1)} %param.39), channel_id=1, source_target_pairs={{0,16},{8,24},{16,0},{24,8},{1,17},{9,25},{17,1},{25,9},{2,18},{10... | collective-permute-start | bytes 3145736 | tf_op jit(solution)/shard_map/ppermute | solution.py:93
  149.2 72.5 %collective-permute-start.2 = (bf16[128,4096]{1,0:T(8,128)(2,1)}, bf16[128,4096]{1,0:T(8,128)(2,1)}, u32[]{:S(2)}, u32[]{:S(2)}) collective-permute-start(bf16[128,4096]{1,0:T(8,128)(2,1)} %param.39), channel_id=1, source_target_pairs={{0,24},{8,0},{16,8},{24,16},{1,25},{9,1},{17,9},{25,17},{2,26},{10... | collective-permute-start | bytes 3145736 | tf_op jit(solution)/shard_map/ppermute | solution.py:93
  178.8 6.7 %copy-start.11 = (bf16[4096,128]{1,0:T(8,128)(2,1)S(1)}, bf16[4096,128]{1,0:T(8,128)(2,1)}, u32[]{:S(2)}) copy-start(bf16[4096,128]{1,0:T(8,128)(2,1)} %param.38) | copy-start | bytes 3145732
  178.8 6.7 %copy-start.12 = (bf16[4096,128]{1,0:T(8,128)(2,1)S(1)}, bf16[4096,128]{1,0:T(8,128)(2,1)}, u32[]{:S(2)}) copy-start(bf16[4096,128]{1,0:T(8,128)(2,1)} %param.37) | copy-start | bytes 3145732
  178.8 6.7 %copy-start.13 = (bf16[4096,128]{1,0:T(8,128)(2,1)S(1)}, bf16[4096,128]{1,0:T(8,128)(2,1)}, u32[]{:S(2)}) copy-start(bf16[4096,128]{1,0:T(8,128)(2,1)} %param.36) | copy-start | bytes 3145732
  199.4 21.4 %all-to-all-start.4 = ((bf16[4,8,32,128]{3,2,1,0:T(8,128)(2,1)}), bf16[4,8,32,128]{3,2,1,0:T(8,128)(2,1)S(1)}, u32[]{:S(2)}, u32[]{:S(2)}) async-start(bf16[4,8,32,128]{3,2,1,0:T(8,128)(2,1)} %bitcast.76), calls=%async_computation.4 | async-start | bytes 524288 | tf_op jit(solution)/shard_map/all_to_all | solution.py:203
  226.6 36.2 %all-to-all-start.5 = ((bf16[8,32,4096]{2,1,0:T(8,128)(2,1)}), bf16[8,32,4096]{2,1,0:T(8,128)(2,1)S(1)}, u32[]{:S(2)}, u32[]{:S(2)}) async-start(bf16[8,32,4096]{2,1,0:T(8,128)(2,1)} %bitcast.89), calls=%async_computation.5 | async-start | bytes 4194304 | tf_op jit(solution)/shard_map/all_to_all | solution.py:212
  (5 other events, 7.5 us)
Sparse Core Ops, SparseCore 0:
  97.4 81.3 all-gather.1

commit v11 on v7

--- a/solution.py
+++ b/solution.py
@@ -184,7 +184,7 @@
     queries = rotate(qkv[:, :head_cols], positions).astype(jnp.bfloat16)
     keys_rot = rotate(qkv[:, head_cols : 2 * head_cols], positions).astype(jnp.bfloat16)
     values_here = qkv[:, 2 * head_cols :].astype(jnp.bfloat16)
-    block_rows = min(512, tok_grp)
+    block_rows = tok_grp
     block_count = tok_grp // block_rows
 
     def attend_block(block_pair):

time: 272 us -> 271 us (level)
  waiting for transfers between devices: 129 us -> 138 us
  other arithmetic: 28.2 us -> 24.1 us
  local copies, waits for them, and re-layouts: 28 us -> 24.6 us
    all_to_all x1, waiting for transfers between devices: 18.8 us -> 24.6 us  [body(): lax.all_to_all(by_core.transpose(1, 0, 2, 3), 'quad', 0, 0, tiled=False)]
    all_to_all x1, waiting for transfers between devices: 12.9 us -> 15.7 us  [body(): lax.all_to_all(jnp.broadcast_to(mine_cols[None], (blk_count,) + mine_cols...]
  transfers between devices with their start and end apart: 10 -> 10, of which waited for: 6 -> 6; matrix products, arithmetic and copies ran while one was open for 28% -> 25% of each run, Pallas kernels for 0% -> 0%
where the time goes in v11:
time: 271 us; the launch traced here: 269 us
  waiting for transfers between devices  138 us (51%)
  starting transfers between devices  43.4 us (16%)
  matrix products  25.1 us (9%)
  local copies, waits for them, and re-layouts  24.6 us (9%)
  other arithmetic  24.1 us (9%)
  between operations  14 us (5%)
    all_to_all x1, waiting for transfers between devices, body(): lax.all_to_all(jnp.broadcast_to(merged_here[None], (blk_count,) + merged_...  34.3 us
    all_to_all x1, waiting for transfers between devices, body(): lax.all_to_all(pair_sum.reshape(chip_count, out_share, -1), 'grp', 0, 0,...  31.6 us
    all_to_all x1, waiting for transfers between devices, body(): lax.all_to_all(by_core.transpose(1, 0, 2, 3), 'quad', 0, 0, tiled=False)  24.6 us
    all_to_all x1, waiting for transfers between devices, body(): lax.all_to_all(partial.reshape(blk_count, row_share, vis_width), BLK, 0,...  21.2 us
    all_to_all x1, waiting for transfers between devices, body(): lax.all_to_all(jnp.broadcast_to(mine_cols[None], (blk_count,) + mine_cols...  15.7 us
    all_to_all x1, waiting for transfers between devices, body(): lax.all_to_all(outgoing, 'req', split_axis=0, concat_axis=0, tiled=True)  9.65 us
    all_to_all x1, starting transfers between devices, body(): lax.all_to_all(outgoing, 'req', split_axis=0, concat_axis=0, tiled=True)  7.74 us
    all_to_all x1, starting transfers between devices, body(): lax.all_to_all(partial.reshape(blk_count, row_share, vis_width), BLK, 0,...  7.58 us
  transfers between devices with their start and end apart: 10, of which 6 were waited for; matrix products, arithmetic and copies ran while one was open for 25% of the time, Pallas kernels for 0%

profile of v11, /device:TPU:8, one launch (start us, length us, event | category | flops | bytes accessed | tf_op | source)
XLA Modules:
  0.0 269.0 jit_solution(17502572194365498925)
XLA Ops:
  9.3 2.0 convert_reduce_fusion.3
  11.3 2.3 multiply_reduce_fusion
  13.6 6.3 %convolution_convert_fusion.1 = bf16[768,1408]{1,0:T(8,128)(2,1)} fusion(bf16[192,1408]{1,0:T(8,128)(2,1)S(1)} %copy-done.10, bf16[1408,192]{0,1:T(8,128)(2,1)S(1)} %copy-done.11, bf16[768,1408]{1,0:T(8,128)(2,1)} %param.20, f32[1408]{0:T(1024)S(1)} %convert_element_type.109, f32[1408]{0:T(1024)S(1)} %convert_element_type.108, ...), kind=kOutput, calls=%fused_computation.38 | convolution fusion | flops 847773696 | bytes 5424896 | tf_op jit(solution)/shard_map/dot_general | solution.py:105
  20.0 7.6 %all-to-all-start = ((bf16[32,24,1408]{2,1,0:T(8,128)(2,1)}), bf16[32,24,1408]{2,1,0:T(8,128)(2,1)}, u32[]{:S(2)}, u32[]{:S(2)}) async-start(bf16[32,24,1408]{2,1,0:T(8,128)(2,1)} %bitcast.65), calls=%async_computation | async-start | bytes 4325376 | tf_op jit(solution)/shard_map/all_to_all | solution.py:108
  27.6 3.9 %convert_element_type.107 = f32[768,1408]{1,0:T(8,128)} convert(bf16[768,1408]{1,0:T(8,128)(2,1)} %param.20) | non-fusion elementwise | flops 1081344 | bytes 6488064 | tf_op jit(solution)/shard_map/convert_element_type | solution.py:99
  31.6 4.5 %reduce-window.19 = s32[8,8,2,128]{3,1,2,0:T(8,128)S(1)} reduce-window(s32[8,8,2,128]{3,1,2,0:T(8,128)S(1)} %convert_bitcast_fusion, s32[]{:T(128)} %constant.75.clone.1), window={size=1x1x1x128 pad=0_0x0_0x0_0x127_0}, to_apply=%region_4.6 | reduce-window | flops 2080768 | bytes 131076 | tf_op jit(solution)/shard_map/reduce-window.2
  36.5 21.2 %all-to-all-done = bf16[32,24,1408]{2,1,0:T(8,128)(2,1)} async-done(((bf16[32,24,1408]{2,1,0:T(8,128)(2,1)}), bf16[32,24,1408]{2,1,0:T(8,128)(2,1)}, u32[]{:S(2)}, u32[]{:S(2)}) %all-to-all-start) | async-done | bytes 2162720 | tf_op jit(solution)/shard_map/all_to_all | solution.py:108
  57.7 1.9 convert_reduce_fusion
  62.9 7.0 %all-to-all-start.1 = ((bf16[32,6,5632]{2,1,0:T(8,128)(2,1)}), bf16[32,6,5632]{2,1,0:T(8,128)(2,1)}, u32[]{:S(2)}, u32[]{:S(2)}) async-start(bf16[32,6,5632]{2,1,0:T(8,128)(2,1)} %broadcast_in_dim.130), calls=%async_computation.1 | async-start | bytes 5767168 | tf_op jit(solution)/shard_map/all_to_all | solution.py:116
  72.2 6.2 %scatter_custom_fusion = s32[192]{0:T(256)S(1)} fusion(s32[1536]{0:T(1024)S(1)} %compare_select_fusion, s32[1536]{0:T(1024)S(1)} %iota.42, s32[]{:T(128)} %constant.75.clone.1), kind=kCustom, calls=%fused_computation.208 | custom fusion | bytes 772 | tf_op jit(solution)/shard_map/scatter | solution.py:157
  79.8 34.3 %all-to-all-done.1 = bf16[32,6,5632]{2,1,0:T(8,128)(2,1)} async-done(((bf16[32,6,5632]{2,1,0:T(8,128)(2,1)}), bf16[32,6,5632]{2,1,0:T(8,128)(2,1)}, u32[]{:S(2)}, u32[]{:S(2)}) %all-to-all-start.1) | async-done | bytes 2162720 | tf_op jit(solution)/shard_map/all_to_all | solution.py:116
  114.1 4.3 %reshape.361 = bf16[192,5632]{1,0:T(8,128)(2,1)} reshape(bf16[32,6,5632]{2,1,0:T(8,128)(2,1)} %all-to-all-done.1) | data formatting | bytes 4325376 | tf_op jit(solution)/shard_map/reshape | solution.py:124
  118.4 2.3 fusion.27
  123.6 7.7 %all-to-all-start.2 = ((bf16[8,66,128]{2,1,0:T(8,128)(2,1)}), bf16[8,66,128]{2,1,0:T(8,128)(2,1)S(1)}, u32[]{:S(2)}, u32[]{:S(2)}) async-start(bf16[8,66,128]{2,1,0:T(8,128)(2,1)} %broadcast_select_fusion), calls=%async_computation.2 | async-start | bytes 294912 | tf_op jit(solution)/shard_map/all_to_all | solution.py:149
  131.4 9.6 %all-to-all-done.2 = bf16[8,66,128]{2,1,0:T(8,128)(2,1)S(1)} async-done(((bf16[8,66,128]{2,1,0:T(8,128)(2,1)}), bf16[8,66,128]{2,1,0:T(8,128)(2,1)S(1)}, u32[]{:S(2)}, u32[]{:S(2)}) %all-to-all-start.2) | async-done | bytes 135200 | tf_op jit(solution)/shard_map/all_to_all | solution.py:149
  143.5 7.3 %all-to-all-start.3 = ((bf16[32,192,128]{2,1,0:T(8,128)(2,1)}), bf16[32,192,128]{2,1,0:T(8,128)(2,1)S(1)}, u32[]{:S(2)}, u32[]{:S(2)}) async-start(bf16[32,192,128]{2,1,0:T(8,128)(2,1)} %broadcast_in_dim.135), calls=%async_computation.3 | async-start | bytes 3145728 | tf_op jit(solution)/shard_map/all_to_all | solution.py:160
  156.0 15.7 %all-to-all-done.3 = bf16[32,192,128]{2,1,0:T(8,128)(2,1)S(1)} async-done(((bf16[32,192,128]{2,1,0:T(8,128)(2,1)}), bf16[32,192,128]{2,1,0:T(8,128)(2,1)S(1)}, u32[]{:S(2)}, u32[]{:S(2)}) %all-to-all-start.3) | async-done | bytes 1572896 | tf_op jit(solution)/shard_map/all_to_all | solution.py:160
  171.7 6.2 %fusion = (f32[1024]{0:T(1024)S(1)}, bf16[1024,4096]{1,0:T(8,128)(2,1)S(1)}) fusion(bf16[1024,4096]{1,0:T(8,128)(2,1)} %all-gather.2.cloned.1.call-done, s32[1024]{0:T(1024)S(1)} %scatter_custom_fusion.1, pred[1024]{0:T(1024)(128)(4,1)S(1)} %broadcast_compare_fusion.1, bf16[32,192,128]{2,1,0:T(8,128)(2,1)S(1)} %all-to-all-done.3), kind=kOutput, calls=%fused_computation.10 | convolution fusion | flops 1631779840 | bytes 18359296 | tf_op jit(solution)/shard_map/dot_general | solution.py:172
  178.0 3.9 %fusion.3 = f32[1024,384]{0,1:T(8,128)S(1)} fusion(bf16[1024,4096]{1,0:T(8,128)(2,1)S(1)} %get-tuple-element.41, f32[4096]{0:T(1024)S(1)} %convert_element_type.123, f32[1024]{0:T(1024)S(1)} %add_rsqrt_fusion, bf16[4096,128]{1,0:T(8,128)(2,1)S(1)} %copy-done.6, bf16[4096,128]{1,0:T(8,128)(2,1)S(1)} %copy-done.7, bf16[4096,128]{1,0:T(8,128)(2,1)S(1)} %copy-done.8), kind=kOutput, calls=%fused_computation.13 | convolution fusion | flops 3247439872 | bytes 13127680 | tf_op jit(solution)/shard_map/dot_general | solution.py:183
  186.6 5.7 %all-to-all-start.4 = ((bf16[4,8,32,128]{3,2,1,0:T(8,128)(2,1)}), bf16[4,8,32,128]{3,2,1,0:T(8,128)(2,1)S(1)}, u32[]{:S(2)}, u32[]{:S(2)}) async-start(bf16[4,8,32,128]{3,2,1,0:T(8,128)(2,1)} %bitcast.64), calls=%async_computation.4 | async-start | bytes 524288 | tf_op jit(solution)/shard_map/all_to_all | solution.py:202
  192.3 24.6 %all-to-all-done.4 = bf16[4,8,32,128]{3,2,1,0:T(8,128)(2,1)S(1)} async-done(((bf16[4,8,32,128]{3,2,1,0:T(8,128)(2,1)}), bf16[4,8,32,128]{3,2,1,0:T(8,128)(2,1)S(1)}, u32[]{:S(2)}, u32[]{:S(2)}) %all-to-all-start.4) | async-done | bytes 262176 | tf_op jit(solution)/shard_map/all_to_all | solution.py:202
  217.8 4.5 %convolution_convert_fusion = bf16[256,4096]{1,0:T(8,128)(2,1)} fusion(bf16[128,4096]{1,0:T(8,128)(2,1)} %collective-permute-done.2, bf16[128,4096]{1,0:T(8,128)(2,1)} %collective-permute-done.1, bf16[128,4096]{1,0:T(8,128)(2,1)} %collective-permute-done, bf16[128,4096]{1,0:T(8,128)(2,1)S(1)} %copy-done.9, bf16[32,8,4,128]{3,2,1,0:T(4,128)(2,1)S(1)} %bitcast.68), kind=kOutput, calls=%fused_computation.19 | convolution fusion | flops 1091567616 | bytes 6553600 | tf_op jit(solution)/shard_map/dot_general | solution.py:207
  222.3 6.2 %all-to-all-start.5 = ((bf16[8,32,4096]{2,1,0:T(8,128)(2,1)}), bf16[8,32,4096]{2,1,0:T(8,128)(2,1)S(1)}, u32[]{:S(2)}, u32[]{:S(2)}) async-start(bf16[8,32,4096]{2,1,0:T(8,128)(2,1)} %bitcast.66), calls=%async_computation.5 | async-start | bytes 4194304 | tf_op jit(solution)/shard_map/all_to_all | solution.py:211
  228.5 31.6 %all-to-all-done.5 = bf16[8,32,4096]{2,1,0:T(8,128)(2,1)S(1)} async-done(((bf16[8,32,4096]{2,1,0:T(8,128)(2,1)}), bf16[8,32,4096]{2,1,0:T(8,128)(2,1)S(1)}, u32[]{:S(2)}, u32[]{:S(2)}) %all-to-all-start.5) | async-done | bytes 2097184 | tf_op jit(solution)/shard_map/all_to_all | solution.py:211
  (118 shorter events, 28.2 us)
Async XLA Ops:
  6.5 111.9 %copy-start = (bf16[5632,128]{1,0:T(8,128)(2,1)S(1)}, bf16[5632,128]{1,0:T(8,128)(2,1)}, u32[]{:S(2)}) copy-start(bf16[5632,128]{1,0:T(8,128)(2,1)} %param.28) | copy-start | bytes 4325380
  6.5 7.1 %copy-start.11 = (bf16[1408,192]{0,1:T(8,128)(2,1)S(1)}, bf16[1408,192]{0,1:T(8,128)(2,1)}, u32[]{:S(2)}) copy-start(bf16[1408,192]{0,1:T(8,128)(2,1)} %param.23) | copy-start | bytes 1622020
  6.5 7.1 %copy-start.10 = (bf16[192,1408]{1,0:T(8,128)(2,1)S(1)}, bf16[192,1408]{1,0:T(8,128)(2,1)}, u32[]{:S(2)}) copy-start(bf16[192,1408]{1,0:T(8,128)(2,1)} %param.25) | copy-start | bytes 1622020
  6.5 165.2 %all-gather.2.cloned.1.call-start = ((), (), s32[]{:S(2)}) async-start(), calls=%async_computation.6 | async-start | bytes 8650752 | tf_op jit(solution)/shard_map/all_gather | solution.py:92
  20.0 37.8 %all-to-all-start = ((bf16[32,24,1408]{2,1,0:T(8,128)(2,1)}), bf16[32,24,1408]{2,1,0:T(8,128)(2,1)}, u32[]{:S(2)}, u32[]{:S(2)}) async-start(bf16[32,24,1408]{2,1,0:T(8,128)(2,1)} %bitcast.65), calls=%async_computation | async-start | bytes 4325376 | tf_op jit(solution)/shard_map/all_to_all | solution.py:108
  27.5 3.9 %copy-start.4 = (bf16[1408]{0:T(1024)(128)(2,1)S(1)}, bf16[1408]{0:T(1024)(128)(2,1)}, u32[]{:S(2)}) copy-start(bf16[1408]{0:T(1024)(128)(2,1)} %param.26) | copy-start | bytes 8452
  27.6 3.9 %copy-start.5 = (bf16[1408]{0:T(1024)(128)(2,1)S(1)}, bf16[1408]{0:T(1024)(128)(2,1)}, u32[]{:S(2)}) copy-start(bf16[1408]{0:T(1024)(128)(2,1)} %param.27) | copy-start | bytes 8452
  27.6 3.9 %copy-start.1 = (s32[1536]{0:T(1024)S(1)}, s32[1536]{0:T(1024)}, u32[]{:S(2)}) copy-start(s32[1536]{0:T(1024)} %param.30) | copy-start | bytes 18436
  61.0 8.9 %copy-start.13 = (bf16[128]{0:T(256)(128)(2,1)S(1)}, bf16[128]{0:T(256)(128)(2,1)}, u32[]{:S(2)}) copy-start(bf16[128]{0:T(256)(128)(2,1)} %param.29) | copy-start | bytes 772
  62.9 51.2 %all-to-all-start.1 = ((bf16[32,6,5632]{2,1,0:T(8,128)(2,1)}), bf16[32,6,5632]{2,1,0:T(8,128)(2,1)}, u32[]{:S(2)}, u32[]{:S(2)}) async-start(bf16[32,6,5632]{2,1,0:T(8,128)(2,1)} %broadcast_in_dim.130), calls=%async_computation.1 | async-start | bytes 5767168 | tf_op jit(solution)/shard_map/all_to_all | solution.py:116
  120.8 33.5 %copy-start.2 = (bf16[4096]{0:T(1024)(128)(2,1)S(1)}, bf16[4096]{0:T(1024)(128)(2,1)}, u32[]{:S(2)}) copy-start(bf16[4096]{0:T(1024)(128)(2,1)} %param.33) | copy-start | bytes 24580
  120.8 33.5 %copy-start.12 = (s32[1,1024]{1,0:T(1,128)S(1)}, s32[1,1024]{1,0:T(1,128)}, u32[]{:S(2)}) copy-start(s32[1,1024]{1,0:T(1,128)} %param.32) | copy-start | bytes 12292
  123.6 17.4 %all-to-all-start.2 = ((bf16[8,66,128]{2,1,0:T(8,128)(2,1)}), bf16[8,66,128]{2,1,0:T(8,128)(2,1)S(1)}, u32[]{:S(2)}, u32[]{:S(2)}) async-start(bf16[8,66,128]{2,1,0:T(8,128)(2,1)} %broadcast_select_fusion), calls=%async_computation.2 | async-start | bytes 294912 | tf_op jit(solution)/shard_map/all_to_all | solution.py:149
  143.5 28.2 %all-to-all-start.3 = ((bf16[32,192,128]{2,1,0:T(8,128)(2,1)}), bf16[32,192,128]{2,1,0:T(8,128)(2,1)S(1)}, u32[]{:S(2)}, u32[]{:S(2)}) async-start(bf16[32,192,128]{2,1,0:T(8,128)(2,1)} %broadcast_in_dim.135), calls=%async_computation.3 | async-start | bytes 3145728 | tf_op jit(solution)/shard_map/all_to_all | solution.py:160
  150.8 67.0 %collective-permute-start = (bf16[128,4096]{1,0:T(8,128)(2,1)}, bf16[128,4096]{1,0:T(8,128)(2,1)}, u32[]{:S(2)}, u32[]{:S(2)}) collective-permute-start(bf16[128,4096]{1,0:T(8,128)(2,1)} %param.37), channel_id=1, source_target_pairs={{0,8},{8,16},{16,24},{24,0},{1,9},{9,17},{17,25},{25,1},{2,10},{10... | collective-permute-start | bytes 3145736 | tf_op jit(solution)/shard_map/ppermute | solution.py:94
  151.2 66.6 %collective-permute-start.1 = (bf16[128,4096]{1,0:T(8,128)(2,1)}, bf16[128,4096]{1,0:T(8,128)(2,1)}, u32[]{:S(2)}, u32[]{:S(2)}) collective-permute-start(bf16[128,4096]{1,0:T(8,128)(2,1)} %param.37), channel_id=1, source_target_pairs={{0,16},{8,24},{16,0},{24,8},{1,17},{9,25},{17,1},{25,9},{2,18},{10... | collective-permute-start | bytes 3145736 | tf_op jit(solution)/shard_map/ppermute | solution.py:94
  151.6 66.2 %collective-permute-start.2 = (bf16[128,4096]{1,0:T(8,128)(2,1)}, bf16[128,4096]{1,0:T(8,128)(2,1)}, u32[]{:S(2)}, u32[]{:S(2)}) collective-permute-start(bf16[128,4096]{1,0:T(8,128)(2,1)} %param.37), channel_id=1, source_target_pairs={{0,24},{8,0},{16,8},{24,16},{1,25},{9,1},{17,9},{25,17},{2,26},{10... | collective-permute-start | bytes 3145736 | tf_op jit(solution)/shard_map/ppermute | solution.py:94
  171.7 6.3 %copy-start.6 = (bf16[4096,128]{1,0:T(8,128)(2,1)S(1)}, bf16[4096,128]{1,0:T(8,128)(2,1)}, u32[]{:S(2)}) copy-start(bf16[4096,128]{1,0:T(8,128)(2,1)} %param.36) | copy-start | bytes 3145732
  171.7 6.3 %copy-start.7 = (bf16[4096,128]{1,0:T(8,128)(2,1)S(1)}, bf16[4096,128]{1,0:T(8,128)(2,1)}, u32[]{:S(2)}) copy-start(bf16[4096,128]{1,0:T(8,128)(2,1)} %param.35) | copy-start | bytes 3145732
  171.7 6.3 %copy-start.8 = (bf16[4096,128]{1,0:T(8,128)(2,1)S(1)}, bf16[4096,128]{1,0:T(8,128)(2,1)}, u32[]{:S(2)}) copy-start(bf16[4096,128]{1,0:T(8,128)(2,1)} %param.34) | copy-start | bytes 3145732
  178.0 3.9 %copy-start.3 = (bf16[1024,4096]{1,0:T(8,128)(2,1)}, bf16[1024,4096]{1,0:T(8,128)(2,1)S(1)}, u32[]{:S(2)}) copy-start(bf16[1024,4096]{1,0:T(8,128)(2,1)S(1)} %get-tuple-element.41) | copy-start | bytes 25165828
  184.8 33.0 %copy-start.9 = (bf16[128,4096]{1,0:T(8,128)(2,1)S(1)}, bf16[128,4096]{1,0:T(8,128)(2,1)}, u32[]{:S(2)}) copy-start(bf16[128,4096]{1,0:T(8,128)(2,1)} %param.37) | copy-start | bytes 3145732
  186.6 30.2 %all-to-all-start.4 = ((bf16[4,8,32,128]{3,2,1,0:T(8,128)(2,1)}), bf16[4,8,32,128]{3,2,1,0:T(8,128)(2,1)S(1)}, u32[]{:S(2)}, u32[]{:S(2)}) async-start(bf16[4,8,32,128]{3,2,1,0:T(8,128)(2,1)} %bitcast.64), calls=%async_computation.4 | async-start | bytes 524288 | tf_op jit(solution)/shard_map/all_to_all | solution.py:202
  222.3 37.8 %all-to-all-start.5 = ((bf16[8,32,4096]{2,1,0:T(8,128)(2,1)}), bf16[8,32,4096]{2,1,0:T(8,128)(2,1)S(1)}, u32[]{:S(2)}, u32[]{:S(2)}) async-start(bf16[8,32,4096]{2,1,0:T(8,128)(2,1)} %bitcast.66), calls=%async_computation.5 | async-start | bytes 4194304 | tf_op jit(solution)/shard_map/all_to_all | solution.py:211
Sparse Core Ops, SparseCore 0:
  9.8 114.3 all-gather.1
